TPU v7x, 256 devices: a whole 4x4x8 slice. The times are simulated.
256 devices in a mesh: seq: 64 (over x, z, core), tensor: 4 (over y).
Axes of the slice: x: 4, y: 4, z: 8, core: 2. Of those that a mesh axis runs over, the one named last changes fastest.
Arguments:
- hidden: bfloat16 [8192, 8192], P('seq'), may hold values from -6 to 6
- gain: bfloat16 [8192], replicated, may hold values from 0.5 to 1.5
- w_query: bfloat16 [8192, 4096], P('seq', 'tensor'), may hold values from -0.0625 to 0.0625
- q_bias: bfloat16 [4096], P('tensor'), may hold values from -3 to 3
- w_keyval: bfloat16 [8192, 2, 512], P('seq', None, 'tensor'), may hold values from -0.125 to 0.125
- kv_bias: bfloat16 [2, 512], P(None, 'tensor'), may hold values from -3 to 3
- prefix_keys: bfloat16 [2, 4096, 4, 128], P(None, 'seq', 'tensor'), may hold values from -128 to 128, as said below
- prefix_values: bfloat16 [2, 4096, 4, 128], P(None, 'seq', 'tensor'), may hold values from -6 to 6
- lengths: int32 [32], replicated, may hold values from 1 to 384, 8192 in all
- assignment: int32 [32], replicated, may hold values from 0 to 1
Outputs:
- attention: bfloat16 [8192, 4096], P('seq', 'tensor')
- suffix_keys: bfloat16 [8192, 4, 128], P('seq', 'tensor')
- suffix_values: bfloat16 [8192, 4, 128], P('seq', 'tensor')
Inputs may be any that keep to these rules, and one draw needn't show every extreme that they name: Request r occupies the next lengths[r] rows of the token arrays, in order; the lengths sum to 8192 and the largest is 384. `assignment`: the prefix that request r continues. `prefix_keys`: cached keys, already rotated to positions 0 to 4095.
All inputs are finite; a program needn't handle non-finite values.
Results may differ from a plain program's by a relative error of at most 0.01.
The roundings to bfloat16 on the way count: a program that leaves them out, or rounds other values in their place, can miss the bound.
Values may be sent and summed in bfloat16 or wider, within the bound.
No kernel may reach another device: no remote copies, remote signals or barrier semaphores. Data moves between devices by JAX's collectives and lax.ppermute only.
A program may use at most 128 MiB of HBM per device.

v0:
```python
import math

import jax
import jax.numpy as jnp
from jax import lax
from jax.sharding import PartitionSpec as P

EPS = 1e-06
THETA = 1000000.0


def from_behind(shard, axis, by):
    size = lax.axis_size(axis)
    pairs = [(i, i + by) for i in range(size) if 0 <= i + by < size]
    return lax.ppermute(shard, axis, pairs)


def row_tables(lengths, assignment, all_rows):
    request_end = jnp.cumsum(lengths)
    request_start = request_end - lengths
    row_ids = jnp.arange(all_rows, dtype=jnp.int32)
    segment = jnp.sum((row_ids[:, None] >= request_end[None, :]).astype(jnp.int32), axis=1)
    request_ids = jnp.arange(lengths.shape[0], dtype=jnp.int32)
    onehot = (segment[:, None] == request_ids[None, :]).astype(jnp.int32)
    offset = row_ids - jnp.sum(onehot * request_start[None, :], axis=1)
    prefix = jnp.sum(onehot * assignment[None, :], axis=1)
    return (segment, offset, prefix)


def rotate(values, positions):
    head_size = values.shape[-1]
    half_dim = head_size // 2
    frequency = THETA ** (-2.0 * jnp.arange(half_dim, dtype=jnp.float32) / head_size)
    angles = positions.astype(jnp.float32)[:, None] * frequency[None, :]
    cosine = jnp.concatenate([jnp.cos(angles), jnp.cos(angles)], axis=-1)[:, None, :]
    sine_part = jnp.concatenate([jnp.sin(angles), jnp.sin(angles)], axis=-1)[:, None, :]
    turned = jnp.concatenate([-values[..., half_dim:], values[..., :half_dim]], axis=-1)
    return values * cosine + turned * sine_part


def local(
    hidden,
    gain,
    w_query,
    q_bias,
    w_keyval,
    kv_bias,
    prefix_keys,
    prefix_values,
    lengths,
    assignment,
):
    row_count = hidden.shape[0]
    seq_count = lax.axis_size("seq")
    seq_index = lax.axis_index("seq")
    all_rows = row_count * seq_count
    head_dim = prefix_keys.shape[3]
    kv_local = prefix_keys.shape[2]
    prefix_count = prefix_keys.shape[0]
    query_width = w_query.shape[1]
    heads_local = query_width // head_dim
    group_size = heads_local // kv_local
    pair_width = w_keyval.shape[1] * w_keyval.shape[2]
    key_width = pair_width // 2
    cache_length = prefix_keys.shape[1] * seq_count
    score_scale = head_dim ** (-0.5)
    first_row = seq_index * row_count
    prefix_ids = jnp.arange(prefix_count, dtype=jnp.int32)
    hidden_f = hidden.astype(jnp.float32)
    normed = (
        hidden_f
        * lax.rsqrt(jnp.mean(hidden_f * hidden_f, axis=1, keepdims=True) + EPS)
        * gain.astype(jnp.float32)
    ).astype(jnp.bfloat16)
    segment, offset, prefix = row_tables(lengths, assignment, all_rows)
    positions = offset + cache_length
    own_positions = lax.dynamic_slice_in_dim(positions, first_row, row_count)
    own_segment = lax.dynamic_slice_in_dim(segment, first_row, row_count)
    own_prefix = lax.dynamic_slice_in_dim(prefix, first_row, row_count)
    w_pairs = w_keyval.reshape(w_keyval.shape[0], pair_width)
    combined = jnp.concatenate([w_query, w_pairs], axis=1)
    summed = jnp.dot(
        normed,
        lax.all_gather(combined, "seq", axis=0, tiled=True),
        preferred_element_type=jnp.float32,
    )
    query_own = summed[:, :query_width] + q_bias.astype(jnp.float32)
    pairs_own = summed[:, query_width:] + kv_bias.reshape(pair_width).astype(jnp.float32)
    own_queries = rotate(query_own.reshape(row_count, heads_local, head_dim), own_positions).astype(
        jnp.bfloat16
    )
    own_keys = rotate(
        pairs_own[:, :key_width].reshape(row_count, kv_local, head_dim), own_positions
    ).astype(jnp.bfloat16)
    own_values = (
        pairs_own[:, key_width:].reshape(row_count, kv_local, head_dim).astype(jnp.bfloat16)
    )
    own_blocks = own_queries.reshape(row_count, kv_local, group_size, head_dim)
    allowed_own = (own_prefix[:, None] == prefix_ids[None, :])[:, None, None, :, None]
    initial = (
        jnp.full((row_count, kv_local, group_size), -jnp.inf, jnp.float32),
        jnp.zeros((row_count, kv_local, group_size), jnp.float32),
        jnp.zeros((row_count, kv_local, group_size, head_dim), jnp.float32),
    )
    keys_piece = lax.all_gather(prefix_keys, "seq", axis=1, tiled=True)
    values_piece = lax.all_gather(prefix_values, "seq", axis=1, tiled=True)
    piece_len = keys_piece.shape[1]
    step_rows = math.gcd(piece_len, 512)

    def inner(state, block_index):
        run_top, run_mass, run_acc = state
        key_block = lax.dynamic_slice_in_dim(keys_piece, block_index * step_rows, step_rows, 1)
        value_block = lax.dynamic_slice_in_dim(values_piece, block_index * step_rows, step_rows, 1)
        scores = (
            jnp.einsum(
                "bgqd,plgd->bgqpl", own_blocks, key_block, preferred_element_type=jnp.float32
            )
            * score_scale
        )
        scores = jnp.where(allowed_own, scores, -jnp.inf)
        new_top = jnp.maximum(run_top, jnp.max(scores, axis=(3, 4)))
        keep_share = jnp.exp(run_top - new_top)
        weights = jnp.exp(scores - new_top[..., None, None])
        new_mass = run_mass * keep_share + jnp.sum(weights, axis=(3, 4))
        new_acc = run_acc * keep_share[..., None] + jnp.einsum(
            "bgqpl,plgd->bgqd",
            weights.astype(jnp.bfloat16),
            value_block,
            preferred_element_type=jnp.float32,
        )
        return ((new_top, new_mass, new_acc), None)

    result, unused = lax.scan(inner, initial, jnp.arange(piece_len // step_rows, dtype=jnp.int32))
    fold_top, fold_mass, fold_acc = result
    prefix_top = fold_top.reshape(row_count, heads_local)
    prefix_mass = fold_mass.reshape(row_count, heads_local)
    prefix_acc = fold_acc.reshape(row_count, heads_local, head_dim)
    pair_rows = jnp.concatenate(
        [own_keys.reshape(row_count, key_width), own_values.reshape(row_count, key_width)], axis=1
    )
    depth = min(3, seq_count - 1)
    earlier = []
    for distance in range(depth, 0, -1):
        earlier.append(from_behind(pair_rows, "seq", distance))
    near_rows = jnp.concatenate(earlier + [pair_rows], axis=0)
    near_index = (
        first_row - depth * row_count + jnp.arange((depth + 1) * row_count, dtype=jnp.int32)
    )
    near_keys = near_rows[:, :key_width].reshape(near_rows.shape[0], kv_local, head_dim)
    near_values = near_rows[:, key_width:].reshape(near_rows.shape[0], kv_local, head_dim)
    near_segment = segment[jnp.clip(near_index, 0, all_rows - 1)]
    own_rows = first_row + jnp.arange(row_count, dtype=jnp.int32)
    visible = (
        (near_index[None, :] >= 0)
        & (near_segment[None, :] == own_segment[:, None])
        & (near_index[None, :] <= own_rows[:, None])
    )
    scores = (
        jnp.einsum("bgqd,ngd->bgqn", own_blocks, near_keys, preferred_element_type=jnp.float32)
        * score_scale
    )
    scores = jnp.where(visible[:, None, None, :], scores, -jnp.inf)
    local_top = jnp.max(scores, axis=3)
    weights = jnp.exp(scores - local_top[..., None])
    local_mass = jnp.sum(weights, axis=3).reshape(row_count, heads_local)
    local_acc = jnp.einsum(
        "bgqn,ngd->bgqd",
        weights.astype(jnp.bfloat16),
        near_values,
        preferred_element_type=jnp.float32,
    ).reshape(row_count, heads_local, head_dim)
    local_top = local_top.reshape(row_count, heads_local)
    joint_top = jnp.maximum(prefix_top, local_top)
    far_scale = jnp.exp(prefix_top - joint_top)
    near_scale = jnp.exp(local_top - joint_top)
    numerator = prefix_acc * far_scale[..., None] + local_acc * near_scale[..., None]
    denominator = prefix_mass * far_scale + local_mass * near_scale
    attention = (
        (numerator / denominator[..., None]).astype(jnp.bfloat16).reshape(row_count, query_width)
    )
    return (attention, own_keys, own_values)


def solution(mesh):
    in_specs = (
        P("seq", None),
        P(),
        P("seq", "tensor"),
        P("tensor"),
        P("seq", None, "tensor"),
        P(None, "tensor"),
        P(None, "seq", "tensor", None),
        P(None, "seq", "tensor", None),
        P(),
        P(),
    )
    out_specs = (P("seq", "tensor"), P("seq", "tensor", None), P("seq", "tensor", None))
    return jax.shard_map(local, mesh=mesh, in_specs=in_specs, out_specs=out_specs, check_vma=False)
```

profile of v0, /device:TPU:1, one launch (start us, length us, event | category | flops | bytes accessed | tf_op | source)
XLA Modules:
  0.0 376.9 jit_solution(10367872859374238164)
XLA Ops:
  7.3 1.0 copy.127
  8.2 1.7 pad_maximum_fusion
  10.0 1.4 copy.68
  12.2 0.7 copy.64
  14.8 2.1 fusion.24
  17.5 3.1 gather_fusion
  22.4 102.5 %all-gather.6.cloned.1.call-done = bf16[8192,1280]{1,0:T(8,128)(2,1)} async-done(((bf16[128,1280]{1,0:T(8,128)(2,1)}), bf16[8192,1280]{1,0:T(8,128)(2,1)}) %all-gather.6.cloned.1.call-update) | async-done | bytes 20971536 | tf_op jit(solution)/shard_map/all_gather | solution.py:84
  124.9 9.9 %fusion.27 = f32[128,1280]{1,0:T(8,128)S(1)} fusion(bf16[8192,1280]{1,0:T(8,128)(2,1)} %all-gather.6.cloned.1.call-done, bf16[128,8192]{1,0:T(8,128)(2,1)S(1)} %copy-done.1, f32[8192]{0:T(1024)S(1)} %convert_element_type.68, f32[128]{0:T(128)} %add_rsqrt_fusion), kind=kOutput, calls=%fused_computation.33 | convolution fusion | flops 2688548864 | bytes 23757312 | tf_op jit(solution)/shard_map/dot_general | solution.py:82
  135.2 3.1 collective-permute-start
  138.2 4.4 %collective-permute-start.1 = (bf16[128,256]{1,0:T(8,128)(2,1)S(1)}, bf16[128,256]{1,0:T(8,128)(2,1)}, u32[]{:S(2)}, u32[]{:S(2)}) collective-permute-start(bf16[128,256]{1,0:T(8,128)(2,1)S(1)} %pad_maximum_fusion.3), channel_id=1, source_target_pairs={{0,8},{4,12},{8,16},{12,20},{16,24},{20,28},{24,32},{28,36},{32,40... | collective-permute-start | bytes 196616 | tf_op jit(solution)/shard_map/ppermute | solution.py:15
  142.7 2.2 collective-permute-start.2
  145.8 56.8 %all-gather.8.cloned.1.call-done = bf16[2,4096,1,128]{3,0,2,1:T(2,128)(2,1)} async-done(((bf16[2,64,1,128]{3,0,2,1:T(2,128)(2,1)}), bf16[2,4096,1,128]{3,0,2,1:T(2,128)(2,1)}) %all-gather.8.cloned.1.call-update) | async-done | bytes 2097168 | tf_op jit(solution)/shard_map/all_gather | solution.py:106
  202.6 77.8 %all-gather.4.cloned.1.call-done = bf16[2,4096,1,128]{3,1,0,2:T(8,128)(2,1)} async-done(((bf16[2,64,1,128]{3,1,0,2:T(8,128)(2,1)}), bf16[2,4096,1,128]{3,1,0,2:T(8,128)(2,1)}) %all-gather.4.cloned.1.call-update) | async-done | bytes 2097168 | tf_op jit(solution)/shard_map/all_gather | solution.py:105
  280.4 84.7 %while.15 = (s32[]{:T(128)}, f32[128,1,8]{0,2,1:T(8,128)S(1)}, f32[128,1,8]{0,2,1:T(8,128)S(1)}, f32[128,1,8,128]{0,3,2,1:T(8,128)S(1)}, s32[8]{0:T(128)S(1)}, /...) while((s32[]{:T(128)}, f32[128,1,8]{0,2,1:T(8,128)S(1)}, ...), condition=%wide.region_8.9_spmd.clone, body=%wide.region_5.8_spmd.clone.sunk | while | flops 548804864 | bytes 32311012 | solution.py:133
  281.6 3.6 fusion.76
  285.2 1.1 constant_dynamic-slice_fusion.2
  286.5 3.5 fusion.79
  290.1 0.8 fusion.78
  292.2 3.6 fusion.76
  295.8 1.1 constant_dynamic-slice_fusion.2
  297.1 3.5 fusion.79
  300.6 0.8 fusion.78
  302.8 3.6 fusion.76
  306.4 1.1 constant_dynamic-slice_fusion.2
  307.7 3.5 fusion.79
  311.2 0.8 fusion.78
  313.4 3.6 fusion.76
  317.0 1.1 constant_dynamic-slice_fusion.2
  318.3 3.5 fusion.79
  321.8 0.8 fusion.78
  323.9 3.6 fusion.76
  327.6 1.1 constant_dynamic-slice_fusion.2
  328.9 3.5 fusion.79
  332.4 0.8 fusion.78
  334.5 3.6 fusion.76
  338.1 1.1 constant_dynamic-slice_fusion.2
  339.5 3.5 fusion.79
  343.0 0.8 fusion.78
  345.1 3.6 fusion.76
  348.7 1.1 constant_dynamic-slice_fusion.2
  350.1 3.5 fusion.79
  353.6 0.8 fusion.78
  355.7 3.6 fusion.76
  359.3 1.1 constant_dynamic-slice_fusion.2
  360.6 3.5 fusion.79
  364.1 0.8 fusion.78
  365.9 0.9 maximum_maximum_fusion
  369.4 1.0 fusion.37
  (134 shorter events, 15.7 us)
Async XLA Ops:
  7.2 117.8 %copy-start.1 = (bf16[128,8192]{1,0:T(8,128)(2,1)S(1)}, bf16[128,8192]{1,0:T(8,128)(2,1)}, u32[]{:S(2)}) copy-start(bf16[128,8192]{1,0:T(8,128)(2,1)} %param.12) | copy-start | bytes 6291460
  7.2 13.5 %copy-start.3 = (bf16[1024]{0:T(1024)(128)(2,1)S(1)}, bf16[1024]{0:T(1024)(128)(2,1)}, u32[]{:S(2)}) copy-start(bf16[1024]{0:T(1024)(128)(2,1)} %param.15) | copy-start | bytes 6148
  7.2 13.5 %copy-start.4 = (s32[32]{0:T(128)S(1)}, s32[32]{0:T(128)}, u32[]{:S(2)}) copy-start(s32[32]{0:T(128)} %param.21) | copy-start | bytes 388
  7.2 14.6 %copy-start.5 = (bf16[2,128]{1,0:T(2,128)(2,1)S(1)}, bf16[2,128]{1,0:T(2,128)(2,1)}, u32[]{:S(2)}) copy-start(bf16[2,128]{1,0:T(2,128)(2,1)} %param.17) | copy-start | bytes 1540
  7.2 117.7 %all-gather.6.cloned.1.call-start = ((), (), s32[]{:S(2)}) async-start(), calls=%async_computation.1 | async-start | bytes 21299200 | tf_op jit(solution)/shard_map/all_gather | solution.py:84
  10.0 192.6 %all-gather.8.cloned.1.call-start = ((), (), s32[]{:S(2)}) async-start(), calls=%async_computation.2 | async-start | bytes 2129920 | tf_op jit(solution)/shard_map/all_gather | solution.py:106
  11.5 268.9 %all-gather.4.cloned.1.call-start = ((), (), s32[]{:S(2)}) async-start(), calls=%async_computation | async-start | bytes 2129920 | tf_op jit(solution)/shard_map/all_gather | solution.py:105
  135.1 230.8 %copy-start.2 = (bf16[128,128]{1,0:T(8,128)(2,1)}, bf16[128,128]{1,0:T(8,128)(2,1)S(1)}, u32[]{:S(2)}) copy-start(bf16[128,128]{1,0:T(8,128)(2,1)S(1)} %get-tuple-element.139) | copy-start | bytes 98308
  135.2 230.7 %collective-permute-start = (bf16[128,256]{1,0:T(8,128)(2,1)S(1)}, bf16[128,256]{1,0:T(8,128)(2,1)}, u32[]{:S(2)}, u32[]{:S(2)}) collective-permute-start(bf16[128,256]{1,0:T(8,128)(2,1)S(1)} %pad_maximum_fusion.3), channel_id=1, source_target_pairs={{0,12},{4,16},{8,20},{12,24},{16,28},{20,32},{24,36},{28,40},{32,4... | collective-permute-start | bytes 196616 | tf_op jit(solution)/shard_map/ppermute | solution.py:15
  138.2 227.6 %collective-permute-start.1 = (bf16[128,256]{1,0:T(8,128)(2,1)S(1)}, bf16[128,256]{1,0:T(8,128)(2,1)}, u32[]{:S(2)}, u32[]{:S(2)}) collective-permute-start(bf16[128,256]{1,0:T(8,128)(2,1)S(1)} %pad_maximum_fusion.3), channel_id=1, source_target_pairs={{0,8},{4,12},{8,16},{12,20},{16,24},{20,28},{24,32},{28,36},{32,40... | collective-permute-start | bytes 196616 | tf_op jit(solution)/shard_map/ppermute | solution.py:15
  142.7 223.2 %collective-permute-start.2 = (bf16[128,256]{1,0:T(8,128)(2,1)S(1)}, bf16[128,256]{1,0:T(8,128)(2,1)}, u32[]{:S(2)}, u32[]{:S(2)}) collective-permute-start(bf16[128,256]{1,0:T(8,128)(2,1)S(1)} %pad_maximum_fusion.3), channel_id=1, source_target_pairs={{0,4},{4,8},{8,12},{12,16},{16,20},{20,24},{24,28},{28,32},{32,36}... | collective-permute-start | bytes 196616 | tf_op jit(solution)/shard_map/ppermute | solution.py:15
  144.9 135.4 %copy-start.6 = (s32[128]{0:T(128)S(1)}, s32[128]{0:T(128)}, u32[]{:S(2)}) copy-start(s32[128]{0:T(128)} %dynamic_slice.19) | copy-start | bytes 1540
  286.5 3.5 copy-start
  297.1 3.5 copy-start
  307.7 3.5 copy-start
  318.3 3.5 copy-start
  328.9 3.5 copy-start
  339.5 3.5 copy-start
  350.0 3.5 copy-start
  360.6 3.5 copy-start
Sparse Core Ops, SparseCore 0:
  10.8 114.1 all-gather.5
  128.3 74.2 all-gather.7
  205.4 74.8 all-gather.3
where the time goes:
time: 378 us; the launch traced here: 377 us
  waiting for transfers between devices  238 us (63%)
  matrix products  67.8 us (18%)
  local copies, waits for them, and re-layouts  24.4 us (6%)
  other arithmetic  17.2 us (5%)
  between operations  14.1 us (4%)
  starting transfers between devices  9.81 us (3%)
  loops' own time  5.83 us (2%)
    all_gather x1, waiting for transfers between devices, local(): lax.all_gather(combined, 'seq', axis=0, tiled=True)  103 us
    all_gather x1, waiting for transfers between devices, local(): keys_piece = lax.all_gather(prefix_keys, 'seq', axis=1, tiled=True)  77.8 us
    all_gather x1, waiting for transfers between devices, local(): values_piece = lax.all_gather(prefix_values, 'seq', axis=1, tiled=True)  56.8 us
    dot_general x8, matrix products, inner(): jnp.einsum('bgqd,plgd->bgqpl', own_blocks, key_block, preferred_element_t...  28.9 us
    dot_general x8, matrix products, inner(): jnp.einsum('bgqpl,plgd->bgqd', weights.astype(jnp.bfloat16), value_block,...  27.9 us
    dynamic_slice x16, local copies, waits for them, and re-layouts, inner(): lax.dynamic_slice_in_dim(values_piece, block_index * step_rows, step_rows...  10.4 us
    dot_general x1, matrix products, local(): jnp.dot(normed, lax.all_gather(combined, 'seq', axis=0, tiled=True), pref...  9.93 us
    ppermute x3, starting transfers between devices, from_behind(): return lax.ppermute(shard, axis, pairs)  9.69 us
  transfers between devices with their start and end apart: 6, of which 3 were waited for; matrix products, arithmetic and copies ran while one was open for 27% of the time, Pallas kernels for 0%

commit v1 on v0

v1 whole, which is shorter than its diff:
```python
import math

import jax
import jax.numpy as jnp
from jax import lax
from jax.experimental import pallas as pl
from jax.experimental.pallas import tpu as pltpu
from jax.sharding import Mesh
from jax.sharding import PartitionSpec as P

EPS = 1e-06
THETA = 1000000.0
SEQ = ("sx", "sc")


def from_behind(shard, axis, by):
    size = lax.axis_size(axis)
    pairs = [(i, i + by) for i in range(size) if 0 <= i + by < size]
    return lax.ppermute(shard, axis, pairs)


def row_tables(lengths, assignment, all_rows):
    request_end = jnp.cumsum(lengths)
    request_start = request_end - lengths
    row_ids = jnp.arange(all_rows, dtype=jnp.int32)
    segment = jnp.sum((row_ids[:, None] >= request_end[None, :]).astype(jnp.int32), axis=1)
    request_ids = jnp.arange(lengths.shape[0], dtype=jnp.int32)
    onehot = (segment[:, None] == request_ids[None, :]).astype(jnp.int32)
    offset = row_ids - jnp.sum(onehot * request_start[None, :], axis=1)
    prefix = jnp.sum(onehot * assignment[None, :], axis=1)
    return (segment, offset, prefix)


def rotate(values, positions):
    head_size = values.shape[-1]
    half_dim = head_size // 2
    frequency = THETA ** (-2.0 * jnp.arange(half_dim, dtype=jnp.float32) / head_size)
    angles = positions.astype(jnp.float32)[:, None] * frequency[None, :]
    cosine = jnp.concatenate([jnp.cos(angles), jnp.cos(angles)], axis=-1)[:, None, :]
    sine_part = jnp.concatenate([jnp.sin(angles), jnp.sin(angles)], axis=-1)[:, None, :]
    turned = jnp.concatenate([-values[..., half_dim:], values[..., :half_dim]], axis=-1)
    return values * cosine + turned * sine_part


def attention_kernel(q_ref, row_ref, col_ref, kv_ref, near_ref, o_ref, *, head_dim, scale):
    d = head_dim
    dims = (((1,), (1,)), ((), ()))
    q = q_ref[...]
    rows = row_ref[...]
    use_first = rows[:, 0:1] == 0
    row_seg = rows[:, 1:2]
    row_idx = rows[:, 2:3]
    cols = col_ref[...]
    far0 = lax.dot_general(q, kv_ref[:, 0:d], dims, preferred_element_type=jnp.float32) * scale
    far1 = lax.dot_general(q, kv_ref[:, d : 2 * d], dims, preferred_element_type=jnp.float32) * scale
    far = jnp.where(use_first, far0, far1)
    near = lax.dot_general(q, near_ref[:, 0:d], dims, preferred_element_type=jnp.float32) * scale
    visible = (cols[0:1, :] == row_seg) & (cols[1:2, :] <= row_idx)
    near = jnp.where(visible, near, -jnp.inf)
    top = jnp.maximum(jnp.max(far, axis=1, keepdims=True), jnp.max(near, axis=1, keepdims=True))
    far_w = jnp.exp(far - top)
    near_w = jnp.exp(near - top)
    mass = jnp.sum(far_w, axis=1, keepdims=True) + jnp.sum(near_w, axis=1, keepdims=True)
    far_b = far_w.astype(jnp.bfloat16)
    zero = jnp.zeros_like(far_b)
    acc = jnp.dot(jnp.where(use_first, far_b, zero), kv_ref[:, 2 * d : 3 * d], preferred_element_type=jnp.float32)
    acc = acc + jnp.dot(jnp.where(use_first, zero, far_b), kv_ref[:, 3 * d : 4 * d], preferred_element_type=jnp.float32)
    acc = acc + jnp.dot(near_w.astype(jnp.bfloat16), near_ref[:, d : 2 * d], preferred_element_type=jnp.float32)
    o_ref[...] = (acc / mass).astype(o_ref.dtype)


def attend(q_rows, row_info, col_info, kv_slab, near_slab, head_dim):
    n_rows = q_rows.shape[0]
    block = math.gcd(n_rows, 256)
    cache_len = kv_slab.shape[0]
    near_len = near_slab.shape[0]
    kernel = lambda *refs: attention_kernel(*refs, head_dim=head_dim, scale=head_dim ** (-0.5))
    keys_total = 2 * cache_len + near_len
    cost = pl.CostEstimate(
        flops=4 * n_rows * keys_total * head_dim,
        transcendentals=n_rows * (cache_len + near_len),
        bytes_accessed=kv_slab.size * 2 + near_slab.size * 2 + q_rows.size * 4,
    )
    return pl.pallas_call(
        kernel,
        grid=(n_rows // block,),
        in_specs=[
            pl.BlockSpec((block, head_dim), lambda i: (i, 0)),
            pl.BlockSpec((block, row_info.shape[1]), lambda i: (i, 0)),
            pl.BlockSpec(col_info.shape, lambda i: (0, 0)),
            pl.BlockSpec(kv_slab.shape, lambda i: (0, 0)),
            pl.BlockSpec(near_slab.shape, lambda i: (0, 0)),
        ],
        out_specs=pl.BlockSpec((block, head_dim), lambda i: (i, 0)),
        out_shape=jax.ShapeDtypeStruct((n_rows, head_dim), jnp.bfloat16),
        cost_estimate=cost,
        compiler_params=pltpu.CompilerParams(vmem_limit_bytes=48 * 1024 * 1024),
    )(q_rows, row_info, col_info, kv_slab, near_slab)


def local(
    hidden,
    gain,
    w_query,
    q_bias,
    w_keyval,
    kv_bias,
    prefix_keys,
    prefix_values,
    lengths,
    assignment,
):
    row_count = hidden.shape[0]
    pair_count = lax.axis_size("sc")
    seq_count = lax.axis_size("sx") * pair_count
    seq_index = lax.axis_index("sx") * pair_count + lax.axis_index("sc")
    all_rows = row_count * seq_count
    head_dim = prefix_keys.shape[3]
    kv_local = prefix_keys.shape[2]
    query_width = w_query.shape[1]
    heads_local = query_width // head_dim
    pair_width = w_keyval.shape[1] * w_keyval.shape[2]
    key_width = pair_width // 2
    cache_length = prefix_keys.shape[1] * seq_count
    first_row = seq_index * row_count
    hidden_f = hidden.astype(jnp.float32)
    normed = (
        hidden_f
        * lax.rsqrt(jnp.mean(hidden_f * hidden_f, axis=1, keepdims=True) + EPS)
        * gain.astype(jnp.float32)
    ).astype(jnp.bfloat16)
    segment, offset, prefix = row_tables(lengths, assignment, all_rows)
    positions = offset + cache_length
    own_positions = lax.dynamic_slice_in_dim(positions, first_row, row_count)
    own_segment = lax.dynamic_slice_in_dim(segment, first_row, row_count)
    own_prefix = lax.dynamic_slice_in_dim(prefix, first_row, row_count)

    slab = jnp.concatenate(
        [prefix_keys[0, :, 0, :], prefix_keys[1, :, 0, :], prefix_values[0, :, 0, :], prefix_values[1, :, 0, :]],
        axis=1,
    )

    w_pairs = w_keyval.reshape(w_keyval.shape[0], pair_width)
    combined = jnp.concatenate([w_query, w_pairs], axis=1)
    total_width = combined.shape[1]
    half_width = total_width // pair_count
    halves = lax.all_to_all(
        combined.reshape(row_count, pair_count, half_width), "sc", 1, 0, tiled=True
    ).reshape(row_count * pair_count, half_width)
    w_half = lax.all_gather(halves, "sx", axis=0, tiled=True)
    kv_slab = lax.all_gather(slab, SEQ, axis=0, tiled=True)
    normed_pair = lax.all_gather(normed, "sc", axis=0, tiled=True)
    part = jnp.dot(normed_pair, w_half, preferred_element_type=jnp.float32)
    summed = lax.all_to_all(
        part.reshape(pair_count, row_count, 1, half_width), "sc", 0, 2, tiled=True
    ).reshape(row_count, total_width)
    bias = jnp.concatenate([q_bias, kv_bias.reshape(pair_width)]).astype(jnp.float32)
    summed = summed + bias
    query_own = summed[:, :query_width]
    pairs_own = summed[:, query_width:]
    own_queries = rotate(query_own.reshape(row_count, heads_local, head_dim), own_positions).astype(
        jnp.bfloat16
    )
    own_keys = rotate(
        pairs_own[:, :key_width].reshape(row_count, kv_local, head_dim), own_positions
    ).astype(jnp.bfloat16)
    own_values = (
        pairs_own[:, key_width:].reshape(row_count, kv_local, head_dim).astype(jnp.bfloat16)
    )
    pair_rows = jnp.concatenate(
        [own_keys.reshape(row_count, key_width), own_values.reshape(row_count, key_width)], axis=1
    )
    depth = min(3, seq_count - 1)
    earlier = []
    for distance in range(depth, 0, -1):
        earlier.append(from_behind(pair_rows, SEQ, distance))
    near_rows = jnp.concatenate(earlier + [pair_rows], axis=0)
    near_count = near_rows.shape[0]
    near_index = first_row - depth * row_count + jnp.arange(near_count, dtype=jnp.int32)
    near_segment = segment[jnp.clip(near_index, 0, all_rows - 1)]
    near_segment = jnp.where(near_index >= 0, near_segment, -1)
    col_info = jnp.concatenate(
        [near_segment[None, :], near_index[None, :], jnp.zeros((6, near_count), jnp.int32)], axis=0
    )
    own_rows = first_row + jnp.arange(row_count, dtype=jnp.int32)
    row_info = jnp.stack(
        [own_prefix, own_segment, own_rows, jnp.zeros_like(own_rows)], axis=1
    ).astype(jnp.int32)
    row_info = jnp.repeat(row_info, heads_local, axis=0)
    out_rows = attend(
        own_queries.reshape(row_count * heads_local, head_dim),
        row_info,
        col_info,
        kv_slab,
        near_rows,
        head_dim,
    )
    attention = out_rows.reshape(row_count, query_width)
    return (attention, own_keys, own_values)


def solution(mesh):
    seq_size = mesh.shape["seq"]
    grid = Mesh(
        mesh.devices.reshape(seq_size // 2, 2, mesh.shape["tensor"]), ("sx", "sc", "tensor")
    )
    in_specs = (
        P(SEQ, None),
        P(),
        P(SEQ, "tensor"),
        P("tensor"),
        P(SEQ, None, "tensor"),
        P(None, "tensor"),
        P(None, SEQ, "tensor", None),
        P(None, SEQ, "tensor", None),
        P(),
        P(),
    )
    out_specs = (P(SEQ, "tensor"), P(SEQ, "tensor", None), P(SEQ, "tensor", None))
    return jax.shard_map(local, mesh=grid, in_specs=in_specs, out_specs=out_specs, check_vma=False)
```

time: 378 us -> 254 us (0.67)
  waiting for transfers between devices: 238 us -> 176 us
  matrix products: 67.8 us -> 8.26 us
  local copies, waits for them, and re-layouts: 24.4 us -> 9.34 us
  Pallas kernels: 0 us -> 14.8 us
  blocking collectives: 0 us -> 12.1 us
  other arithmetic: 17.2 us -> 9.09 us
  loops' own time: 5.83 us -> 0 us
    all_gather x3, waiting for transfers between devices: 237 us -> 176 us  [the longest x1 111 us: local(): w_half = lax.all_gather(halves, 'sx', axis=0, tiled=True)]
    dot_general x19 -> x1, matrix products: 67.8 us -> 8.26 us  [local(): part = jnp.dot(normed_pair, w_half, preferred_element_type=jnp.float32)]
    dynamic_slice x26 -> x0, local copies, waits for them, and re-layouts: 15.8 us -> none  [the longest x16 10.4 us: inner(): lax.dynamic_slice_in_dim(values_piece, block_index * step_rows, step_rows...]
    pallas_call x0 -> x1, Pallas kernels: none -> 14.8 us  [attend(): pl.pallas_call(kernel, grid=(n_rows // block,), in_specs=[pl.BlockSpec((b...]
    all_to_all x0 -> x2, blocking collectives: none -> 12.1 us  [the longest x1 6.83 us: local(): lax.all_to_all(combined.reshape(row_count, pair_count, half_width), 'sc',...]
    reduce_sum x9 -> x0, other arithmetic: 7 us -> none  [the longest x8 6.71 us: inner(): new_mass = run_mass * keep_share + jnp.sum(weights, axis=(3, 4))]
    another operation x1 -> x0, loops' own time: 5.83 us -> none  [local(): lax.scan(inner, initial, jnp.arange(piece_len // step_rows, dtype=jnp.int...]
  transfers between devices with their start and end apart: 6 -> 6, of which waited for: 3 -> 4; matrix products, arithmetic and copies ran while one was open for 27% -> 7% of each run, Pallas kernels for 0% -> 0%
where the time goes in v1:
time: 254 us; the launch traced here: 253 us
  waiting for transfers between devices  176 us (69%)
  Pallas kernels  14.8 us (6%)
  between operations  14.1 us (6%)
  blocking collectives  12.1 us (5%)
  starting transfers between devices  9.51 us (4%)
  local copies, waits for them, and re-layouts  9.34 us (4%)
  other arithmetic  9.09 us (4%)
  matrix products  8.26 us (3%)
    all_gather x1, waiting for transfers between devices, local(): w_half = lax.all_gather(halves, 'sx', axis=0, tiled=True)  111 us
    all_gather x1, waiting for transfers between devices, local(): kv_slab = lax.all_gather(slab, SEQ, axis=0, tiled=True)  55.3 us
    pallas_call x1, Pallas kernels, attend(): pl.pallas_call(kernel, grid=(n_rows // block,), in_specs=[pl.BlockSpec((b...  14.8 us
    all_gather x1, waiting for transfers between devices, local(): normed_pair = lax.all_gather(normed, 'sc', axis=0, tiled=True)  9.69 us
    ppermute x3, starting transfers between devices, from_behind(): return lax.ppermute(shard, axis, pairs)  9.39 us
    dot_general x1, matrix products, local(): part = jnp.dot(normed_pair, w_half, preferred_element_type=jnp.float32)  8.26 us
    all_to_all x1, blocking collectives, local(): lax.all_to_all(combined.reshape(row_count, pair_count, half_width), 'sc',...  6.83 us
    all_to_all x1, blocking collectives, local(): lax.all_to_all(part.reshape(pair_count, row_count, 1, half_width), 'sc',...  5.28 us
  transfers between devices with their start and end apart: 6, of which 4 were waited for; matrix products, arithmetic and copies ran while one was open for 7% of the time, Pallas kernels for 0%

profile of v1, /device:TPU:1, one launch (start us, length us, event | category | flops | bytes accessed | tf_op | source)
XLA Modules:
  0.0 253.1 jit_solution(13874389283485245414)
XLA Ops:
  7.2 0.0 all-gather.4.cloned.1.call-start
  7.2 0.7 convert_element_type.39
  7.9 2.1 fusion
  10.1 3.5 %fusion.2 = bf16[128,8192]{1,0:T(8,128)(2,1)} fusion(bf16[128,8192]{1,0:T(8,128)(2,1)} %param.10, f32[8192]{0:T(1024)S(1)} %convert_element_type.39, f32[128]{0:T(128)S(1)} %add_rsqrt_fusion), kind=kLoop, calls=%fused_computation.5 | loop fusion | flops 4194304 | bytes 4227584 | tf_op jit(solution)/shard_map/convert_element_type | solution.py:131
  13.7 0.0 all-gather.6.cloned.1.call-start
  13.7 0.1 copy.32
  13.8 0.2 copy.33
  14.1 6.8 %all_to_all.30 = bf16[128,2,640]{0,2,1:T(8,128)(2,1)S(1)} all-to-all(bf16[128,2,640]{0,2,1:T(8,128)(2,1)S(1)} %bitcast.64), channel_id=1, replica_groups=mesh['sx'=32,'sc'=2,'tensor'=4] {'sc'}, dimensions={1} | all-to-all | bytes 655360 | tf_op jit(solution)/shard_map/all_to_all | solution.py:147
  20.9 0.9 copy.34
  21.8 0.0 all-gather.6.cloned.1.call-update
  21.8 0.0 all-gather.8.cloned.1.call-start
  21.9 0.6 pad_maximum_fusion.3
  22.5 0.0 all-gather.8.cloned.1.call-update
  22.6 0.1 copy.37
  22.7 0.1 reduce-window.8
  22.7 0.1 reduce
  22.8 0.1 pad.19.clone
  22.9 0.2 convert_reduce_fusion
  23.2 0.4 select_reduce_fusion
  23.6 0.1 dynamic-slice_bitcast_fusion
  23.6 0.1 add_add_fusion.1
  23.7 0.1 copy.38
  23.8 3.1 %gather_fusion = s32[512]{0:T(512)S(1)} fusion(s32[8192]{0:T(1024)S(1)} %convert_reduce_fusion, s32[1024]{0:T(1024)S(1)} %pad_clamp_fusion), kind=kCustom, calls=%fused_computation | custom fusion | bytes 6144 | tf_op jit(solution)/shard_map/gather | solution.py:180
  27.0 0.1 pad.15.clone
  27.1 0.1 fusion.10
  27.2 0.1 add_add_fusion.refs_2_
  27.3 0.3 multiply_cosine_fusion
  27.6 9.7 %all-gather.4.cloned.1.call-done = bf16[256,8192]{1,0:T(8,128)(2,1)} async-done(((bf16[128,8192]{1,0:T(8,128)(2,1)}), bf16[256,8192]{1,0:T(8,128)(2,1)}) %all-gather.4.cloned.1.call-update) | async-done | bytes 4194320 | tf_op jit(solution)/shard_map/all_gather | solution.py:152
  37.3 110.8 %all-gather.6.cloned.1.call-done = bf16[8192,640]{1,0:T(8,128)(2,1)} async-done(((bf16[256,640]{1,0:T(8,128)(2,1)}), bf16[8192,640]{1,0:T(8,128)(2,1)}) %all-gather.6.cloned.1.call-update) | async-done | bytes 10485776 | tf_op jit(solution)/shard_map/all_gather | solution.py:150
  148.2 8.3 %fusion.12 = f32[256,640]{1,0:T(8,128)S(1)} fusion(bf16[256,8192]{1,0:T(8,128)(2,1)} %all-gather.4.cloned.1.call-done, bf16[8192,640]{1,0:T(8,128)(2,1)} %all-gather.6.cloned.1.call-done), kind=kOutput, calls=%fused_computation.58 | convolution fusion | flops 2684354560 | bytes 15335424 | tf_op jit(solution)/shard_map/dot_general | solution.py:153
  156.4 5.3 %all_to_all.31 = f32[2,128,1,640]{3,1,2,0:T(8,128)S(1)} all-to-all(f32[2,128,1,640]{3,1,2,0:T(8,128)S(1)} %bitcast.66), channel_id=1, replica_groups=mesh['sx'=32,'sc'=2,'tensor'=4] {'sc'}, dimensions={0} | all-to-all | bytes 1310720 | tf_op jit(solution)/shard_map/all_to_all | solution.py:154
  161.7 0.5 copy.36
  162.4 0.1 fusion.6
  162.4 0.1 fusion.8
  162.6 1.9 collective-permute-start.2
  164.5 2.9 %collective-permute-start.1 = (bf16[128,256]{1,0:T(8,128)(2,1)S(1)}, bf16[128,256]{1,0:T(8,128)(2,1)S(1)}, u32[]{:S(2)}, u32[]{:S(2)}) collective-permute-start(bf16[128,256]{1,0:T(8,128)(2,1)S(1)} %pad_maximum_fusion.4), channel_id=1, source_target_pairs={{0,8},{4,12},{8,16},{12,20},{16,24},{20,28},{24,32},{28,36},{32,40... | collective-permute-start | bytes 196616 | tf_op jit(solution)/shard_map/ppermute | solution.py:19
  167.5 4.5 %collective-permute-start = (bf16[128,256]{1,0:T(8,128)(2,1)S(1)}, bf16[128,256]{1,0:T(8,128)(2,1)S(1)}, u32[]{:S(2)}, u32[]{:S(2)}) collective-permute-start(bf16[128,256]{1,0:T(8,128)(2,1)S(1)} %pad_maximum_fusion.4), channel_id=1, source_target_pairs={{0,12},{4,16},{8,20},{12,24},{16,28},{20,32},{24,36},{28,40},{32,4... | collective-permute-start | bytes 196616 | tf_op jit(solution)/shard_map/ppermute | solution.py:19
  172.0 0.1 fusion.11
  172.1 0.1 copy.40
  172.2 0.1 reshape.164
  172.3 0.2 fusion.3
  172.5 0.2 fusion.5.refs_0_
  172.8 0.6 slice_bitcast_fusion.8
  173.4 0.1 collective-permute-done
  173.5 55.3 %all-gather.8.cloned.1.call-done.refs_3_ = bf16[4096,512]{1,0:T(8,128)(2,1)} async-done(((bf16[64,512]{1,0:T(8,128)(2,1)}), bf16[4096,512]{1,0:T(8,128)(2,1)}) %all-gather.8.cloned.1.call-update) | async-done | bytes 4194320 | tf_op jit(solution)/shard_map/all_gather | solution.py:151
  228.8 2.2 copy-done
  231.0 14.8 %shard_map.121 = bf16[1024,128]{1,0:T(8,128)(2,1)S(1)} custom-call(bf16[1024,128]{1,0:T(8,128)(2,1)S(1)} %fusion.5.refs_0_, s32[1024,4]{1,0:T(8,128)S(1)} %broadcast_bitcast_fusion.refs_1_, s32[8,512]{1,0:T(8,128)S(1)} %add_add_fusion.refs_2_, bf16[4096,512]{1,0:T(8,128)(2,1)S(1)} %copy-done, bf16[512,256]{1,0:T(8,128)(2,1)S(1)} %maximum_maximum_fusion.refs_4_), custom_call_target="tpu_custom_call" | custom-call | flops 4563402752 | bytes 4980736 | tf_op jit(solution)/shard_map/pallas_call | solution.py:84
  245.8 0.8 reshape.170
  (40 shorter events, 0.3 us)
Async XLA Ops:
  7.2 30.2 %all-gather.4.cloned.1.call-start = ((), (), s32[]{:S(2)}) async-start(), calls=%async_computation.2 | async-start | bytes 6291456 | tf_op jit(solution)/shard_map/all_gather | solution.py:152
  7.9 5.8 %copy-start.3 = (bf16[128,2,128]{2,1,0:T(2,128)(2,1)S(1)}, bf16[128,2,128]{2,1,0:T(2,128)(2,1)}, u32[]{:S(2)}) copy-start(bf16[128,2,128]{2,1,0:T(2,128)(2,1)} %param.14) | copy-start | bytes 196612
  7.9 5.9 %copy-start.2 = (bf16[128,1024]{1,0:T(8,128)(2,1)S(1)}, bf16[128,1024]{1,0:T(8,128)(2,1)}, u32[]{:S(2)}) copy-start(bf16[128,1024]{1,0:T(8,128)(2,1)} %param.12) | copy-start | bytes 786436
  10.1 11.8 %copy-start.4 = (bf16[2,64,1,128]{3,1,2,0:T(8,128)(2,1)S(1)}, bf16[2,64,1,128]{3,1,2,0:T(8,128)(2,1)}, u32[]{:S(2)}) copy-start(bf16[2,64,1,128]{3,1,2,0:T(8,128)(2,1)} %param.17) | copy-start | bytes 98308
  10.1 11.8 %copy-start.5 = (bf16[2,64,1,128]{3,1,2,0:T(8,128)(2,1)S(1)}, bf16[2,64,1,128]{3,1,2,0:T(8,128)(2,1)}, u32[]{:S(2)}) copy-start(bf16[2,64,1,128]{3,1,2,0:T(8,128)(2,1)} %param.16) | copy-start | bytes 98308
  10.1 12.5 %copy-start.8 = (s32[32]{0:T(128)S(1)}, s32[32]{0:T(128)}, u32[]{:S(2)}) copy-start(s32[32]{0:T(128)} %param.18) | copy-start | bytes 388
  10.1 13.1 %copy-start.7 = (s32[32]{0:T(128)S(1)}, s32[32]{0:T(128)}, u32[]{:S(2)}) copy-start(s32[32]{0:T(128)} %param.19) | copy-start | bytes 388
  13.6 13.5 %copy-start.6 = (bf16[1024]{0:T(1024)(128)(2,1)S(1)}, bf16[1024]{0:T(1024)(128)(2,1)}, u32[]{:S(2)}) copy-start(bf16[1024]{0:T(1024)(128)(2,1)} %param.13) | copy-start | bytes 6148
  13.6 13.6 %copy-start.9 = (bf16[2,128]{1,0:T(2,128)(2,1)S(1)}, bf16[2,128]{1,0:T(2,128)(2,1)}, u32[]{:S(2)}) copy-start(bf16[2,128]{1,0:T(2,128)(2,1)} %param.15) | copy-start | bytes 1540
  13.7 134.5 %all-gather.6.cloned.1.call-start = ((), (), s32[]{:S(2)}) async-start(), calls=%async_computation.3 | async-start | bytes 10813440 | tf_op jit(solution)/shard_map/all_gather | solution.py:150
  21.8 207.0 %all-gather.8.cloned.1.call-start = ((), (), s32[]{:S(2)}) async-start(), calls=%async_computation.4 | async-start | bytes 4259840 | tf_op jit(solution)/shard_map/all_gather | solution.py:151
  162.6 10.9 %copy-start.1 = (bf16[128,128]{1,0:T(8,128)(2,1)}, bf16[128,128]{1,0:T(8,128)(2,1)S(1)}, u32[]{:S(2)}) copy-start(bf16[128,128]{1,0:T(8,128)(2,1)S(1)} %get-tuple-element.9) | copy-start | bytes 98308
  162.6 10.8 %collective-permute-start.2 = (bf16[128,256]{1,0:T(8,128)(2,1)S(1)}, bf16[128,256]{1,0:T(8,128)(2,1)S(1)}, u32[]{:S(2)}, u32[]{:S(2)}) collective-permute-start(bf16[128,256]{1,0:T(8,128)(2,1)S(1)} %pad_maximum_fusion.4), channel_id=1, source_target_pairs={{0,4},{4,8},{8,12},{12,16},{16,20},{20,24},{24,28},{28,32},{32,36}... | collective-permute-start | bytes 196616 | tf_op jit(solution)/shard_map/ppermute | solution.py:19
  164.5 8.9 %collective-permute-start.1 = (bf16[128,256]{1,0:T(8,128)(2,1)S(1)}, bf16[128,256]{1,0:T(8,128)(2,1)S(1)}, u32[]{:S(2)}, u32[]{:S(2)}) collective-permute-start(bf16[128,256]{1,0:T(8,128)(2,1)S(1)} %pad_maximum_fusion.4), channel_id=1, source_target_pairs={{0,8},{4,12},{8,16},{12,20},{16,24},{20,28},{24,32},{28,36},{32,40... | collective-permute-start | bytes 196616 | tf_op jit(solution)/shard_map/ppermute | solution.py:19
  167.5 6.0 %collective-permute-start = (bf16[128,256]{1,0:T(8,128)(2,1)S(1)}, bf16[128,256]{1,0:T(8,128)(2,1)S(1)}, u32[]{:S(2)}, u32[]{:S(2)}) collective-permute-start(bf16[128,256]{1,0:T(8,128)(2,1)S(1)} %pad_maximum_fusion.4), channel_id=1, source_target_pairs={{0,12},{4,16},{8,20},{12,24},{16,28},{20,32},{24,36},{28,40},{32,4... | collective-permute-start | bytes 196616 | tf_op jit(solution)/shard_map/ppermute | solution.py:19
  228.8 2.2 copy-start
Sparse Core Ops, SparseCore 0:
  13.8 23.5 all-gather.3
  39.9 108.2 all-gather.5
  151.5 77.2 all-gather.7

commit v2 on v1

v2 whole, which is shorter than its diff:
```python
import math

import jax
import jax.numpy as jnp
from jax import lax
from jax.experimental import pallas as pl
from jax.experimental.pallas import tpu as pltpu
from jax.sharding import PartitionSpec as P

EPS = 1e-06
THETA = 1000000.0


def from_behind(shard, axis, by):
    size = lax.axis_size(axis)
    pairs = [(i, i + by) for i in range(size) if 0 <= i + by < size]
    return lax.ppermute(shard, axis, pairs)


def row_tables(lengths, assignment, all_rows):
    request_end = jnp.cumsum(lengths)
    request_start = request_end - lengths
    row_ids = jnp.arange(all_rows, dtype=jnp.int32)
    segment = jnp.sum((row_ids[:, None] >= request_end[None, :]).astype(jnp.int32), axis=1)
    request_ids = jnp.arange(lengths.shape[0], dtype=jnp.int32)
    onehot = (segment[:, None] == request_ids[None, :]).astype(jnp.int32)
    offset = row_ids - jnp.sum(onehot * request_start[None, :], axis=1)
    prefix = jnp.sum(onehot * assignment[None, :], axis=1)
    return (segment, offset, prefix)


def rotate(values, positions):
    head_size = values.shape[-1]
    half_dim = head_size // 2
    frequency = THETA ** (-2.0 * jnp.arange(half_dim, dtype=jnp.float32) / head_size)
    angles = positions.astype(jnp.float32)[:, None] * frequency[None, :]
    cosine = jnp.concatenate([jnp.cos(angles), jnp.cos(angles)], axis=-1)[:, None, :]
    sine_part = jnp.concatenate([jnp.sin(angles), jnp.sin(angles)], axis=-1)[:, None, :]
    turned = jnp.concatenate([-values[..., half_dim:], values[..., :half_dim]], axis=-1)
    return values * cosine + turned * sine_part


def attention_kernel(q_ref, row_ref, col_ref, kv_ref, near_ref, o_ref, *, head_dim, packs, scale):
    d = head_dim
    dims = (((1,), (1,)), ((), ()))
    q = q_ref[...]
    rows = row_ref[...]
    use_first = rows[:, 0:1] == 0
    row_seg = rows[:, 1:2]
    row_idx = rows[:, 2:3]
    cols = col_ref[...]
    n_dev, n_sub = kv_ref.shape[0], kv_ref.shape[1]

    def piece(j):
        return kv_ref[:, :, j * d : (j + 1) * d].reshape(n_dev * n_sub, d)

    far = []
    for k in range(packs):
        far0 = lax.dot_general(q, piece(4 * k), dims, preferred_element_type=jnp.float32) * scale
        far1 = lax.dot_general(q, piece(4 * k + 1), dims, preferred_element_type=jnp.float32) * scale
        far.append(jnp.where(use_first, far0, far1))
    near = lax.dot_general(q, near_ref[:, 0:d], dims, preferred_element_type=jnp.float32) * scale
    visible = (cols[0:1, :] == row_seg) & (cols[1:2, :] <= row_idx)
    near = jnp.where(visible, near, -jnp.inf)
    top = jnp.max(near, axis=1, keepdims=True)
    for s in far:
        top = jnp.maximum(top, jnp.max(s, axis=1, keepdims=True))
    near_w = jnp.exp(near - top)
    mass = jnp.sum(near_w, axis=1, keepdims=True)
    acc = jnp.dot(near_w.astype(jnp.bfloat16), near_ref[:, d : 2 * d], preferred_element_type=jnp.float32)
    for k, s in enumerate(far):
        far_w = jnp.exp(s - top)
        mass = mass + jnp.sum(far_w, axis=1, keepdims=True)
        far_b = far_w.astype(jnp.bfloat16)
        zero = jnp.zeros_like(far_b)
        acc = acc + jnp.dot(jnp.where(use_first, far_b, zero), piece(4 * k + 2), preferred_element_type=jnp.float32)
        acc = acc + jnp.dot(jnp.where(use_first, zero, far_b), piece(4 * k + 3), preferred_element_type=jnp.float32)
    o_ref[...] = (acc / mass).astype(o_ref.dtype)


def attend(q_rows, row_info, col_info, gathered, kv_block, kv_rows, near_slab, head_dim):
    n_rows = q_rows.shape[0]
    block = math.gcd(n_rows, 256)
    n_dev = gathered.shape[0]
    width = gathered.shape[2]
    packs = width // (4 * head_dim)
    cache_len = n_dev * kv_rows * packs
    near_len = near_slab.shape[0]
    kernel = lambda *refs: attention_kernel(*refs, head_dim=head_dim, packs=packs, scale=head_dim ** (-0.5))
    keys_total = 2 * cache_len + near_len
    cost = pl.CostEstimate(
        flops=4 * n_rows * keys_total * head_dim,
        transcendentals=n_rows * (cache_len + near_len),
        bytes_accessed=n_dev * kv_rows * width * 2 + near_slab.size * 2 + q_rows.size * 4,
    )
    return pl.pallas_call(
        kernel,
        grid=(n_rows // block,),
        in_specs=[
            pl.BlockSpec((block, head_dim), lambda i: (i, 0)),
            pl.BlockSpec((block, row_info.shape[1]), lambda i: (i, 0)),
            pl.BlockSpec(col_info.shape, lambda i: (0, 0)),
            pl.BlockSpec((n_dev, kv_rows, width), lambda i: (0, kv_block, 0)),
            pl.BlockSpec(near_slab.shape, lambda i: (0, 0)),
        ],
        out_specs=pl.BlockSpec((block, head_dim), lambda i: (i, 0)),
        out_shape=jax.ShapeDtypeStruct((n_rows, head_dim), jnp.bfloat16),
        cost_estimate=cost,
        compiler_params=pltpu.CompilerParams(vmem_limit_bytes=48 * 1024 * 1024),
    )(q_rows, row_info, col_info, gathered, near_slab)


def local(
    hidden,
    gain,
    w_query,
    q_bias,
    w_keyval,
    kv_bias,
    prefix_keys,
    prefix_values,
    lengths,
    assignment,
):
    row_count = hidden.shape[0]
    seq_count = lax.axis_size("seq")
    seq_index = lax.axis_index("seq")
    all_rows = row_count * seq_count
    head_dim = prefix_keys.shape[3]
    kv_local = prefix_keys.shape[2]
    query_width = w_query.shape[1]
    heads_local = query_width // head_dim
    pair_width = w_keyval.shape[1] * w_keyval.shape[2]
    key_width = pair_width // 2
    cache_local = prefix_keys.shape[1]
    cache_length = cache_local * seq_count
    first_row = seq_index * row_count
    hidden_f = hidden.astype(jnp.float32)
    normed = (
        hidden_f
        * lax.rsqrt(jnp.mean(hidden_f * hidden_f, axis=1, keepdims=True) + EPS)
        * gain.astype(jnp.float32)
    ).astype(jnp.bfloat16)
    segment, offset, prefix = row_tables(lengths, assignment, all_rows)
    positions = offset + cache_length
    own_positions = lax.dynamic_slice_in_dim(positions, first_row, row_count)
    own_segment = lax.dynamic_slice_in_dim(segment, first_row, row_count)
    own_prefix = lax.dynamic_slice_in_dim(prefix, first_row, row_count)

    w_pairs = w_keyval.reshape(w_keyval.shape[0], pair_width)
    combined = jnp.concatenate([w_query, w_pairs], axis=1)
    total_width = combined.shape[1]
    entry = 4 * head_dim
    packs = total_width // entry
    kv_rows = -(-cache_local // packs)
    kv_rows = -(-kv_rows // 16) * 16
    slab = jnp.concatenate(
        [prefix_keys[0, :, 0, :], prefix_keys[1, :, 0, :], prefix_values[0, :, 0, :], prefix_values[1, :, 0, :]],
        axis=1,
    )
    slab = jnp.pad(slab, ((0, kv_rows * packs - cache_local), (0, 0)))
    slab = slab.reshape(packs, kv_rows, entry).transpose(1, 0, 2).reshape(kv_rows, packs * entry)
    slab = jnp.pad(slab, ((0, 0), (0, total_width - packs * entry)))
    assert kv_rows * packs == cache_local and row_count % kv_rows == 0
    block_rows = row_count + kv_rows
    gathered = lax.all_gather(jnp.concatenate([combined, slab], axis=0), "seq", axis=0, tiled=True)
    gathered = gathered.reshape(seq_count, block_rows, total_width)
    w_full = gathered[:, :row_count, :].reshape(seq_count * row_count, total_width)
    summed = jnp.dot(normed, w_full, preferred_element_type=jnp.float32)
    bias = jnp.concatenate([q_bias, kv_bias.reshape(pair_width)]).astype(jnp.float32)
    summed = summed + bias
    query_own = summed[:, :query_width]
    pairs_own = summed[:, query_width:]
    own_queries = rotate(query_own.reshape(row_count, heads_local, head_dim), own_positions).astype(
        jnp.bfloat16
    )
    own_keys = rotate(
        pairs_own[:, :key_width].reshape(row_count, kv_local, head_dim), own_positions
    ).astype(jnp.bfloat16)
    own_values = (
        pairs_own[:, key_width:].reshape(row_count, kv_local, head_dim).astype(jnp.bfloat16)
    )
    pair_rows = jnp.concatenate(
        [own_keys.reshape(row_count, key_width), own_values.reshape(row_count, key_width)], axis=1
    )
    depth = min(3, seq_count - 1)
    earlier = []
    for distance in range(depth, 0, -1):
        earlier.append(from_behind(pair_rows, "seq", distance))
    near_rows = jnp.concatenate(earlier + [pair_rows], axis=0)
    near_count = near_rows.shape[0]
    near_index = first_row - depth * row_count + jnp.arange(near_count, dtype=jnp.int32)
    near_segment = segment[jnp.clip(near_index, 0, all_rows - 1)]
    near_segment = jnp.where(near_index >= 0, near_segment, -1)
    col_info = jnp.concatenate(
        [near_segment[None, :], near_index[None, :], jnp.zeros((6, near_count), jnp.int32)], axis=0
    )
    own_rows = first_row + jnp.arange(row_count, dtype=jnp.int32)
    row_info = jnp.stack(
        [own_prefix, own_segment, own_rows, jnp.zeros_like(own_rows)], axis=1
    ).astype(jnp.int32)
    row_info = jnp.repeat(row_info, heads_local, axis=0)
    out_rows = attend(
        own_queries.reshape(row_count * heads_local, head_dim),
        row_info,
        col_info,
        gathered,
        row_count // kv_rows,
        kv_rows,
        near_rows,
        head_dim,
    )
    attention = out_rows.reshape(row_count, query_width)
    return (attention, own_keys, own_values)


def solution(mesh):
    in_specs = (
        P("seq", None),
        P(),
        P("seq", "tensor"),
        P("tensor"),
        P("seq", None, "tensor"),
        P(None, "tensor"),
        P(None, "seq", "tensor", None),
        P(None, "seq", "tensor", None),
        P(),
        P(),
    )
    out_specs = (P("seq", "tensor"), P("seq", "tensor", None), P("seq", "tensor", None))
    return jax.shard_map(local, mesh=mesh, in_specs=in_specs, out_specs=out_specs, check_vma=False)
```

time: 254 us -> 191 us (0.75)
  waiting for transfers between devices: 176 us -> 119 us
  blocking collectives: 12.1 us -> 0 us
  local copies, waits for them, and re-layouts: 9.34 us -> 19 us
  matrix products: 8.26 us -> 2.95 us
    all_gather x3 -> x1, waiting for transfers between devices: 176 us -> 119 us  [local(): lax.all_gather(jnp.concatenate([combined, slab], axis=0), 'seq', axis=0,...]
    all_to_all x2 -> x0, blocking collectives: 12.1 us -> none  [the longest x1 6.83 us: local(): lax.all_to_all(combined.reshape(row_count, pair_count, half_width), 'sc',...]
    slice x0 -> x3, local copies, waits for them, and re-layouts: none -> 12.1 us  [the longest x1 10.5 us: local(): gathered[:, :row_count, :].reshape(seq_count * row_count, total_width)]
    dot_general x1, matrix products: 8.26 us -> 2.95 us  [local(): summed = jnp.dot(normed, w_full, preferred_element_type=jnp.float32)]
    convert_element_type x1 -> x0, other arithmetic: 3.51 us -> none  [local(): normed = (hidden_f * lax.rsqrt(jnp.mean(hidden_f * hidden_f, axis=1, keep...]
  transfers between devices with their start and end apart: 6 -> 4, of which waited for: 4 -> 1; matrix products, arithmetic and copies ran while one was open for 7% -> 5% of each run, Pallas kernels for 0% -> 0%
where the time goes in v2:
time: 191 us; the launch traced here: 190 us
  waiting for transfers between devices  119 us (62%)
  local copies, waits for them, and re-layouts  19 us (10%)
  Pallas kernels  17.2 us (9%)
  between operations  14.3 us (7%)
  starting transfers between devices  9.93 us (5%)
  other arithmetic  7.82 us (4%)
  matrix products  2.95 us (2%)
    all_gather x1, waiting for transfers between devices, local(): lax.all_gather(jnp.concatenate([combined, slab], axis=0), 'seq', axis=0,...  119 us
    pallas_call x1, Pallas kernels, attend(): pl.pallas_call(kernel, grid=(n_rows // block,), in_specs=[pl.BlockSpec((b...  17.2 us
    slice x1, local copies, waits for them, and re-layouts, local(): gathered[:, :row_count, :].reshape(seq_count * row_count, total_width)  10.5 us
    ppermute x3, starting transfers between devices, from_behind(): return lax.ppermute(shard, axis, pairs)  9.89 us
  transfers between devices with their start and end apart: 4, of which 1 were waited for; matrix products, arithmetic and copies ran while one was open for 5% of the time, Pallas kernels for 0%

profile of v2, /device:TPU:1, one launch (start us, length us, event | category | flops | bytes accessed | tf_op | source)
XLA Modules:
  0.0 189.9 jit_solution(3632155875819797999)
XLA Ops:
  7.2 0.0 copy-start.4
  7.2 0.0 copy-start.3
  7.2 0.0 all-gather.2.cloned.1.call-start
  7.2 0.9 fusion.18
  8.1 0.7 fusion.17
  8.9 0.9 copy.26
  9.7 1.7 fusion.10
  11.5 0.0 all-gather.2.cloned.1.call-update
  11.5 0.7 convert_element_type.41
  12.2 0.7 copy.20
  13.0 0.1 reduce-window.8
  13.0 0.1 reduce
  13.1 0.7 sub.9
  13.8 0.1 pad.20.clone
  13.9 0.2 convert_reduce_fusion
  14.1 1.0 select_reduce_fusion
  15.1 0.1 dynamic-slice_bitcast_fusion
  15.2 0.1 add_add_fusion.1
  15.3 0.1 copy.21
  15.4 3.1 %gather_fusion = s32[512]{0:T(512)S(1)} fusion(s32[8192]{0:T(1024)S(1)} %convert_reduce_fusion, s32[1024]{0:T(1024)S(1)} %pad_clamp_fusion), kind=kCustom, calls=%fused_computation | custom fusion | bytes 6144 | tf_op jit(solution)/shard_map/gather | solution.py:193
  18.6 0.1 pad.16.clone
  18.7 0.1 fusion.15
  18.8 0.0 copy-done.4
  18.8 0.5 fusion
  19.3 0.1 add_add_fusion.refs_2_
  19.4 0.9 multiply_cosine_fusion
  20.4 118.8 %all-gather.2.cloned.1.call-done = bf16[10240,1280]{1,0:T(8,128)(2,1)} async-done(((bf16[160,1280]{1,0:T(8,128)(2,1)}), bf16[10240,1280]{1,0:T(8,128)(2,1)}) %all-gather.2.cloned.1.call-update) | async-done | bytes 26214416 | tf_op jit(solution)/shard_map/all_gather | solution.py:166
  139.1 10.5 %slice.54 = bf16[64,128,1280]{2,1,0:T(8,128)(2,1)S(1)} slice(bf16[64,160,1280]{2,1,0:T(8,128)(2,1)} %bitcast.49), slice={[0:64], [0:128], [0:1280]} | slice | bytes 41943040 | tf_op jit(solution)/shard_map/slice | solution.py:168
  149.6 0.0 copy-start.2
  149.6 3.0 %convolution_add_fusion = f32[128,1280]{1,0:T(8,128)S(1)} fusion(bf16[8192,1280]{1,0:T(8,128)(2,1)S(1)} %bitcast.48, bf16[128,8192]{1,0:T(8,128)(2,1)S(1)} %copy-done, f32[8192]{0:T(1024)S(1)} %convert_element_type.41, f32[128]{0:T(128)S(1)} %add_rsqrt_fusion, f32[1280]{0:T(1024)S(1)} %maximum_convert_fusion), kind=kOutput, calls=%fused_computation.6 | convolution fusion | flops 2688712704 | bytes 23762432 | tf_op jit(solution)/shard_map/dot_general | solution.py:169
  152.6 0.1 fusion.16
  152.7 0.1 fusion.11
  152.8 0.1 fusion.13
  153.0 0.0 copy-start.1
  153.0 1.9 %collective-permute-start.2 = (bf16[128,256]{1,0:T(8,128)(2,1)S(1)}, bf16[128,256]{1,0:T(8,128)(2,1)}, u32[]{:S(2)}, u32[]{:S(2)}) collective-permute-start(bf16[128,256]{1,0:T(8,128)(2,1)S(1)} %pad_maximum_fusion.2), channel_id=1, source_target_pairs={{0,4},{4,8},{8,12},{12,16},{16,20},{20,24},{24,28},{28,32},{32,36}... | collective-permute-start | bytes 196616 | tf_op jit(solution)/shard_map/ppermute | solution.py:17
  154.9 3.3 %collective-permute-start.1 = (bf16[128,256]{1,0:T(8,128)(2,1)S(1)}, bf16[128,256]{1,0:T(8,128)(2,1)}, u32[]{:S(2)}, u32[]{:S(2)}) collective-permute-start(bf16[128,256]{1,0:T(8,128)(2,1)S(1)} %pad_maximum_fusion.2), channel_id=1, source_target_pairs={{0,8},{4,12},{8,16},{12,20},{16,24},{20,28},{24,32},{28,36},{32,40... | collective-permute-start | bytes 196616 | tf_op jit(solution)/shard_map/ppermute | solution.py:17
  158.2 4.6 %collective-permute-start = (bf16[128,256]{1,0:T(8,128)(2,1)S(1)}, bf16[128,256]{1,0:T(8,128)(2,1)}, u32[]{:S(2)}, u32[]{:S(2)}) collective-permute-start(bf16[128,256]{1,0:T(8,128)(2,1)S(1)} %pad_maximum_fusion.2), channel_id=1, source_target_pairs={{0,12},{4,16},{8,20},{12,24},{16,28},{20,32},{24,36},{28,40},{32,4... | collective-permute-start | bytes 196616 | tf_op jit(solution)/shard_map/ppermute | solution.py:17
  162.9 0.1 copy.24
  163.0 0.2 fusion.7
  163.2 0.1 reshape.167
  163.3 0.2 fusion.9.refs_0_
  163.5 0.6 slice_bitcast_fusion.4
  164.1 0.0 collective-permute-done.2
  164.1 0.0 collective-permute-done.1
  164.1 0.0 collective-permute-done
  164.1 0.9 maximum_maximum_fusion.refs_4_
  165.1 17.2 %shard_map.121 = bf16[1024,128]{1,0:T(8,128)(2,1)S(1)} custom-call(bf16[1024,128]{1,0:T(8,128)(2,1)S(1)} %fusion.9.refs_0_, s32[1024,4]{1,0:T(8,128)S(1)} %broadcast_bitcast_fusion.refs_1_, s32[8,512]{1,0:T(8,128)S(1)} %add_add_fusion.refs_2_, bf16[64,160,1280]{2,1,0:T(8,128)(2,1)} %bitcast.50, bf16[512,256]{1,0:T(8,128)(2,1)S(1)} %maximum_maximum_fusion.refs_4_), custom_call_target="tpu_custom_call" | custom-call | flops 4563402752 | bytes 6029312 | tf_op jit(solution)/shard_map/pallas_call | solution.py:96
  182.2 0.8 reshape.173
  (19 shorter events, 0.1 us)
Async XLA Ops:
  7.2 11.6 %copy-start.4 = (bf16[2,128]{1,0:T(2,128)(2,1)S(1)}, bf16[2,128]{1,0:T(2,128)(2,1)}, u32[]{:S(2)}) copy-start(bf16[2,128]{1,0:T(2,128)(2,1)} %param.15) | copy-start | bytes 1540
  7.2 11.6 %copy-start.3 = (bf16[1024]{0:T(1024)(128)(2,1)S(1)}, bf16[1024]{0:T(1024)(128)(2,1)}, u32[]{:S(2)}) copy-start(bf16[1024]{0:T(1024)(128)(2,1)} %param.13) | copy-start | bytes 6148
  7.2 11.6 %copy-start = (bf16[128,8192]{1,0:T(8,128)(2,1)S(1)}, bf16[128,8192]{1,0:T(8,128)(2,1)}, u32[]{:S(2)}) copy-start(bf16[128,8192]{1,0:T(8,128)(2,1)} %param.10) | copy-start | bytes 6291460
  7.2 131.9 %all-gather.2.cloned.1.call-start = ((), (), s32[]{:S(2)}) async-start(), calls=%async_computation | async-start | bytes 26624000 | tf_op jit(solution)/shard_map/all_gather | solution.py:166
  149.6 3.2 %copy-start.2 = (f32[128,64]{1,0:T(8,128)S(1)}, f32[128,64]{1,0:T(8,128)}, u32[]{:S(2)}) copy-start(f32[128,64]{1,0:T(8,128)} %get-tuple-element.19) | copy-start | bytes 98308
  153.0 29.3 %copy-start.1 = (bf16[128,128]{1,0:T(8,128)(2,1)}, bf16[128,128]{1,0:T(8,128)(2,1)S(1)}, u32[]{:S(2)}) copy-start(bf16[128,128]{1,0:T(8,128)(2,1)S(1)} %get-tuple-element.9) | copy-start | bytes 98308
  153.0 11.1 %collective-permute-start.2 = (bf16[128,256]{1,0:T(8,128)(2,1)S(1)}, bf16[128,256]{1,0:T(8,128)(2,1)}, u32[]{:S(2)}, u32[]{:S(2)}) collective-permute-start(bf16[128,256]{1,0:T(8,128)(2,1)S(1)} %pad_maximum_fusion.2), channel_id=1, source_target_pairs={{0,4},{4,8},{8,12},{12,16},{16,20},{20,24},{24,28},{28,32},{32,36}... | collective-permute-start | bytes 196616 | tf_op jit(solution)/shard_map/ppermute | solution.py:17
  154.9 9.2 %collective-permute-start.1 = (bf16[128,256]{1,0:T(8,128)(2,1)S(1)}, bf16[128,256]{1,0:T(8,128)(2,1)}, u32[]{:S(2)}, u32[]{:S(2)}) collective-permute-start(bf16[128,256]{1,0:T(8,128)(2,1)S(1)} %pad_maximum_fusion.2), channel_id=1, source_target_pairs={{0,8},{4,12},{8,16},{12,20},{16,24},{20,28},{24,32},{28,36},{32,40... | collective-permute-start | bytes 196616 | tf_op jit(solution)/shard_map/ppermute | solution.py:17
  158.2 5.9 %collective-permute-start = (bf16[128,256]{1,0:T(8,128)(2,1)S(1)}, bf16[128,256]{1,0:T(8,128)(2,1)}, u32[]{:S(2)}, u32[]{:S(2)}) collective-permute-start(bf16[128,256]{1,0:T(8,128)(2,1)S(1)} %pad_maximum_fusion.2), channel_id=1, source_target_pairs={{0,12},{4,16},{8,20},{12,24},{16,28},{20,32},{24,36},{28,40},{32,4... | collective-permute-start | bytes 196616 | tf_op jit(solution)/shard_map/ppermute | solution.py:17
Sparse Core Ops, SparseCore 0:
  11.6 127.4 all-gather.1

commit v3 on v2

--- a/solution.py
+++ b/solution.py
@@ -108,6 +108,35 @@
         cost_estimate=cost,
         compiler_params=pltpu.CompilerParams(vmem_limit_bytes=48 * 1024 * 1024),
     )(q_rows, row_info, col_info, gathered, near_slab)
+
+
+def projection_kernel(x_ref, w_ref, b_ref, o_ref):
+    n_dev, n_sub, width = w_ref.shape
+    w = w_ref[...].reshape(n_dev * n_sub, width)
+    o_ref[...] = jnp.dot(x_ref[...], w, preferred_element_type=jnp.float32) + b_ref[...]
+
+
+def project(x, gathered, bias, first_block, n_blocks, block_width, sub_rows):
+    n_dev = gathered.shape[0]
+    rows = x.shape[0]
+    cost = pl.CostEstimate(
+        flops=2 * rows * x.shape[1] * block_width * n_blocks,
+        transcendentals=0,
+        bytes_accessed=n_dev * sub_rows * block_width * n_blocks * 2 + x.size * 2,
+    )
+    return pl.pallas_call(
+        projection_kernel,
+        grid=(n_blocks,),
+        in_specs=[
+            pl.BlockSpec(x.shape, lambda c: (0, 0)),
+            pl.BlockSpec((n_dev, sub_rows, block_width), lambda c: (0, 0, first_block + c)),
+            pl.BlockSpec((1, block_width), lambda c: (0, c)),
+        ],
+        out_specs=pl.BlockSpec((rows, block_width), lambda c: (0, c)),
+        out_shape=jax.ShapeDtypeStruct((rows, block_width * n_blocks), jnp.float32),
+        cost_estimate=cost,
+        compiler_params=pltpu.CompilerParams(vmem_limit_bytes=48 * 1024 * 1024),
+    )(x, gathered, bias.reshape(1, -1))
 
 
 def local(
@@ -165,14 +194,10 @@
     block_rows = row_count + kv_rows
     gathered = lax.all_gather(jnp.concatenate([combined, slab], axis=0), "seq", axis=0, tiled=True)
     gathered = gathered.reshape(seq_count, block_rows, total_width)
-    w_full = gathered[:, :row_count, :].reshape(seq_count * row_count, total_width)
-    summed = jnp.dot(normed, w_full, preferred_element_type=jnp.float32)
-    bias = jnp.concatenate([q_bias, kv_bias.reshape(pair_width)]).astype(jnp.float32)
-    summed = summed + bias
-    query_own = summed[:, :query_width]
-    pairs_own = summed[:, query_width:]
-    own_queries = rotate(query_own.reshape(row_count, heads_local, head_dim), own_positions).astype(
-        jnp.bfloat16
+    block_width = math.gcd(query_width, pair_width)
+    pairs_own = project(
+        normed, gathered, kv_bias.reshape(pair_width).astype(jnp.float32),
+        query_width // block_width, pair_width // block_width, block_width, row_count,
     )
     own_keys = rotate(
         pairs_own[:, :key_width].reshape(row_count, kv_local, head_dim), own_positions
@@ -187,6 +212,12 @@
     earlier = []
     for distance in range(depth, 0, -1):
         earlier.append(from_behind(pair_rows, "seq", distance))
+    query_own = project(
+        normed, gathered, q_bias.astype(jnp.float32), 0, query_width // block_width, block_width, row_count
+    )
+    own_queries = rotate(query_own.reshape(row_count, heads_local, head_dim), own_positions).astype(
+        jnp.bfloat16
+    )
     near_rows = jnp.concatenate(earlier + [pair_rows], axis=0)
     near_count = near_rows.shape[0]
     near_index = first_row - depth * row_count + jnp.arange(near_count, dtype=jnp.int32)

time: 191 us -> 188 us (0.984)
  Pallas kernels: 17.2 us -> 27.7 us
  local copies, waits for them, and re-layouts: 19 us -> 8.84 us
  matrix products: 2.95 us -> 0 us
  waiting for transfers between devices: 119 us -> 117 us
  other arithmetic: 7.82 us -> 9.75 us
    slice x2 -> x0, local copies, waits for them, and re-layouts: 10.6 us -> none  [the longest x1 10.5 us: local(): gathered[:, :row_count, :].reshape(seq_count * row_count, total_width)]
    pallas_call x0 -> x2, Pallas kernels: none -> 10.5 us  [project(): pl.pallas_call(projection_kernel, grid=(n_blocks,), in_specs=[pl.BlockSpe...]
    dot_general x1 -> x0, matrix products: 2.95 us -> none  [local(): summed = jnp.dot(normed, w_full, preferred_element_type=jnp.float32)]
  transfers between devices with their start and end apart: 4 -> 4, of which waited for: 1 -> 1; matrix products, arithmetic and copies ran while one was open for 5% -> 6% of each run, Pallas kernels for 0% -> 4%
where the time goes in v3:
time: 188 us; the launch traced here: 187 us
  waiting for transfers between devices  117 us (62%)
  Pallas kernels  27.7 us (15%)
  between operations  14.3 us (8%)
  other arithmetic  9.75 us (5%)
  starting transfers between devices  9.48 us (5%)
  local copies, waits for them, and re-layouts  8.84 us (5%)
    all_gather x1, waiting for transfers between devices, local(): lax.all_gather(jnp.concatenate([combined, slab], axis=0), 'seq', axis=0,...  117 us
    pallas_call x1, Pallas kernels, attend(): pl.pallas_call(kernel, grid=(n_rows // block,), in_specs=[pl.BlockSpec((b...  17.2 us
    pallas_call x2, Pallas kernels, project(): pl.pallas_call(projection_kernel, grid=(n_blocks,), in_specs=[pl.BlockSpe...  10.5 us
    ppermute x3, starting transfers between devices, from_behind(): return lax.ppermute(shard, axis, pairs)  9.45 us
  transfers between devices with their start and end apart: 4, of which 1 were waited for; matrix products, arithmetic and copies ran while one was open for 6% of the time, Pallas kernels for 4%

profile of v3, /device:TPU:1, one launch (start us, length us, event | category | flops | bytes accessed | tf_op | source)
XLA Modules:
  0.0 187.0 jit_solution(13647588312432141697)
XLA Ops:
  7.2 0.0 copy-start
  7.2 0.0 all-gather.2.cloned.1.call-start
  7.2 0.9 fusion.13
  8.1 0.7 fusion.14
  8.9 0.9 copy.26
  9.7 1.7 fusion.7
  11.4 0.0 all-gather.2.cloned.1.call-update
  11.5 0.7 copy.20
  12.2 0.1 reduce-window.8
  12.3 0.1 reduce
  12.4 0.7 sub.9
  13.0 0.7 convert_element_type.48
  13.8 0.7 convert_element_type.58
  14.4 0.7 reshape.174
  15.1 0.1 pad.20.clone
  15.2 0.2 convert_reduce_fusion
  15.4 1.0 select_reduce_fusion
  16.5 0.1 dynamic-slice_bitcast_fusion
  16.5 0.1 add_add_fusion.1
  16.6 0.1 copy.21
  16.8 3.1 %gather_fusion = s32[512]{0:T(512)S(1)} fusion(s32[8192]{0:T(1024)S(1)} %convert_reduce_fusion, s32[1024]{0:T(1024)S(1)} %pad_clamp_fusion), kind=kCustom, calls=%fused_computation | custom fusion | bytes 6144 | tf_op jit(solution)/shard_map/gather | solution.py:224
  19.9 0.0 copy-start.1
  19.9 0.1 pad.16.clone
  20.0 0.1 fusion.12
  20.1 0.5 fusion
  20.6 0.1 add_add_fusion.refs_2_
  20.7 0.3 multiply_cosine_fusion
  21.0 0.5 copy-done.1
  21.5 0.6 fusion.2.x_ref
  22.1 117.0 %all-gather.2.cloned.1.call-done = bf16[10240,1280]{1,0:T(8,128)(2,1)} async-done(((bf16[160,1280]{1,0:T(8,128)(2,1)}), bf16[10240,1280]{1,0:T(8,128)(2,1)}) %all-gather.2.cloned.1.call-update) | async-done | bytes 26214416 | tf_op jit(solution)/shard_map/all_gather | solution.py:195
  139.0 3.0 %shard_map.122 = f32[128,256]{1,0:T(8,128)S(1)} custom-call(bf16[128,8192]{1,0:T(8,128)(2,1)S(1)} %fusion.2.x_ref, bf16[64,160,1280]{2,1,0:T(8,128)(2,1)} %bitcast.49, f32[1,256]{1,0:T(1,128)S(1)} %bitcast.48), custom_call_target="tpu_custom_call" | custom-call | flops 536870912 | bytes 6291456 | tf_op jit(solution)/shard_map/pallas_call | solution.py:127
  142.1 0.1 fusion.8
  142.2 0.1 fusion.10
  142.3 0.0 copy-start.2
  142.4 0.6 pad_maximum_fusion.2
  143.0 3.1 %collective-permute-start = (bf16[128,256]{1,0:T(8,128)(2,1)}, bf16[128,256]{1,0:T(8,128)(2,1)}, u32[]{:S(2)}, u32[]{:S(2)}) collective-permute-start(bf16[128,256]{1,0:T(8,128)(2,1)} %pad_maximum_fusion.2), channel_id=1, source_target_pairs={{0,12},{4,16},{8,20},{12,24},{16,28},{20,32},{24,36},{28,40},{32,4... | collective-permute-start | bytes 196616 | tf_op jit(solution)/shard_map/ppermute | solution.py:17
  146.1 4.4 %collective-permute-start.1 = (bf16[128,256]{1,0:T(8,128)(2,1)}, bf16[128,256]{1,0:T(8,128)(2,1)}, u32[]{:S(2)}, u32[]{:S(2)}) collective-permute-start(bf16[128,256]{1,0:T(8,128)(2,1)} %pad_maximum_fusion.2), channel_id=1, source_target_pairs={{0,8},{4,12},{8,16},{12,20},{16,24},{20,28},{24,32},{28,36},{32,40... | collective-permute-start | bytes 196616 | tf_op jit(solution)/shard_map/ppermute | solution.py:17
  150.5 2.0 %collective-permute-start.2 = (bf16[128,256]{1,0:T(8,128)(2,1)}, bf16[128,256]{1,0:T(8,128)(2,1)}, u32[]{:S(2)}, u32[]{:S(2)}) collective-permute-start(bf16[128,256]{1,0:T(8,128)(2,1)} %pad_maximum_fusion.2), channel_id=1, source_target_pairs={{0,4},{4,8},{8,12},{12,16},{16,20},{20,24},{24,28},{28,32},{32,36}... | collective-permute-start | bytes 196616 | tf_op jit(solution)/shard_map/ppermute | solution.py:17
  152.5 7.5 %shard_map.121 = f32[128,1024]{1,0:T(8,128)S(1)} custom-call(bf16[128,8192]{1,0:T(8,128)(2,1)S(1)} %fusion.2.x_ref, bf16[64,160,1280]{2,1,0:T(8,128)(2,1)} %bitcast.50, f32[1,1024]{1,0:T(1,128)S(1)} %bitcast.47), custom_call_target="tpu_custom_call" | custom-call | flops 2147483648 | bytes 18874368 | tf_op jit(solution)/shard_map/pallas_call | solution.py:127
  159.9 0.1 reshape.167
  160.0 0.1 copy.24
  160.1 0.2 fusion.4
  160.3 0.3 fusion.6.refs_0_
  160.6 0.6 slice_bitcast_fusion.3
  161.2 0.0 collective-permute-done
  161.2 0.9 maximum_maximum_fusion.refs_4_
  162.2 17.2 %shard_map.123 = bf16[1024,128]{1,0:T(8,128)(2,1)S(1)} custom-call(bf16[1024,128]{1,0:T(8,128)(2,1)S(1)} %fusion.6.refs_0_, s32[1024,4]{1,0:T(8,128)S(1)} %broadcast_bitcast_fusion.refs_1_, s32[8,512]{1,0:T(8,128)S(1)} %add_add_fusion.refs_2_, bf16[64,160,1280]{2,1,0:T(8,128)(2,1)} %bitcast.51, bf16[512,256]{1,0:T(8,128)(2,1)S(1)} %maximum_maximum_fusion.refs_4_), custom_call_target="tpu_custom_call" | custom-call | flops 4563402752 | bytes 6029312 | tf_op jit(solution)/shard_map/pallas_call | solution.py:96
  179.3 0.8 reshape.173
  (16 shorter events, 0.1 us)
Async XLA Ops:
  7.2 12.9 %copy-start = (bf16[128,8192]{1,0:T(8,128)(2,1)S(1)}, bf16[128,8192]{1,0:T(8,128)(2,1)}, u32[]{:S(2)}) copy-start(bf16[128,8192]{1,0:T(8,128)(2,1)} %param.10) | copy-start | bytes 6291460
  7.2 131.9 %all-gather.2.cloned.1.call-start = ((), (), s32[]{:S(2)}) async-start(), calls=%async_computation | async-start | bytes 26624000 | tf_op jit(solution)/shard_map/all_gather | solution.py:195
  19.9 1.6 copy-start.1
  142.3 18.9 %copy-start.2 = (bf16[128,128]{1,0:T(8,128)(2,1)}, bf16[128,128]{1,0:T(8,128)(2,1)S(1)}, u32[]{:S(2)}) copy-start(bf16[128,128]{1,0:T(8,128)(2,1)S(1)} %get-tuple-element.7) | copy-start | bytes 98308
  143.0 18.2 %collective-permute-start = (bf16[128,256]{1,0:T(8,128)(2,1)}, bf16[128,256]{1,0:T(8,128)(2,1)}, u32[]{:S(2)}, u32[]{:S(2)}) collective-permute-start(bf16[128,256]{1,0:T(8,128)(2,1)} %pad_maximum_fusion.2), channel_id=1, source_target_pairs={{0,12},{4,16},{8,20},{12,24},{16,28},{20,32},{24,36},{28,40},{32,4... | collective-permute-start | bytes 196616 | tf_op jit(solution)/shard_map/ppermute | solution.py:17
  146.1 15.2 %collective-permute-start.1 = (bf16[128,256]{1,0:T(8,128)(2,1)}, bf16[128,256]{1,0:T(8,128)(2,1)}, u32[]{:S(2)}, u32[]{:S(2)}) collective-permute-start(bf16[128,256]{1,0:T(8,128)(2,1)} %pad_maximum_fusion.2), channel_id=1, source_target_pairs={{0,8},{4,12},{8,16},{12,20},{16,24},{20,28},{24,32},{28,36},{32,40... | collective-permute-start | bytes 196616 | tf_op jit(solution)/shard_map/ppermute | solution.py:17
  150.5 10.8 %collective-permute-start.2 = (bf16[128,256]{1,0:T(8,128)(2,1)}, bf16[128,256]{1,0:T(8,128)(2,1)}, u32[]{:S(2)}, u32[]{:S(2)}) collective-permute-start(bf16[128,256]{1,0:T(8,128)(2,1)} %pad_maximum_fusion.2), channel_id=1, source_target_pairs={{0,4},{4,8},{8,12},{12,16},{16,20},{20,24},{24,28},{28,32},{32,36}... | collective-permute-start | bytes 196616 | tf_op jit(solution)/shard_map/ppermute | solution.py:17
Sparse Core Ops, SparseCore 0:
  11.6 127.4 all-gather.1

commit v4 on v3

--- a/solution.py
+++ b/solution.py
@@ -40,74 +40,112 @@
     return values * cosine + turned * sine_part
 
 
-def attention_kernel(q_ref, row_ref, col_ref, kv_ref, near_ref, o_ref, *, head_dim, packs, scale):
+def attention_kernel(flag_ref, q_ref, row_ref, col_ref, kv_ref, near_ref, o_ref, *, head_dim, packs, scale):
     d = head_dim
     dims = (((1,), (1,)), ((), ()))
-    q = q_ref[...]
-    rows = row_ref[...]
-    use_first = rows[:, 0:1] == 0
-    row_seg = rows[:, 1:2]
-    row_idx = rows[:, 2:3]
-    cols = col_ref[...]
+    block = pl.program_id(0)
+    uses = (flag_ref[block, 0] > 0, flag_ref[block, 1] > 0)
     n_dev, n_sub = kv_ref.shape[0], kv_ref.shape[1]
 
     def piece(j):
         return kv_ref[:, :, j * d : (j + 1) * d].reshape(n_dev * n_sub, d)
 
-    far = []
-    for k in range(packs):
-        far0 = lax.dot_general(q, piece(4 * k), dims, preferred_element_type=jnp.float32) * scale
-        far1 = lax.dot_general(q, piece(4 * k + 1), dims, preferred_element_type=jnp.float32) * scale
-        far.append(jnp.where(use_first, far0, far1))
-    near = lax.dot_general(q, near_ref[:, 0:d], dims, preferred_element_type=jnp.float32) * scale
-    visible = (cols[0:1, :] == row_seg) & (cols[1:2, :] <= row_idx)
-    near = jnp.where(visible, near, -jnp.inf)
-    top = jnp.max(near, axis=1, keepdims=True)
-    for s in far:
-        top = jnp.maximum(top, jnp.max(s, axis=1, keepdims=True))
-    near_w = jnp.exp(near - top)
-    mass = jnp.sum(near_w, axis=1, keepdims=True)
-    acc = jnp.dot(near_w.astype(jnp.bfloat16), near_ref[:, d : 2 * d], preferred_element_type=jnp.float32)
-    for k, s in enumerate(far):
-        far_w = jnp.exp(s - top)
-        mass = mass + jnp.sum(far_w, axis=1, keepdims=True)
-        far_b = far_w.astype(jnp.bfloat16)
-        zero = jnp.zeros_like(far_b)
-        acc = acc + jnp.dot(jnp.where(use_first, far_b, zero), piece(4 * k + 2), preferred_element_type=jnp.float32)
-        acc = acc + jnp.dot(jnp.where(use_first, zero, far_b), piece(4 * k + 3), preferred_element_type=jnp.float32)
-    o_ref[...] = (acc / mass).astype(o_ref.dtype)
+    def near_part(q):
+        rows = row_ref[...]
+        cols = col_ref[...]
+        near = lax.dot_general(q, near_ref[:, 0:d], dims, preferred_element_type=jnp.float32) * scale
+        visible = (cols[0:1, :] == rows[:, 1:2]) & (cols[1:2, :] <= rows[:, 2:3])
+        return jnp.where(visible, near, -jnp.inf)
+
+    def finish(q, far, values):
+        near = near_part(q)
+        top = jnp.max(near, axis=1, keepdims=True)
+        for s in far:
+            top = jnp.maximum(top, jnp.max(s, axis=1, keepdims=True))
+        near_w = jnp.exp(near - top)
+        mass = jnp.sum(near_w, axis=1, keepdims=True)
+        acc = jnp.dot(near_w.astype(jnp.bfloat16), near_ref[:, d : 2 * d], preferred_element_type=jnp.float32)
+        for s, value in zip(far, values):
+            far_w = jnp.exp(s - top)
+            mass = mass + jnp.sum(far_w, axis=1, keepdims=True)
+            acc = value(far_w.astype(jnp.bfloat16), acc)
+        o_ref[...] = (acc / mass).astype(o_ref.dtype)
+
+    def single(p):
+        q = q_ref[...]
+        far = [
+            lax.dot_general(q, piece(4 * k + p), dims, preferred_element_type=jnp.float32) * scale
+            for k in range(packs)
+        ]
+
+        def value_of(k):
+            return lambda w, acc: acc + jnp.dot(w, piece(4 * k + 2 + p), preferred_element_type=jnp.float32)
+
+        finish(q, far, [value_of(k) for k in range(packs)])
+
+    def both():
+        q = q_ref[...]
+        use_first = row_ref[...][:, 0:1] == 0
+        far = []
+        for k in range(packs):
+            far0 = lax.dot_general(q, piece(4 * k), dims, preferred_element_type=jnp.float32) * scale
+            far1 = lax.dot_general(q, piece(4 * k + 1), dims, preferred_element_type=jnp.float32) * scale
+            far.append(jnp.where(use_first, far0, far1))
+
+        def value_of(k):
+            def value(w, acc):
+                zero = jnp.zeros_like(w)
+                acc = acc + jnp.dot(jnp.where(use_first, w, zero), piece(4 * k + 2), preferred_element_type=jnp.float32)
+                return acc + jnp.dot(jnp.where(use_first, zero, w), piece(4 * k + 3), preferred_element_type=jnp.float32)
+
+            return value
+
+        finish(q, far, [value_of(k) for k in range(packs)])
+
+    pl.when(uses[0] & uses[1])(both)
+    pl.when(uses[0] & jnp.logical_not(uses[1]))(lambda: single(0))
+    pl.when(jnp.logical_not(uses[0]) & uses[1])(lambda: single(1))
 
 
 def attend(q_rows, row_info, col_info, gathered, kv_block, kv_rows, near_slab, head_dim):
     n_rows = q_rows.shape[0]
     block = math.gcd(n_rows, 256)
+    n_blocks = n_rows // block
     n_dev = gathered.shape[0]
     width = gathered.shape[2]
     packs = width // (4 * head_dim)
     cache_len = n_dev * kv_rows * packs
     near_len = near_slab.shape[0]
+    block_prefix = row_info[:, 0].reshape(n_blocks, block)
+    flags = jnp.stack(
+        [jnp.any(block_prefix == 0, axis=1), jnp.any(block_prefix != 0, axis=1)], axis=1
+    ).astype(jnp.int32)
     kernel = lambda *refs: attention_kernel(*refs, head_dim=head_dim, packs=packs, scale=head_dim ** (-0.5))
-    keys_total = 2 * cache_len + near_len
+    keys_total = cache_len + near_len
     cost = pl.CostEstimate(
         flops=4 * n_rows * keys_total * head_dim,
         transcendentals=n_rows * (cache_len + near_len),
         bytes_accessed=n_dev * kv_rows * width * 2 + near_slab.size * 2 + q_rows.size * 4,
     )
+    grid_spec = pltpu.PrefetchScalarGridSpec(
+        num_scalar_prefetch=1,
+        grid=(n_blocks,),
+        in_specs=[
+            pl.BlockSpec((block, head_dim), lambda i, f: (i, 0)),
+            pl.BlockSpec((block, row_info.shape[1]), lambda i, f: (i, 0)),
+            pl.BlockSpec(col_info.shape, lambda i, f: (0, 0)),
+            pl.BlockSpec((n_dev, kv_rows, width), lambda i, f: (0, kv_block, 0)),
+            pl.BlockSpec(near_slab.shape, lambda i, f: (0, 0)),
+        ],
+        out_specs=pl.BlockSpec((block, head_dim), lambda i, f: (i, 0)),
+    )
     return pl.pallas_call(
         kernel,
-        grid=(n_rows // block,),
-        in_specs=[
-            pl.BlockSpec((block, head_dim), lambda i: (i, 0)),
-            pl.BlockSpec((block, row_info.shape[1]), lambda i: (i, 0)),
-            pl.BlockSpec(col_info.shape, lambda i: (0, 0)),
-            pl.BlockSpec((n_dev, kv_rows, width), lambda i: (0, kv_block, 0)),
-            pl.BlockSpec(near_slab.shape, lambda i: (0, 0)),
-        ],
-        out_specs=pl.BlockSpec((block, head_dim), lambda i: (i, 0)),
+        grid_spec=grid_spec,
         out_shape=jax.ShapeDtypeStruct((n_rows, head_dim), jnp.bfloat16),
         cost_estimate=cost,
         compiler_params=pltpu.CompilerParams(vmem_limit_bytes=48 * 1024 * 1024),
-    )(q_rows, row_info, col_info, gathered, near_slab)
+    )(flags, q_rows, row_info, col_info, gathered, near_slab)
 
 
 def projection_kernel(x_ref, w_ref, b_ref, o_ref):

time: 188 us -> 184 us (0.979)
  Pallas kernels: 27.7 us -> 24.8 us
  other arithmetic: 9.75 us -> 12 us
  waiting for transfers between devices: 117 us -> 115 us
    pallas_call x1, Pallas kernels: 17.2 us -> 14.2 us  [attend(): pl.pallas_call(kernel, grid_spec=grid_spec, out_shape=jax.ShapeDtypeStruc...]
    all_gather x1, waiting for transfers between devices: 117 us -> 115 us  [local(): lax.all_gather(jnp.concatenate([combined, slab], axis=0), 'seq', axis=0,...]
  transfers between devices with their start and end apart: 4 -> 4, of which waited for: 1 -> 1; matrix products, arithmetic and copies ran while one was open for 6% -> 7% of each run, Pallas kernels for 4% -> 4%
where the time goes in v4:
time: 184 us
  waiting for transfers between devices  115 us (62%)
  Pallas kernels  24.8 us (13%)
  between operations  14.3 us (8%)
  other arithmetic  12 us (7%)
  starting transfers between devices  9.66 us (5%)
  local copies, waits for them, and re-layouts  8.63 us (5%)
    all_gather x1, waiting for transfers between devices, local(): lax.all_gather(jnp.concatenate([combined, slab], axis=0), 'seq', axis=0,...  115 us
    pallas_call x1, Pallas kernels, attend(): pl.pallas_call(kernel, grid_spec=grid_spec, out_shape=jax.ShapeDtypeStruc...  14.2 us
    pallas_call x2, Pallas kernels, project(): pl.pallas_call(projection_kernel, grid=(n_blocks,), in_specs=[pl.BlockSpe...  10.6 us
    ppermute x3, starting transfers between devices, from_behind(): return lax.ppermute(shard, axis, pairs)  9.63 us
  transfers between devices with their start and end apart: 4, of which 1 were waited for; matrix products, arithmetic and copies ran while one was open for 7% of the time, Pallas kernels for 4%

profile of v4, /device:TPU:1, one launch (start us, length us, event | category | flops | bytes accessed | tf_op | source)
XLA Modules:
  0.0 184.3 jit_solution(6143029896529120555)
XLA Ops:
  7.2 0.0 all-gather.2.cloned.1.call-start
  7.2 0.9 fusion.13
  8.1 0.7 fusion.14
  8.9 0.9 copy.32
  9.7 1.7 fusion.7
  11.5 0.7 copy.23
  12.2 0.1 reduce-window.8
  12.3 0.1 reduce
  12.4 0.7 sub.9
  13.1 0.7 convert_element_type.53
  13.8 0.7 convert_element_type.62
  14.4 0.7 reshape.178
  15.1 0.1 pad.35.clone
  15.2 0.2 convert_reduce_fusion
  15.4 1.0 select_reduce_fusion
  16.5 0.1 dynamic-slice_bitcast_fusion
  16.6 0.1 add_add_fusion.1
  16.6 0.1 copy.24
  16.8 0.3 compare_reduce_fusion.1
  17.1 0.1 reduce_or.18
  17.3 0.1 copy.25
  17.4 0.1 reduce_or.19
  17.5 0.1 copy.26
  17.7 3.1 %gather_fusion = s32[512]{0:T(512)S(1)} fusion(s32[8192]{0:T(1024)S(1)} %convert_reduce_fusion, s32[1024]{0:T(1024)S(1)} %pad_clamp_fusion), kind=kCustom, calls=%fused_computation | custom fusion | bytes 6144 | tf_op jit(solution)/shard_map/gather | solution.py:262
  20.8 0.1 pad.16.clone
  20.9 0.1 fusion.12
  21.0 0.1 add_convert_fusion.refs_0_
  21.1 0.5 fusion
  21.6 0.1 add_add_fusion.refs_3_
  21.7 0.3 multiply_cosine_fusion
  22.0 2.2 %fusion.2.x_ref = bf16[128,8192]{1,0:T(8,128)(2,1)S(1)} fusion(bf16[128,8192]{1,0:T(8,128)(2,1)} %param.10, f32[8192]{0:T(1024)S(1)} %convert_element_type.53, f32[128]{0:T(128)S(1)} %add_rsqrt_fusion), kind=kLoop, calls=%fused_computation.5 | loop fusion | flops 4194304 | bytes 4227584 | tf_op jit(solution)/shard_map/convert_element_type | solution.py:210
  24.1 114.9 %all-gather.2.cloned.1.call-done = bf16[10240,1280]{1,0:T(8,128)(2,1)} async-done(((bf16[160,1280]{1,0:T(8,128)(2,1)}), bf16[10240,1280]{1,0:T(8,128)(2,1)}) %all-gather.2.cloned.1.call-update) | async-done | bytes 26214416 | tf_op jit(solution)/shard_map/all_gather | solution.py:233
  139.1 3.0 %shard_map.122 = f32[128,256]{1,0:T(8,128)S(1)} custom-call(bf16[128,8192]{1,0:T(8,128)(2,1)S(1)} %fusion.2.x_ref, bf16[64,160,1280]{2,1,0:T(8,128)(2,1)} %bitcast.51, f32[1,256]{1,0:T(1,128)S(1)} %bitcast.50), custom_call_target="tpu_custom_call" | custom-call | flops 536870912 | bytes 6291456 | tf_op jit(solution)/shard_map/pallas_call | solution.py:165
  142.1 0.1 fusion.8
  142.2 0.1 fusion.10
  142.3 0.6 pad_maximum_fusion.2
  142.9 3.0 %collective-permute-start = (bf16[128,256]{1,0:T(8,128)(2,1)}, bf16[128,256]{1,0:T(8,128)(2,1)}, u32[]{:S(2)}, u32[]{:S(2)}) collective-permute-start(bf16[128,256]{1,0:T(8,128)(2,1)} %pad_maximum_fusion.2), channel_id=1, source_target_pairs={{0,12},{4,16},{8,20},{12,24},{16,28},{20,32},{24,36},{28,40},{32,4... | collective-permute-start | bytes 196616 | tf_op jit(solution)/shard_map/ppermute | solution.py:17
  146.0 4.4 %collective-permute-start.1 = (bf16[128,256]{1,0:T(8,128)(2,1)}, bf16[128,256]{1,0:T(8,128)(2,1)}, u32[]{:S(2)}, u32[]{:S(2)}) collective-permute-start(bf16[128,256]{1,0:T(8,128)(2,1)} %pad_maximum_fusion.2), channel_id=1, source_target_pairs={{0,8},{4,12},{8,16},{12,20},{16,24},{20,28},{24,32},{28,36},{32,40... | collective-permute-start | bytes 196616 | tf_op jit(solution)/shard_map/ppermute | solution.py:17
  150.4 2.2 %collective-permute-start.2 = (bf16[128,256]{1,0:T(8,128)(2,1)}, bf16[128,256]{1,0:T(8,128)(2,1)}, u32[]{:S(2)}, u32[]{:S(2)}) collective-permute-start(bf16[128,256]{1,0:T(8,128)(2,1)} %pad_maximum_fusion.2), channel_id=1, source_target_pairs={{0,4},{4,8},{8,12},{12,16},{16,20},{20,24},{24,28},{28,32},{32,36}... | collective-permute-start | bytes 196616 | tf_op jit(solution)/shard_map/ppermute | solution.py:17
  152.6 7.6 %shard_map.121 = f32[128,1024]{1,0:T(8,128)S(1)} custom-call(bf16[128,8192]{1,0:T(8,128)(2,1)S(1)} %fusion.2.x_ref, bf16[64,160,1280]{2,1,0:T(8,128)(2,1)} %bitcast.52, f32[1,1024]{1,0:T(1,128)S(1)} %bitcast.49), custom_call_target="tpu_custom_call" | custom-call | flops 2147483648 | bytes 18874368 | tf_op jit(solution)/shard_map/pallas_call | solution.py:165
  160.2 0.1 reshape.174
  160.3 0.1 copy.30
  160.4 0.2 fusion.4
  160.6 0.2 fusion.6.refs_1_
  160.8 0.6 slice_bitcast_fusion.3
  161.5 0.9 maximum_maximum_fusion.refs_5_
  162.4 14.2 %shard_map.123 = bf16[1024,128]{1,0:T(8,128)(2,1)S(1)} custom-call(s32[4,2]{1,0:T(4,128)S(1)} %add_convert_fusion.refs_0_, bf16[1024,128]{1,0:T(8,128)(2,1)S(1)} %fusion.6.refs_1_, s32[1024,4]{1,0:T(8,128)S(1)} %broadcast_bitcast_fusion.refs_2_, s32[8,512]{1,0:T(8,128)S(1)} %add_add_fusion.refs_3_, bf16[64,160,1280]{2,1,0:T(8,128)(2,1)} %bitcast.53, ...), custom_call_target="tpu_custom_call" | custom-call | flops 2415919104 | bytes 6029312 | tf_op jit(solution)/shard_map/pallas_call | solution.py:142
  176.6 0.8 reshape.177
  (22 shorter events, 0.2 us)
Async XLA Ops:
  7.2 13.9 %copy-start = (bf16[128,8192]{1,0:T(8,128)(2,1)S(1)}, bf16[128,8192]{1,0:T(8,128)(2,1)}, u32[]{:S(2)}) copy-start(bf16[128,8192]{1,0:T(8,128)(2,1)} %param.10) | copy-start | bytes 6291460
  7.2 131.9 %all-gather.2.cloned.1.call-start = ((), (), s32[]{:S(2)}) async-start(), calls=%async_computation | async-start | bytes 26624000 | tf_op jit(solution)/shard_map/all_gather | solution.py:233
  142.3 19.2 %copy-start.1 = (bf16[128,128]{1,0:T(8,128)(2,1)}, bf16[128,128]{1,0:T(8,128)(2,1)S(1)}, u32[]{:S(2)}) copy-start(bf16[128,128]{1,0:T(8,128)(2,1)S(1)} %get-tuple-element.9) | copy-start | bytes 98308
  142.9 18.5 %collective-permute-start = (bf16[128,256]{1,0:T(8,128)(2,1)}, bf16[128,256]{1,0:T(8,128)(2,1)}, u32[]{:S(2)}, u32[]{:S(2)}) collective-permute-start(bf16[128,256]{1,0:T(8,128)(2,1)} %pad_maximum_fusion.2), channel_id=1, source_target_pairs={{0,12},{4,16},{8,20},{12,24},{16,28},{20,32},{24,36},{28,40},{32,4... | collective-permute-start | bytes 196616 | tf_op jit(solution)/shard_map/ppermute | solution.py:17
  146.0 15.5 %collective-permute-start.1 = (bf16[128,256]{1,0:T(8,128)(2,1)}, bf16[128,256]{1,0:T(8,128)(2,1)}, u32[]{:S(2)}, u32[]{:S(2)}) collective-permute-start(bf16[128,256]{1,0:T(8,128)(2,1)} %pad_maximum_fusion.2), channel_id=1, source_target_pairs={{0,8},{4,12},{8,16},{12,20},{16,24},{20,28},{24,32},{28,36},{32,40... | collective-permute-start | bytes 196616 | tf_op jit(solution)/shard_map/ppermute | solution.py:17
  150.4 11.1 %collective-permute-start.2 = (bf16[128,256]{1,0:T(8,128)(2,1)}, bf16[128,256]{1,0:T(8,128)(2,1)}, u32[]{:S(2)}, u32[]{:S(2)}) collective-permute-start(bf16[128,256]{1,0:T(8,128)(2,1)} %pad_maximum_fusion.2), channel_id=1, source_target_pairs={{0,4},{4,8},{8,12},{12,16},{16,20},{20,24},{24,28},{28,32},{32,36}... | collective-permute-start | bytes 196616 | tf_op jit(solution)/shard_map/ppermute | solution.py:17
Sparse Core Ops, SparseCore 0:
  11.6 127.3 all-gather.1

commit v5 on v4

v5 whole, which is shorter than its diff:
```python
import math

import jax
import jax.numpy as jnp
from jax import lax
from jax.experimental import pallas as pl
from jax.experimental.pallas import tpu as pltpu
from jax.sharding import PartitionSpec as P

EPS = 1e-06
THETA = 1000000.0


def from_behind(shard, axis, by):
    size = lax.axis_size(axis)
    pairs = [(i, i + by) for i in range(size) if 0 <= i + by < size]
    return lax.ppermute(shard, axis, pairs)


def row_tables(lengths, assignment, all_rows):
    request_end = jnp.cumsum(lengths)
    request_start = request_end - lengths
    row_ids = jnp.arange(all_rows, dtype=jnp.int32)
    segment = jnp.sum((row_ids[:, None] >= request_end[None, :]).astype(jnp.int32), axis=1)
    request_ids = jnp.arange(lengths.shape[0], dtype=jnp.int32)
    onehot = (segment[:, None] == request_ids[None, :]).astype(jnp.int32)
    offset = row_ids - jnp.sum(onehot * request_start[None, :], axis=1)
    prefix = jnp.sum(onehot * assignment[None, :], axis=1)
    return (segment, offset, prefix)


def rotate(values, positions):
    head_size = values.shape[-1]
    half_dim = head_size // 2
    frequency = THETA ** (-2.0 * jnp.arange(half_dim, dtype=jnp.float32) / head_size)
    angles = positions.astype(jnp.float32)[:, None] * frequency[None, :]
    cosine = jnp.concatenate([jnp.cos(angles), jnp.cos(angles)], axis=-1)[:, None, :]
    sine_part = jnp.concatenate([jnp.sin(angles), jnp.sin(angles)], axis=-1)[:, None, :]
    turned = jnp.concatenate([-values[..., half_dim:], values[..., :half_dim]], axis=-1)
    return values * cosine + turned * sine_part


def attention_kernel(flag_ref, q_ref, row_ref, col_ref, k0_ref, k1_ref, v0_ref, v1_ref, near_ref, o_ref, *, scale):
    d = q_ref.shape[1]
    dims = (((1,), (1,)), ((), ()))
    block = pl.program_id(0)
    uses = (flag_ref[block, 0] > 0, flag_ref[block, 1] > 0)
    key_refs = (k0_ref, k1_ref)
    value_refs = (v0_ref, v1_ref)

    def full(ref):
        return ref[...].reshape(ref.shape[0] * ref.shape[1], ref.shape[2])

    def finish(q, far, value):
        rows = row_ref[...]
        cols = col_ref[...]
        near = lax.dot_general(q, near_ref[:, 0:d], dims, preferred_element_type=jnp.float32) * scale
        visible = (cols[0:1, :] == rows[:, 1:2]) & (cols[1:2, :] <= rows[:, 2:3])
        near = jnp.where(visible, near, -jnp.inf)
        top = jnp.maximum(jnp.max(near, axis=1, keepdims=True), jnp.max(far, axis=1, keepdims=True))
        near_w = jnp.exp(near - top)
        far_w = jnp.exp(far - top)
        mass = jnp.sum(near_w, axis=1, keepdims=True) + jnp.sum(far_w, axis=1, keepdims=True)
        acc = jnp.dot(near_w.astype(jnp.bfloat16), near_ref[:, d : 2 * d], preferred_element_type=jnp.float32)
        acc = value(far_w.astype(jnp.bfloat16), acc)
        o_ref[...] = (acc / mass).astype(o_ref.dtype)

    def single(p):
        q = q_ref[...]
        far = lax.dot_general(q, full(key_refs[p]), dims, preferred_element_type=jnp.float32) * scale
        finish(q, far, lambda w, acc: acc + jnp.dot(w, full(value_refs[p]), preferred_element_type=jnp.float32))

    def both():
        q = q_ref[...]
        use_first = row_ref[...][:, 0:1] == 0
        far0 = lax.dot_general(q, full(k0_ref), dims, preferred_element_type=jnp.float32) * scale
        far1 = lax.dot_general(q, full(k1_ref), dims, preferred_element_type=jnp.float32) * scale

        def value(w, acc):
            zero = jnp.zeros_like(w)
            acc = acc + jnp.dot(jnp.where(use_first, w, zero), full(v0_ref), preferred_element_type=jnp.float32)
            return acc + jnp.dot(jnp.where(use_first, zero, w), full(v1_ref), preferred_element_type=jnp.float32)

        finish(q, jnp.where(use_first, far0, far1), value)

    pl.when(uses[0] & uses[1])(both)
    pl.when(uses[0] & jnp.logical_not(uses[1]))(lambda: single(0))
    pl.when(jnp.logical_not(uses[0]) & uses[1])(lambda: single(1))


def attend(q_rows, row_info, col_info, cache, kv_column, near_slab):
    n_rows, head_dim = q_rows.shape
    block = math.gcd(n_rows, 256)
    n_blocks = n_rows // block
    n_dev, _, cache_local, _ = cache.shape
    cache_len = n_dev * cache_local
    near_len = near_slab.shape[0]
    block_prefix = row_info[:, 0].reshape(n_blocks, block)
    flags = jnp.stack(
        [jnp.any(block_prefix == 0, axis=1), jnp.any(block_prefix != 0, axis=1)], axis=1
    ).astype(jnp.int32)
    kernel = lambda *refs: attention_kernel(*refs, scale=head_dim ** (-0.5))
    cost = pl.CostEstimate(
        flops=4 * n_rows * (cache_len + near_len) * head_dim,
        transcendentals=n_rows * (cache_len + near_len),
        bytes_accessed=4 * cache_len * head_dim * 2 + near_slab.size * 2 + q_rows.size * 4,
    )

    def cache_spec(kind, p):
        return pl.BlockSpec((n_dev, None, cache_local, head_dim), lambda i, f: (0, kind, 0, kv_column + p))

    grid_spec = pltpu.PrefetchScalarGridSpec(
        num_scalar_prefetch=1,
        grid=(n_blocks,),
        in_specs=[
            pl.BlockSpec((block, head_dim), lambda i, f: (i, 0)),
            pl.BlockSpec((block, row_info.shape[1]), lambda i, f: (i, 0)),
            pl.BlockSpec(col_info.shape, lambda i, f: (0, 0)),
            cache_spec(0, 0),
            cache_spec(0, 1),
            cache_spec(1, 0),
            cache_spec(1, 1),
            pl.BlockSpec(near_slab.shape, lambda i, f: (0, 0)),
        ],
        out_specs=pl.BlockSpec((block, head_dim), lambda i, f: (i, 0)),
    )
    return pl.pallas_call(
        kernel,
        grid_spec=grid_spec,
        out_shape=jax.ShapeDtypeStruct((n_rows, head_dim), jnp.bfloat16),
        cost_estimate=cost,
        compiler_params=pltpu.CompilerParams(vmem_limit_bytes=48 * 1024 * 1024),
    )(flags, q_rows, row_info, col_info, cache, cache, cache, cache, near_slab)


def projection_kernel(x_ref, w_ref, b_ref, o_ref):
    o_ref[...] = jnp.dot(x_ref[...], w_ref[...], preferred_element_type=jnp.float32) + b_ref[...]


def project(x, gathered, bias, first_block, n_blocks, block_width):
    rows = x.shape[0]
    depth = gathered.shape[0]
    cost = pl.CostEstimate(
        flops=2 * rows * depth * block_width * n_blocks,
        transcendentals=0,
        bytes_accessed=depth * block_width * n_blocks * 2 + x.size * 2,
    )
    return pl.pallas_call(
        projection_kernel,
        grid=(n_blocks,),
        in_specs=[
            pl.BlockSpec(x.shape, lambda c: (0, 0)),
            pl.BlockSpec((depth, block_width), lambda c: (0, first_block + c)),
            pl.BlockSpec((1, block_width), lambda c: (0, c)),
        ],
        out_specs=pl.BlockSpec((rows, block_width), lambda c: (0, c)),
        out_shape=jax.ShapeDtypeStruct((rows, block_width * n_blocks), jnp.float32),
        cost_estimate=cost,
        compiler_params=pltpu.CompilerParams(vmem_limit_bytes=48 * 1024 * 1024),
    )(x, gathered, bias.reshape(1, -1))


def local(
    hidden,
    gain,
    w_query,
    q_bias,
    w_keyval,
    kv_bias,
    prefix_keys,
    prefix_values,
    lengths,
    assignment,
):
    row_count = hidden.shape[0]
    seq_count = lax.axis_size("seq")
    seq_index = lax.axis_index("seq")
    all_rows = row_count * seq_count
    head_dim = prefix_keys.shape[3]
    kv_local = prefix_keys.shape[2]
    query_width = w_query.shape[1]
    heads_local = query_width // head_dim
    pair_width = w_keyval.shape[1] * w_keyval.shape[2]
    key_width = pair_width // 2
    cache_local = prefix_keys.shape[1]
    cache_length = cache_local * seq_count
    first_row = seq_index * row_count
    hidden_f = hidden.astype(jnp.float32)
    normed = (
        hidden_f
        * lax.rsqrt(jnp.mean(hidden_f * hidden_f, axis=1, keepdims=True) + EPS)
        * gain.astype(jnp.float32)
    ).astype(jnp.bfloat16)
    segment, offset, prefix = row_tables(lengths, assignment, all_rows)
    positions = offset + cache_length
    own_positions = lax.dynamic_slice_in_dim(positions, first_row, row_count)
    own_segment = lax.dynamic_slice_in_dim(segment, first_row, row_count)
    own_prefix = lax.dynamic_slice_in_dim(prefix, first_row, row_count)

    w_pairs = w_keyval.reshape(w_keyval.shape[0], pair_width)
    block_width = math.gcd(query_width, pair_width)
    cache_width = 2 * head_dim
    assert 2 * cache_local == row_count and cache_width % block_width == 0
    cache_keys = jnp.concatenate([prefix_keys[0, :, 0, :], prefix_keys[1, :, 0, :]], axis=1)
    cache_values = jnp.concatenate([prefix_values[0, :, 0, :], prefix_values[1, :, 0, :]], axis=1)
    combined = jnp.concatenate(
        [w_query, w_pairs, jnp.concatenate([cache_keys, cache_values], axis=0)], axis=1
    )
    total_width = combined.shape[1]
    gathered = lax.all_gather(combined, "seq", axis=0, tiled=True)
    pairs_own = project(
        normed, gathered, kv_bias.reshape(pair_width).astype(jnp.float32),
        query_width // block_width, pair_width // block_width, block_width,
    )
    own_keys = rotate(
        pairs_own[:, :key_width].reshape(row_count, kv_local, head_dim), own_positions
    ).astype(jnp.bfloat16)
    own_values = (
        pairs_own[:, key_width:].reshape(row_count, kv_local, head_dim).astype(jnp.bfloat16)
    )
    pair_rows = jnp.concatenate(
        [own_keys.reshape(row_count, key_width), own_values.reshape(row_count, key_width)], axis=1
    )
    depth = min(3, seq_count - 1)
    earlier = []
    for distance in range(depth, 0, -1):
        earlier.append(from_behind(pair_rows, "seq", distance))
    query_own = project(normed, gathered, q_bias.astype(jnp.float32), 0, query_width // block_width, block_width)
    own_queries = rotate(query_own.reshape(row_count, heads_local, head_dim), own_positions).astype(
        jnp.bfloat16
    )
    near_rows = jnp.concatenate(earlier + [pair_rows], axis=0)
    near_count = near_rows.shape[0]
    near_index = first_row - depth * row_count + jnp.arange(near_count, dtype=jnp.int32)
    near_segment = segment[jnp.clip(near_index, 0, all_rows - 1)]
    near_segment = jnp.where(near_index >= 0, near_segment, -1)
    col_info = jnp.concatenate(
        [near_segment[None, :], near_index[None, :], jnp.zeros((6, near_count), jnp.int32)], axis=0
    )
    own_rows = first_row + jnp.arange(row_count, dtype=jnp.int32)
    row_info = jnp.stack(
        [own_prefix, own_segment, own_rows, jnp.zeros_like(own_rows)], axis=1
    ).astype(jnp.int32)
    row_info = jnp.repeat(row_info, heads_local, axis=0)
    cache = gathered.reshape(seq_count, 2, cache_local, total_width)
    out_rows = attend(
        own_queries.reshape(row_count * heads_local, head_dim),
        row_info,
        col_info,
        cache,
        (query_width + pair_width) // head_dim,
        near_rows,
    )
    attention = out_rows.reshape(row_count, query_width)
    return (attention, own_keys, own_values)


def solution(mesh):
    in_specs = (
        P("seq", None),
        P(),
        P("seq", "tensor"),
        P("tensor"),
        P("seq", None, "tensor"),
        P(None, "tensor"),
        P(None, "seq", "tensor", None),
        P(None, "seq", "tensor", None),
        P(),
        P(),
    )
    out_specs = (P("seq", "tensor"), P("seq", "tensor", None), P("seq", "tensor", None))
    return jax.shard_map(local, mesh=mesh, in_specs=in_specs, out_specs=out_specs, check_vma=False)
```

time: 184 us -> 180 us (0.978)
  waiting for transfers between devices: 115 us -> 112 us
    all_gather x1, waiting for transfers between devices: 115 us -> 112 us  [local(): gathered = lax.all_gather(combined, 'seq', axis=0, tiled=True)]
  transfers between devices with their start and end apart: 4 -> 4, of which waited for: 1 -> 1; matrix products, arithmetic and copies ran while one was open for 7% -> 8% of each run, Pallas kernels for 4% -> 4%
where the time goes in v5:
time: 180 us
  waiting for transfers between devices  112 us (62%)
  Pallas kernels  23.7 us (13%)
  between operations  14.2 us (8%)
  other arithmetic  12 us (7%)
  starting transfers between devices  9.68 us (5%)
  local copies, waits for them, and re-layouts  7.92 us (4%)
    all_gather x1, waiting for transfers between devices, local(): gathered = lax.all_gather(combined, 'seq', axis=0, tiled=True)  112 us
    pallas_call x1, Pallas kernels, attend(): pl.pallas_call(kernel, grid_spec=grid_spec, out_shape=jax.ShapeDtypeStruc...  13.2 us
    pallas_call x2, Pallas kernels, project(): pl.pallas_call(projection_kernel, grid=(n_blocks,), in_specs=[pl.BlockSpe...  10.4 us
    ppermute x3, starting transfers between devices, from_behind(): return lax.ppermute(shard, axis, pairs)  9.64 us
  transfers between devices with their start and end apart: 4, of which 1 were waited for; matrix products, arithmetic and copies ran while one was open for 8% of the time, Pallas kernels for 4%

profile of v5, /device:TPU:1, one launch (start us, length us, event | category | flops | bytes accessed | tf_op | source)
XLA Modules:
  0.0 179.7 jit_solution(5307015651144118135)
XLA Ops:
  7.2 0.0 all-gather.2.cloned.1.call-start
  7.2 1.0 copy.28
  8.2 0.8 slice_bitcast_fusion.4
  9.0 1.8 maximum_maximum_fusion
  10.8 0.0 all-gather.2.cloned.1.call-update
  10.8 0.7 convert_element_type.51
  11.5 0.7 convert_element_type.60
  12.2 0.7 copy.21
  12.9 0.1 reduce-window.8
  13.0 0.1 reduce
  13.1 0.7 sub.9
  13.7 0.7 reshape.165
  14.4 0.1 pad.29.clone
  14.5 0.2 convert_reduce_fusion
  14.7 1.0 select_reduce_fusion
  15.8 0.1 dynamic-slice_bitcast_fusion
  15.9 0.1 add_add_fusion.1
  15.9 0.1 copy.22
  16.1 0.3 compare_reduce_fusion.1
  16.4 0.1 reduce_or.18
  16.6 0.1 copy.23
  16.7 0.1 reduce_or.19
  16.8 0.1 copy.24
  17.0 3.1 %gather_fusion = s32[512]{0:T(512)S(1)} fusion(s32[8192]{0:T(1024)S(1)} %convert_reduce_fusion, s32[1024]{0:T(1024)S(1)} %pad_clamp_fusion), kind=kCustom, calls=%fused_computation | custom fusion | bytes 6144 | tf_op jit(solution)/shard_map/gather | solution.py:235
  20.1 0.1 pad.11.clone
  20.2 0.1 fusion.10
  20.3 0.1 add_convert_fusion.refs_0_
  20.4 0.5 fusion
  20.9 0.1 add_add_fusion.refs_3_
  21.0 0.3 multiply_cosine_fusion
  21.3 2.2 %fusion.2.x_ref = bf16[128,8192]{1,0:T(8,128)(2,1)S(1)} fusion(bf16[128,8192]{1,0:T(8,128)(2,1)} %param.10, f32[8192]{0:T(1024)S(1)} %convert_element_type.51, f32[128]{0:T(128)S(1)} %add_rsqrt_fusion), kind=kLoop, calls=%fused_computation.5 | loop fusion | flops 4194304 | bytes 4227584 | tf_op jit(solution)/shard_map/convert_element_type | solution.py:193
  23.4 112.2 %all-gather.2.cloned.1.call-done.w_ref = bf16[8192,1536]{1,0:T(8,128)(2,1)} async-done(((bf16[128,1536]{1,0:T(8,128)(2,1)}), bf16[8192,1536]{1,0:T(8,128)(2,1)}) %all-gather.2.cloned.1.call-update) | async-done | bytes 25165840 | tf_op jit(solution)/shard_map/all_gather | solution.py:210
  135.6 2.9 %shard_map.122 = f32[128,256]{1,0:T(8,128)S(1)} custom-call(bf16[128,8192]{1,0:T(8,128)(2,1)S(1)} %fusion.2.x_ref, bf16[8192,1536]{1,0:T(8,128)(2,1)} %all-gather.2.cloned.1.call-done.w_ref, f32[1,256]{1,0:T(1,128)S(1)} %bitcast.50), custom_call_target="tpu_custom_call" | custom-call | flops 536870912 | bytes 6291456 | tf_op jit(solution)/shard_map/pallas_call | solution.py:148
  138.6 0.1 fusion.6
  138.7 0.1 fusion.8
  138.8 0.6 pad_maximum_fusion.2
  139.5 3.1 %collective-permute-start = (bf16[128,256]{1,0:T(8,128)(2,1)}, bf16[128,256]{1,0:T(8,128)(2,1)}, u32[]{:S(2)}, u32[]{:S(2)}) collective-permute-start(bf16[128,256]{1,0:T(8,128)(2,1)} %pad_maximum_fusion.2), channel_id=1, source_target_pairs={{0,12},{4,16},{8,20},{12,24},{16,28},{20,32},{24,36},{28,40},{32,4... | collective-permute-start | bytes 196616 | tf_op jit(solution)/shard_map/ppermute | solution.py:17
  142.5 4.4 %collective-permute-start.1 = (bf16[128,256]{1,0:T(8,128)(2,1)}, bf16[128,256]{1,0:T(8,128)(2,1)}, u32[]{:S(2)}, u32[]{:S(2)}) collective-permute-start(bf16[128,256]{1,0:T(8,128)(2,1)} %pad_maximum_fusion.2), channel_id=1, source_target_pairs={{0,8},{4,12},{8,16},{12,20},{16,24},{20,28},{24,32},{28,36},{32,40... | collective-permute-start | bytes 196616 | tf_op jit(solution)/shard_map/ppermute | solution.py:17
  146.9 2.2 %collective-permute-start.2 = (bf16[128,256]{1,0:T(8,128)(2,1)}, bf16[128,256]{1,0:T(8,128)(2,1)}, u32[]{:S(2)}, u32[]{:S(2)}) collective-permute-start(bf16[128,256]{1,0:T(8,128)(2,1)} %pad_maximum_fusion.2), channel_id=1, source_target_pairs={{0,4},{4,8},{8,12},{12,16},{16,20},{20,24},{24,28},{28,32},{32,36}... | collective-permute-start | bytes 196616 | tf_op jit(solution)/shard_map/ppermute | solution.py:17
  149.1 7.5 %shard_map.121 = f32[128,1024]{1,0:T(8,128)S(1)} custom-call(bf16[128,8192]{1,0:T(8,128)(2,1)S(1)} %fusion.2.x_ref, bf16[8192,1536]{1,0:T(8,128)(2,1)} %all-gather.2.cloned.1.call-done.w_ref, f32[1,1024]{1,0:T(1,128)S(1)} %bitcast.49), custom_call_target="tpu_custom_call" | custom-call | flops 2147483648 | bytes 18874368 | tf_op jit(solution)/shard_map/pallas_call | solution.py:148
  156.6 0.1 reshape.160
  156.7 0.1 copy.26
  156.8 0.2 fusion.3
  157.0 0.2 fusion.5.refs_1_
  157.3 0.6 slice_bitcast_fusion.7
  157.9 0.9 maximum_maximum_fusion.1.refs_8_
  158.8 13.2 %shard_map.123 = bf16[1024,128]{1,0:T(8,128)(2,1)S(1)} custom-call(s32[4,2]{1,0:T(4,128)S(1)} %add_convert_fusion.refs_0_, bf16[1024,128]{1,0:T(8,128)(2,1)S(1)} %fusion.5.refs_1_, s32[1024,4]{1,0:T(8,128)S(1)} %broadcast_bitcast_fusion.refs_2_, s32[8,512]{1,0:T(8,128)S(1)} %add_add_fusion.refs_3_, bf16[64,2,64,1536]{3,2,1,0:T(8,128)(2,1)} %bitcast.51, ...), custom_call_target="tpu_custom_call" | custom-call | flops 2415919104 | bytes 4980736 | tf_op jit(solution)/shard_map/pallas_call | solution.py:127
  172.1 0.8 reshape.164
  (19 shorter events, 0.1 us)
Async XLA Ops:
  7.2 13.2 %copy-start = (bf16[128,8192]{1,0:T(8,128)(2,1)S(1)}, bf16[128,8192]{1,0:T(8,128)(2,1)}, u32[]{:S(2)}) copy-start(bf16[128,8192]{1,0:T(8,128)(2,1)} %param.10) | copy-start | bytes 6291460
  7.2 128.4 %all-gather.2.cloned.1.call-start = ((), (), s32[]{:S(2)}) async-start(), calls=%async_computation | async-start | bytes 25559040 | tf_op jit(solution)/shard_map/all_gather | solution.py:210
  138.8 19.1 %copy-start.1 = (bf16[128,128]{1,0:T(8,128)(2,1)}, bf16[128,128]{1,0:T(8,128)(2,1)S(1)}, u32[]{:S(2)}) copy-start(bf16[128,128]{1,0:T(8,128)(2,1)S(1)} %get-tuple-element.9) | copy-start | bytes 98308
  139.5 18.4 %collective-permute-start = (bf16[128,256]{1,0:T(8,128)(2,1)}, bf16[128,256]{1,0:T(8,128)(2,1)}, u32[]{:S(2)}, u32[]{:S(2)}) collective-permute-start(bf16[128,256]{1,0:T(8,128)(2,1)} %pad_maximum_fusion.2), channel_id=1, source_target_pairs={{0,12},{4,16},{8,20},{12,24},{16,28},{20,32},{24,36},{28,40},{32,4... | collective-permute-start | bytes 196616 | tf_op jit(solution)/shard_map/ppermute | solution.py:17
  142.5 15.4 %collective-permute-start.1 = (bf16[128,256]{1,0:T(8,128)(2,1)}, bf16[128,256]{1,0:T(8,128)(2,1)}, u32[]{:S(2)}, u32[]{:S(2)}) collective-permute-start(bf16[128,256]{1,0:T(8,128)(2,1)} %pad_maximum_fusion.2), channel_id=1, source_target_pairs={{0,8},{4,12},{8,16},{12,20},{16,24},{20,28},{24,32},{28,36},{32,40... | collective-permute-start | bytes 196616 | tf_op jit(solution)/shard_map/ppermute | solution.py:17
  146.9 11.0 %collective-permute-start.2 = (bf16[128,256]{1,0:T(8,128)(2,1)}, bf16[128,256]{1,0:T(8,128)(2,1)}, u32[]{:S(2)}, u32[]{:S(2)}) collective-permute-start(bf16[128,256]{1,0:T(8,128)(2,1)} %pad_maximum_fusion.2), channel_id=1, source_target_pairs={{0,4},{4,8},{8,12},{12,16},{16,20},{20,24},{24,28},{28,32},{32,36}... | collective-permute-start | bytes 196616 | tf_op jit(solution)/shard_map/ppermute | solution.py:17
Sparse Core Ops, SparseCore 0:
  10.9 124.6 all-gather.1

commit v6 on v5

--- a/solution.py
+++ b/solution.py
@@ -221,15 +221,16 @@
     pair_rows = jnp.concatenate(
         [own_keys.reshape(row_count, key_width), own_values.reshape(row_count, key_width)], axis=1
     )
-    depth = min(3, seq_count - 1)
-    earlier = []
-    for distance in range(depth, 0, -1):
-        earlier.append(from_behind(pair_rows, "seq", distance))
+    depth = 1
+    near_rows = pair_rows
+    while depth < 3:
+        near_rows = jnp.concatenate([from_behind(near_rows, "seq", depth), near_rows], axis=0)
+        depth = 2 * depth
+    depth = depth - 1
     query_own = project(normed, gathered, q_bias.astype(jnp.float32), 0, query_width // block_width, block_width)
     own_queries = rotate(query_own.reshape(row_count, heads_local, head_dim), own_positions).astype(
         jnp.bfloat16
     )
-    near_rows = jnp.concatenate(earlier + [pair_rows], axis=0)
     near_count = near_rows.shape[0]
     near_index = first_row - depth * row_count + jnp.arange(near_count, dtype=jnp.int32)
     near_segment = segment[jnp.clip(near_index, 0, all_rows - 1)]

time: 180 us -> 181 us (level); the launches traced: 180 us -> 178 us
  starting transfers between devices: 9.68 us -> 4.86 us
  waiting for transfers between devices: 112 us -> 115 us
    ppermute x3 -> x2, starting transfers between devices: 9.64 us -> 4.82 us  [from_behind(): return lax.ppermute(shard, axis, pairs)]
    ppermute x3 -> x2, waiting for transfers between devices: 0.01 us -> 2.38 us  [from_behind(): return lax.ppermute(shard, axis, pairs)]
  transfers between devices with their start and end apart: 4 -> 3, of which waited for: 1 -> 2; matrix products, arithmetic and copies ran while one was open for 8% -> 8% of each run, Pallas kernels for 4% -> 4%
where the time goes in v6:
time: 181 us; the launch traced here: 178 us
  waiting for transfers between devices  115 us (64%)
  Pallas kernels  23.7 us (13%)
  between operations  14.2 us (8%)
  other arithmetic  12.8 us (7%)
  local copies, waits for them, and re-layouts  7.92 us (4%)
  starting transfers between devices  4.86 us (3%)
    all_gather x1, waiting for transfers between devices, local(): gathered = lax.all_gather(combined, 'seq', axis=0, tiled=True)  112 us
    pallas_call x1, Pallas kernels, attend(): pl.pallas_call(kernel, grid_spec=grid_spec, out_shape=jax.ShapeDtypeStruc...  13.2 us
    pallas_call x2, Pallas kernels, project(): pl.pallas_call(projection_kernel, grid=(n_blocks,), in_specs=[pl.BlockSpe...  10.4 us
    ppermute x2, starting transfers between devices, from_behind(): return lax.ppermute(shard, axis, pairs)  4.82 us
  transfers between devices with their start and end apart: 3, of which 2 were waited for; matrix products, arithmetic and copies ran while one was open for 8% of the time, Pallas kernels for 4%

profile of v6, /device:TPU:1, one launch (start us, length us, event | category | flops | bytes accessed | tf_op | source)
XLA Modules:
  0.0 178.1 jit_solution(15526312169359847434)
XLA Ops:
  7.2 0.0 all-gather.2.cloned.1.call-start
  7.2 1.0 copy.28
  8.2 0.8 slice_bitcast_fusion.4
  9.0 1.8 maximum_maximum_fusion
  10.8 0.7 convert_element_type.51
  11.5 0.7 convert_element_type.60
  12.2 0.7 copy.21
  12.9 0.1 reduce-window.8
  13.0 0.1 reduce
  13.1 0.7 sub.9
  13.7 0.7 reshape.165
  14.4 0.1 pad.31.clone
  14.5 0.2 convert_reduce_fusion
  14.7 1.0 select_reduce_fusion
  15.8 0.1 dynamic-slice_bitcast_fusion
  15.9 0.1 add_add_fusion.1
  15.9 0.1 copy.22
  16.1 0.3 compare_reduce_fusion.1
  16.4 0.1 reduce_or.18
  16.6 0.1 copy.23
  16.7 0.1 reduce_or.19
  16.8 0.1 copy.24
  17.0 3.1 %gather_fusion = s32[512]{0:T(512)S(1)} fusion(s32[8192]{0:T(1024)S(1)} %convert_reduce_fusion, s32[1024]{0:T(1024)S(1)} %pad_clamp_fusion), kind=kCustom, calls=%fused_computation | custom fusion | bytes 6144 | tf_op jit(solution)/shard_map/gather | solution.py:236
  20.1 0.1 pad.13.clone
  20.2 0.1 fusion.10
  20.3 0.1 add_convert_fusion.refs_0_
  20.4 0.5 fusion
  20.9 0.1 add_add_fusion.refs_3_
  21.0 0.3 multiply_cosine_fusion
  21.3 2.2 %fusion.2.x_ref = bf16[128,8192]{1,0:T(8,128)(2,1)S(1)} fusion(bf16[128,8192]{1,0:T(8,128)(2,1)} %param.10, f32[8192]{0:T(1024)S(1)} %convert_element_type.51, f32[128]{0:T(128)S(1)} %add_rsqrt_fusion), kind=kLoop, calls=%fused_computation.5 | loop fusion | flops 4194304 | bytes 4227584 | tf_op jit(solution)/shard_map/convert_element_type | solution.py:193
  23.4 112.2 %all-gather.2.cloned.1.call-done.w_ref = bf16[8192,1536]{1,0:T(8,128)(2,1)} async-done(((bf16[128,1536]{1,0:T(8,128)(2,1)}), bf16[8192,1536]{1,0:T(8,128)(2,1)}) %all-gather.2.cloned.1.call-update) | async-done | bytes 25165840 | tf_op jit(solution)/shard_map/all_gather | solution.py:210
  135.6 2.9 %shard_map.122 = f32[128,256]{1,0:T(8,128)S(1)} custom-call(bf16[128,8192]{1,0:T(8,128)(2,1)S(1)} %fusion.2.x_ref, bf16[8192,1536]{1,0:T(8,128)(2,1)} %all-gather.2.cloned.1.call-done.w_ref, f32[1,256]{1,0:T(1,128)S(1)} %bitcast.50), custom_call_target="tpu_custom_call" | custom-call | flops 536870912 | bytes 6291456 | tf_op jit(solution)/shard_map/pallas_call | solution.py:148
  138.6 0.1 fusion.6
  138.7 0.1 fusion.8
  138.8 0.6 pad_maximum_fusion.2
  139.5 1.9 %collective-permute-start = (bf16[128,256]{1,0:T(8,128)(2,1)}, bf16[128,256]{1,0:T(8,128)(2,1)}, u32[]{:S(2)}, u32[]{:S(2)}) collective-permute-start(bf16[128,256]{1,0:T(8,128)(2,1)} %pad_maximum_fusion.2), channel_id=1, source_target_pairs={{0,4},{4,8},{8,12},{12,16},{16,20},{20,24},{24,28},{28,32},{32,36}... | collective-permute-start | bytes 196616 | tf_op jit(solution)/shard_map/ppermute | solution.py:17
  141.4 7.5 %shard_map.121 = f32[128,1024]{1,0:T(8,128)S(1)} custom-call(bf16[128,8192]{1,0:T(8,128)(2,1)S(1)} %fusion.2.x_ref, bf16[8192,1536]{1,0:T(8,128)(2,1)} %all-gather.2.cloned.1.call-done.w_ref, f32[1,1024]{1,0:T(1,128)S(1)} %bitcast.49), custom_call_target="tpu_custom_call" | custom-call | flops 2147483648 | bytes 18874368 | tf_op jit(solution)/shard_map/pallas_call | solution.py:148
  148.9 0.1 reshape.160
  149.0 0.1 copy.26
  149.1 0.2 fusion.3
  149.3 0.2 fusion.5.refs_1_
  149.5 0.9 maximum_maximum_fusion.2
  150.4 2.9 %collective-permute-start.1 = (bf16[256,256]{1,0:T(8,128)(2,1)S(1)}, bf16[256,256]{1,0:T(8,128)(2,1)S(1)}, u32[]{:S(2)}, u32[]{:S(2)}) collective-permute-start(bf16[256,256]{1,0:T(8,128)(2,1)S(1)} %maximum_maximum_fusion.2), channel_id=1, source_target_pairs={{0,8},{4,12},{8,16},{12,20},{16,24},{20,28},{24,32},{28,36},{32,40... | collective-permute-start | bytes 393224 | tf_op jit(solution)/shard_map/ppermute | solution.py:17
  153.3 0.6 slice_bitcast_fusion.7
  153.9 2.4 %collective-permute-done.1 = bf16[256,256]{1,0:T(8,128)(2,1)S(1)} collective-permute-done((bf16[256,256]{1,0:T(8,128)(2,1)S(1)}, bf16[256,256]{1,0:T(8,128)(2,1)S(1)}, u32[]{:S(2)}, u32[]{:S(2)}) %collective-permute-start.1) | collective-permute-done | bytes 131104 | tf_op jit(solution)/shard_map/ppermute | solution.py:17
  156.3 0.9 maximum_maximum_fusion.1.refs_8_
  157.2 13.2 %shard_map.123 = bf16[1024,128]{1,0:T(8,128)(2,1)S(1)} custom-call(s32[4,2]{1,0:T(4,128)S(1)} %add_convert_fusion.refs_0_, bf16[1024,128]{1,0:T(8,128)(2,1)S(1)} %fusion.5.refs_1_, s32[1024,4]{1,0:T(8,128)S(1)} %broadcast_bitcast_fusion.refs_2_, s32[8,512]{1,0:T(8,128)S(1)} %add_add_fusion.refs_3_, bf16[64,2,64,1536]{3,2,1,0:T(8,128)(2,1)} %bitcast.51, ...), custom_call_target="tpu_custom_call" | custom-call | flops 2415919104 | bytes 4980736 | tf_op jit(solution)/shard_map/pallas_call | solution.py:127
  170.4 0.8 reshape.164
  (18 shorter events, 0.2 us)
Async XLA Ops:
  7.2 13.2 %copy-start = (bf16[128,8192]{1,0:T(8,128)(2,1)S(1)}, bf16[128,8192]{1,0:T(8,128)(2,1)}, u32[]{:S(2)}) copy-start(bf16[128,8192]{1,0:T(8,128)(2,1)} %param.10) | copy-start | bytes 6291460
  7.2 128.4 %all-gather.2.cloned.1.call-start = ((), (), s32[]{:S(2)}) async-start(), calls=%async_computation | async-start | bytes 25559040 | tf_op jit(solution)/shard_map/all_gather | solution.py:210
  138.8 17.5 %copy-start.1 = (bf16[128,128]{1,0:T(8,128)(2,1)}, bf16[128,128]{1,0:T(8,128)(2,1)S(1)}, u32[]{:S(2)}) copy-start(bf16[128,128]{1,0:T(8,128)(2,1)S(1)} %get-tuple-element.9) | copy-start | bytes 98308
  139.5 10.1 %collective-permute-start = (bf16[128,256]{1,0:T(8,128)(2,1)}, bf16[128,256]{1,0:T(8,128)(2,1)}, u32[]{:S(2)}, u32[]{:S(2)}) collective-permute-start(bf16[128,256]{1,0:T(8,128)(2,1)} %pad_maximum_fusion.2), channel_id=1, source_target_pairs={{0,4},{4,8},{8,12},{12,16},{16,20},{20,24},{24,28},{28,32},{32,36}... | collective-permute-start | bytes 196616 | tf_op jit(solution)/shard_map/ppermute | solution.py:17
  150.4 5.9 %collective-permute-start.1 = (bf16[256,256]{1,0:T(8,128)(2,1)S(1)}, bf16[256,256]{1,0:T(8,128)(2,1)S(1)}, u32[]{:S(2)}, u32[]{:S(2)}) collective-permute-start(bf16[256,256]{1,0:T(8,128)(2,1)S(1)} %maximum_maximum_fusion.2), channel_id=1, source_target_pairs={{0,8},{4,12},{8,16},{12,20},{16,24},{20,28},{24,32},{28,36},{32,40... | collective-permute-start | bytes 393224 | tf_op jit(solution)/shard_map/ppermute | solution.py:17
Sparse Core Ops, SparseCore 0:
  10.9 124.6 all-gather.1

commit v7 on v6

--- a/solution.py
+++ b/solution.py
@@ -90,7 +90,7 @@
 
 def attend(q_rows, row_info, col_info, cache, kv_column, near_slab):
     n_rows, head_dim = q_rows.shape
-    block = math.gcd(n_rows, 256)
+    block = math.gcd(n_rows, 512)
     n_blocks = n_rows // block
     n_dev, _, cache_local, _ = cache.shape
     cache_len = n_dev * cache_local

time: 181 us -> 188 us (1.039)
  the two profiles are of different devices: /device:TPU:1 before, /device:TPU:2 now
where the time goes in v7:
time: 188 us
  waiting for transfers between devices  117 us (62%)
  Pallas kernels  31.7 us (17%)
  between operations  14.2 us (8%)
  other arithmetic  12.8 us (7%)
  local copies, waits for them, and re-layouts  7.92 us (4%)
  starting transfers between devices  4.11 us (2%)
    all_gather x1, waiting for transfers between devices, local(): gathered = lax.all_gather(combined, 'seq', axis=0, tiled=True)  110 us
    pallas_call x1, Pallas kernels, attend(): pl.pallas_call(kernel, grid_spec=grid_spec, out_shape=jax.ShapeDtypeStruc...  21.3 us
    pallas_call x2, Pallas kernels, project(): pl.pallas_call(projection_kernel, grid=(n_blocks,), in_specs=[pl.BlockSpe...  10.4 us
    ppermute x2, waiting for transfers between devices, from_behind(): return lax.ppermute(shard, axis, pairs)  7.02 us
    ppermute x2, starting transfers between devices, from_behind(): return lax.ppermute(shard, axis, pairs)  4.07 us
  transfers between devices with their start and end apart: 3, of which 2 were waited for; matrix products, arithmetic and copies ran while one was open for 7% of the time, Pallas kernels for 4%

profile of v7, /device:TPU:2, one launch (start us, length us, event | category | flops | bytes accessed | tf_op | source)
XLA Modules:
  0.0 187.5 jit_solution(2149538515437529101)
XLA Ops:
  7.2 0.0 all-gather.2.cloned.1.call-start
  7.2 1.0 copy.28
  8.2 0.8 slice_bitcast_fusion.4
  9.0 1.8 maximum_maximum_fusion
  10.8 0.7 convert_element_type.51
  11.5 0.7 convert_element_type.60
  12.2 0.7 copy.21
  12.9 0.1 reduce-window.8
  13.0 0.1 reduce
  13.1 0.7 sub.9
  13.7 0.7 reshape.165
  14.4 0.1 pad.31.clone
  14.5 0.2 convert_reduce_fusion
  14.7 1.0 select_reduce_fusion
  15.8 0.1 dynamic-slice_bitcast_fusion
  15.9 0.1 add_add_fusion.1
  15.9 0.1 copy.22
  16.1 0.3 compare_reduce_fusion.1
  16.4 0.1 reduce_or.18
  16.6 0.1 copy.23
  16.7 0.1 reduce_or.19
  16.8 0.1 copy.24
  17.0 3.1 %gather_fusion = s32[512]{0:T(512)S(1)} fusion(s32[8192]{0:T(1024)S(1)} %convert_reduce_fusion, s32[1024]{0:T(1024)S(1)} %pad_clamp_fusion), kind=kCustom, calls=%fused_computation | custom fusion | bytes 6144 | tf_op jit(solution)/shard_map/gather | solution.py:236
  20.1 0.1 pad.13.clone
  20.2 0.1 fusion.10
  20.3 0.1 add_convert_fusion.refs_0_
  20.4 0.5 fusion
  20.9 0.1 add_add_fusion.refs_3_
  21.0 0.3 multiply_cosine_fusion
  21.3 2.2 %fusion.2.x_ref = bf16[128,8192]{1,0:T(8,128)(2,1)S(1)} fusion(bf16[128,8192]{1,0:T(8,128)(2,1)} %param.10, f32[8192]{0:T(1024)S(1)} %convert_element_type.51, f32[128]{0:T(128)S(1)} %add_rsqrt_fusion), kind=kLoop, calls=%fused_computation.5 | loop fusion | flops 4194304 | bytes 4227584 | tf_op jit(solution)/shard_map/convert_element_type | solution.py:193
  23.5 109.7 %all-gather.2.cloned.1.call-done.w_ref = bf16[8192,1536]{1,0:T(8,128)(2,1)} async-done(((bf16[128,1536]{1,0:T(8,128)(2,1)}), bf16[8192,1536]{1,0:T(8,128)(2,1)}) %all-gather.2.cloned.1.call-update) | async-done | bytes 25165840 | tf_op jit(solution)/shard_map/all_gather | solution.py:210
  133.1 2.9 %shard_map.122 = f32[128,256]{1,0:T(8,128)S(1)} custom-call(bf16[128,8192]{1,0:T(8,128)(2,1)S(1)} %fusion.2.x_ref, bf16[8192,1536]{1,0:T(8,128)(2,1)} %all-gather.2.cloned.1.call-done.w_ref, f32[1,256]{1,0:T(1,128)S(1)} %bitcast.50), custom_call_target="tpu_custom_call" | custom-call | flops 536870912 | bytes 6291456 | tf_op jit(solution)/shard_map/pallas_call | solution.py:148
  136.1 0.1 fusion.6
  136.2 0.1 fusion.8
  136.3 0.6 pad_maximum_fusion.2
  137.0 2.1 %collective-permute-start = (bf16[128,256]{1,0:T(8,128)(2,1)}, bf16[128,256]{1,0:T(8,128)(2,1)}, u32[]{:S(2)}, u32[]{:S(2)}) collective-permute-start(bf16[128,256]{1,0:T(8,128)(2,1)} %pad_maximum_fusion.2), channel_id=1, source_target_pairs={{0,4},{4,8},{8,12},{12,16},{16,20},{20,24},{24,28},{28,32},{32,36}... | collective-permute-start | bytes 196616 | tf_op jit(solution)/shard_map/ppermute | solution.py:17
  139.1 7.5 %shard_map.121 = f32[128,1024]{1,0:T(8,128)S(1)} custom-call(bf16[128,8192]{1,0:T(8,128)(2,1)S(1)} %fusion.2.x_ref, bf16[8192,1536]{1,0:T(8,128)(2,1)} %all-gather.2.cloned.1.call-done.w_ref, f32[1,1024]{1,0:T(1,128)S(1)} %bitcast.49), custom_call_target="tpu_custom_call" | custom-call | flops 2147483648 | bytes 18874368 | tf_op jit(solution)/shard_map/pallas_call | solution.py:148
  146.6 0.1 reshape.160
  146.7 0.1 copy.26
  146.8 0.2 fusion.3
  147.0 0.2 fusion.5.refs_1_
  147.3 0.9 maximum_maximum_fusion.2
  148.1 1.9 %collective-permute-start.1 = (bf16[256,256]{1,0:T(8,128)(2,1)S(1)}, bf16[256,256]{1,0:T(8,128)(2,1)S(1)}, u32[]{:S(2)}, u32[]{:S(2)}) collective-permute-start(bf16[256,256]{1,0:T(8,128)(2,1)S(1)} %maximum_maximum_fusion.2), channel_id=1, source_target_pairs={{0,8},{4,12},{8,16},{12,20},{16,24},{20,28},{24,32},{28,36},{32,40... | collective-permute-start | bytes 393224 | tf_op jit(solution)/shard_map/ppermute | solution.py:17
  150.1 0.6 slice_bitcast_fusion.7
  150.7 7.0 %collective-permute-done.1 = bf16[256,256]{1,0:T(8,128)(2,1)S(1)} collective-permute-done((bf16[256,256]{1,0:T(8,128)(2,1)S(1)}, bf16[256,256]{1,0:T(8,128)(2,1)S(1)}, u32[]{:S(2)}, u32[]{:S(2)}) %collective-permute-start.1) | collective-permute-done | bytes 131104 | tf_op jit(solution)/shard_map/ppermute | solution.py:17
  157.7 0.9 maximum_maximum_fusion.1.refs_8_
  158.6 21.3 %shard_map.123 = bf16[1024,128]{1,0:T(8,128)(2,1)S(1)} custom-call(s32[2,2]{1,0:T(2,128)S(1)} %add_convert_fusion.refs_0_, bf16[1024,128]{1,0:T(8,128)(2,1)S(1)} %fusion.5.refs_1_, s32[1024,4]{1,0:T(8,128)S(1)} %broadcast_bitcast_fusion.refs_2_, s32[8,512]{1,0:T(8,128)S(1)} %add_add_fusion.refs_3_, bf16[64,2,64,1536]{3,2,1,0:T(8,128)(2,1)} %bitcast.51, ...), custom_call_target="tpu_custom_call" | custom-call | flops 2415919104 | bytes 4980736 | tf_op jit(solution)/shard_map/pallas_call | solution.py:127
  179.9 0.8 reshape.164
  (18 shorter events, 0.2 us)
Async XLA Ops:
  7.2 13.2 %copy-start = (bf16[128,8192]{1,0:T(8,128)(2,1)S(1)}, bf16[128,8192]{1,0:T(8,128)(2,1)}, u32[]{:S(2)}) copy-start(bf16[128,8192]{1,0:T(8,128)(2,1)} %param.10) | copy-start | bytes 6291460
  7.2 125.9 %all-gather.2.cloned.1.call-start = ((), (), s32[]{:S(2)}) async-start(), calls=%async_computation | async-start | bytes 25559040 | tf_op jit(solution)/shard_map/all_gather | solution.py:210
  136.3 21.4 %copy-start.1 = (bf16[128,128]{1,0:T(8,128)(2,1)}, bf16[128,128]{1,0:T(8,128)(2,1)S(1)}, u32[]{:S(2)}) copy-start(bf16[128,128]{1,0:T(8,128)(2,1)S(1)} %get-tuple-element.9) | copy-start | bytes 98308
  137.0 10.3 %collective-permute-start = (bf16[128,256]{1,0:T(8,128)(2,1)}, bf16[128,256]{1,0:T(8,128)(2,1)}, u32[]{:S(2)}, u32[]{:S(2)}) collective-permute-start(bf16[128,256]{1,0:T(8,128)(2,1)} %pad_maximum_fusion.2), channel_id=1, source_target_pairs={{0,4},{4,8},{8,12},{12,16},{16,20},{20,24},{24,28},{28,32},{32,36}... | collective-permute-start | bytes 196616 | tf_op jit(solution)/shard_map/ppermute | solution.py:17
  148.1 9.6 %collective-permute-start.1 = (bf16[256,256]{1,0:T(8,128)(2,1)S(1)}, bf16[256,256]{1,0:T(8,128)(2,1)S(1)}, u32[]{:S(2)}, u32[]{:S(2)}) collective-permute-start(bf16[256,256]{1,0:T(8,128)(2,1)S(1)} %maximum_maximum_fusion.2), channel_id=1, source_target_pairs={{0,8},{4,12},{8,16},{12,20},{16,24},{20,28},{24,32},{28,36},{32,40... | collective-permute-start | bytes 393224 | tf_op jit(solution)/shard_map/ppermute | solution.py:17
Sparse Core Ops, SparseCore 0:
  10.9 122.1 all-gather.1

commit v8 on v7

--- a/solution.py
+++ b/solution.py
@@ -90,7 +90,7 @@
 
 def attend(q_rows, row_info, col_info, cache, kv_column, near_slab):
     n_rows, head_dim = q_rows.shape
-    block = math.gcd(n_rows, 512)
+    block = math.gcd(n_rows, 128)
     n_blocks = n_rows // block
     n_dev, _, cache_local, _ = cache.shape
     cache_len = n_dev * cache_local

time: 188 us -> 182 us (0.968)
  the two profiles are of different devices: /device:TPU:2 before, /device:TPU:1 now
where the time goes in v8:
time: 182 us; the launch traced here: 180 us
  waiting for transfers between devices  115 us (63%)
  Pallas kernels  25.7 us (14%)
  between operations  14.3 us (8%)
  other arithmetic  12.8 us (7%)
  local copies, waits for them, and re-layouts  7.87 us (4%)
  starting transfers between devices  4.67 us (3%)
    all_gather x1, waiting for transfers between devices, local(): gathered = lax.all_gather(combined, 'seq', axis=0, tiled=True)  112 us
    pallas_call x1, Pallas kernels, attend(): pl.pallas_call(kernel, grid_spec=grid_spec, out_shape=jax.ShapeDtypeStruc...  15.3 us
    pallas_call x2, Pallas kernels, project(): pl.pallas_call(projection_kernel, grid=(n_blocks,), in_specs=[pl.BlockSpe...  10.4 us
    ppermute x2, starting transfers between devices, from_behind(): return lax.ppermute(shard, axis, pairs)  4.64 us
  transfers between devices with their start and end apart: 3, of which 2 were waited for; matrix products, arithmetic and copies ran while one was open for 8% of the time, Pallas kernels for 4%

profile of v8, /device:TPU:1, one launch (start us, length us, event | category | flops | bytes accessed | tf_op | source)
XLA Modules:
  0.0 180.1 jit_solution(7532039690187466199)
XLA Ops:
  7.2 0.0 all-gather.2.cloned.1.call-start
  7.2 1.0 copy.28
  8.2 0.8 slice_bitcast_fusion.4
  9.0 1.8 maximum_maximum_fusion
  10.8 0.7 convert_element_type.51
  11.5 0.7 convert_element_type.60
  12.2 0.7 copy.21
  12.9 0.1 reduce-window.8
  13.0 0.1 reduce
  13.1 0.7 sub.9
  13.7 0.7 reshape.165
  14.4 0.1 pad.31.clone
  14.5 0.2 convert_reduce_fusion
  14.7 1.0 select_reduce_fusion
  15.8 0.1 dynamic-slice_bitcast_fusion
  15.9 0.1 add_add_fusion.1
  15.9 0.1 copy.22
  16.1 0.3 compare_reduce_fusion.1
  16.4 0.1 bitcast_reduce_fusion.1
  16.6 0.1 copy.23
  16.7 0.1 bitcast_reduce_fusion
  16.8 0.1 copy.24
  16.9 3.1 %gather_fusion = s32[512]{0:T(512)S(1)} fusion(s32[8192]{0:T(1024)S(1)} %convert_reduce_fusion, s32[1024]{0:T(1024)S(1)} %pad_clamp_fusion), kind=kCustom, calls=%fused_computation | custom fusion | bytes 6144 | tf_op jit(solution)/shard_map/gather | solution.py:236
  20.1 0.1 pad.13.clone
  20.2 0.1 fusion.10
  20.2 0.1 add_convert_fusion.refs_0_
  20.3 0.5 fusion
  20.8 0.1 add_add_fusion.refs_3_
  20.9 0.3 multiply_cosine_fusion
  21.2 2.2 %fusion.2.x_ref = bf16[128,8192]{1,0:T(8,128)(2,1)S(1)} fusion(bf16[128,8192]{1,0:T(8,128)(2,1)} %param.10, f32[8192]{0:T(1024)S(1)} %convert_element_type.51, f32[128]{0:T(128)S(1)} %add_rsqrt_fusion), kind=kLoop, calls=%fused_computation.5 | loop fusion | flops 4194304 | bytes 4227584 | tf_op jit(solution)/shard_map/convert_element_type | solution.py:193
  23.4 112.2 %all-gather.2.cloned.1.call-done.w_ref = bf16[8192,1536]{1,0:T(8,128)(2,1)} async-done(((bf16[128,1536]{1,0:T(8,128)(2,1)}), bf16[8192,1536]{1,0:T(8,128)(2,1)}) %all-gather.2.cloned.1.call-update) | async-done | bytes 25165840 | tf_op jit(solution)/shard_map/all_gather | solution.py:210
  135.6 2.9 %shard_map.122 = f32[128,256]{1,0:T(8,128)S(1)} custom-call(bf16[128,8192]{1,0:T(8,128)(2,1)S(1)} %fusion.2.x_ref, bf16[8192,1536]{1,0:T(8,128)(2,1)} %all-gather.2.cloned.1.call-done.w_ref, f32[1,256]{1,0:T(1,128)S(1)} %bitcast.54), custom_call_target="tpu_custom_call" | custom-call | flops 536870912 | bytes 6291456 | tf_op jit(solution)/shard_map/pallas_call | solution.py:148
  138.6 0.1 fusion.6
  138.7 0.1 fusion.8
  138.8 0.6 pad_maximum_fusion.2
  139.5 1.9 %collective-permute-start = (bf16[128,256]{1,0:T(8,128)(2,1)}, bf16[128,256]{1,0:T(8,128)(2,1)}, u32[]{:S(2)}, u32[]{:S(2)}) collective-permute-start(bf16[128,256]{1,0:T(8,128)(2,1)} %pad_maximum_fusion.2), channel_id=1, source_target_pairs={{0,4},{4,8},{8,12},{12,16},{16,20},{20,24},{24,28},{28,32},{32,36}... | collective-permute-start | bytes 196616 | tf_op jit(solution)/shard_map/ppermute | solution.py:17
  141.4 7.5 %shard_map.121 = f32[128,1024]{1,0:T(8,128)S(1)} custom-call(bf16[128,8192]{1,0:T(8,128)(2,1)S(1)} %fusion.2.x_ref, bf16[8192,1536]{1,0:T(8,128)(2,1)} %all-gather.2.cloned.1.call-done.w_ref, f32[1,1024]{1,0:T(1,128)S(1)} %bitcast.53), custom_call_target="tpu_custom_call" | custom-call | flops 2147483648 | bytes 18874368 | tf_op jit(solution)/shard_map/pallas_call | solution.py:148
  148.9 0.1 reshape.160
  149.0 0.1 copy.26
  149.1 0.2 fusion.3
  149.3 0.2 fusion.5.refs_1_
  149.6 0.9 maximum_maximum_fusion.2
  150.4 2.7 %collective-permute-start.1 = (bf16[256,256]{1,0:T(8,128)(2,1)S(1)}, bf16[256,256]{1,0:T(8,128)(2,1)S(1)}, u32[]{:S(2)}, u32[]{:S(2)}) collective-permute-start(bf16[256,256]{1,0:T(8,128)(2,1)S(1)} %maximum_maximum_fusion.2), channel_id=1, source_target_pairs={{0,8},{4,12},{8,16},{12,20},{16,24},{20,28},{24,32},{28,36},{32,40... | collective-permute-start | bytes 393224 | tf_op jit(solution)/shard_map/ppermute | solution.py:17
  153.1 0.6 slice_bitcast_fusion.7
  153.8 2.6 %collective-permute-done.1 = bf16[256,256]{1,0:T(8,128)(2,1)S(1)} collective-permute-done((bf16[256,256]{1,0:T(8,128)(2,1)S(1)}, bf16[256,256]{1,0:T(8,128)(2,1)S(1)}, u32[]{:S(2)}, u32[]{:S(2)}) %collective-permute-start.1) | collective-permute-done | bytes 131104 | tf_op jit(solution)/shard_map/ppermute | solution.py:17
  156.3 0.9 maximum_maximum_fusion.1.refs_8_
  157.2 15.3 %shard_map.123 = bf16[1024,128]{1,0:T(8,128)(2,1)S(1)} custom-call(s32[8,2]{1,0:T(8,128)S(1)} %add_convert_fusion.refs_0_, bf16[1024,128]{1,0:T(8,128)(2,1)S(1)} %fusion.5.refs_1_, s32[1024,4]{1,0:T(8,128)S(1)} %broadcast_bitcast_fusion.refs_2_, s32[8,512]{1,0:T(8,128)S(1)} %add_add_fusion.refs_3_, bf16[64,2,64,1536]{3,2,1,0:T(8,128)(2,1)} %bitcast.55, ...), custom_call_target="tpu_custom_call" | custom-call | flops 2415919104 | bytes 4980736 | tf_op jit(solution)/shard_map/pallas_call | solution.py:127
  172.5 0.8 reshape.164
  (16 shorter events, 0.1 us)
Async XLA Ops:
  7.2 13.1 %copy-start = (bf16[128,8192]{1,0:T(8,128)(2,1)S(1)}, bf16[128,8192]{1,0:T(8,128)(2,1)}, u32[]{:S(2)}) copy-start(bf16[128,8192]{1,0:T(8,128)(2,1)} %param.10) | copy-start | bytes 6291460
  7.2 128.4 %all-gather.2.cloned.1.call-start = ((), (), s32[]{:S(2)}) async-start(), calls=%async_computation | async-start | bytes 25559040 | tf_op jit(solution)/shard_map/all_gather | solution.py:210
  138.8 17.5 %copy-start.1 = (bf16[128,128]{1,0:T(8,128)(2,1)}, bf16[128,128]{1,0:T(8,128)(2,1)S(1)}, u32[]{:S(2)}) copy-start(bf16[128,128]{1,0:T(8,128)(2,1)S(1)} %get-tuple-element.9) | copy-start | bytes 98308
  139.5 10.1 %collective-permute-start = (bf16[128,256]{1,0:T(8,128)(2,1)}, bf16[128,256]{1,0:T(8,128)(2,1)}, u32[]{:S(2)}, u32[]{:S(2)}) collective-permute-start(bf16[128,256]{1,0:T(8,128)(2,1)} %pad_maximum_fusion.2), channel_id=1, source_target_pairs={{0,4},{4,8},{8,12},{12,16},{16,20},{20,24},{24,28},{28,32},{32,36}... | collective-permute-start | bytes 196616 | tf_op jit(solution)/shard_map/ppermute | solution.py:17
  150.4 5.9 %collective-permute-start.1 = (bf16[256,256]{1,0:T(8,128)(2,1)S(1)}, bf16[256,256]{1,0:T(8,128)(2,1)S(1)}, u32[]{:S(2)}, u32[]{:S(2)}) collective-permute-start(bf16[256,256]{1,0:T(8,128)(2,1)S(1)} %maximum_maximum_fusion.2), channel_id=1, source_target_pairs={{0,8},{4,12},{8,16},{12,20},{16,24},{20,28},{24,32},{28,36},{32,40... | collective-permute-start | bytes 393224 | tf_op jit(solution)/shard_map/ppermute | solution.py:17
Sparse Core Ops, SparseCore 0:
  10.9 124.6 all-gather.1

commit v9 on v6

--- a/solution.py
+++ b/solution.py
@@ -54,12 +54,12 @@
     def finish(q, far, value):
         rows = row_ref[...]
         cols = col_ref[...]
-        near = lax.dot_general(q, near_ref[:, 0:d], dims, preferred_element_type=jnp.float32) * scale
+        near = lax.dot_general(q, near_ref[:, 0:d], dims, preferred_element_type=jnp.float32)
         visible = (cols[0:1, :] == rows[:, 1:2]) & (cols[1:2, :] <= rows[:, 2:3])
         near = jnp.where(visible, near, -jnp.inf)
-        top = jnp.maximum(jnp.max(near, axis=1, keepdims=True), jnp.max(far, axis=1, keepdims=True))
-        near_w = jnp.exp(near - top)
-        far_w = jnp.exp(far - top)
+        top = jnp.maximum(jnp.max(near, axis=1, keepdims=True), jnp.max(far, axis=1, keepdims=True)) * scale
+        near_w = jnp.exp(near * scale - top)
+        far_w = jnp.exp(far * scale - top)
         mass = jnp.sum(near_w, axis=1, keepdims=True) + jnp.sum(far_w, axis=1, keepdims=True)
         acc = jnp.dot(near_w.astype(jnp.bfloat16), near_ref[:, d : 2 * d], preferred_element_type=jnp.float32)
         acc = value(far_w.astype(jnp.bfloat16), acc)
@@ -67,14 +67,14 @@
 
     def single(p):
         q = q_ref[...]
-        far = lax.dot_general(q, full(key_refs[p]), dims, preferred_element_type=jnp.float32) * scale
+        far = lax.dot_general(q, full(key_refs[p]), dims, preferred_element_type=jnp.float32)
         finish(q, far, lambda w, acc: acc + jnp.dot(w, full(value_refs[p]), preferred_element_type=jnp.float32))
 
     def both():
         q = q_ref[...]
         use_first = row_ref[...][:, 0:1] == 0
-        far0 = lax.dot_general(q, full(k0_ref), dims, preferred_element_type=jnp.float32) * scale
-        far1 = lax.dot_general(q, full(k1_ref), dims, preferred_element_type=jnp.float32) * scale
+        far0 = lax.dot_general(q, full(k0_ref), dims, preferred_element_type=jnp.float32)
+        far1 = lax.dot_general(q, full(k1_ref), dims, preferred_element_type=jnp.float32)
 
         def value(w, acc):
             zero = jnp.zeros_like(w)

time: 181 us -> 180 us (level)
  no operation moved by 1% of the time
where the time goes in v9:
time: 180 us; the launch traced here: 177 us
  waiting for transfers between devices  115 us (64%)
  Pallas kernels  23.1 us (13%)
  between operations  14.2 us (8%)
  other arithmetic  12.8 us (7%)
  local copies, waits for them, and re-layouts  7.92 us (4%)
  starting transfers between devices  4.86 us (3%)
    all_gather x1, waiting for transfers between devices, local(): gathered = lax.all_gather(combined, 'seq', axis=0, tiled=True)  112 us
    pallas_call x1, Pallas kernels, attend(): pl.pallas_call(kernel, grid_spec=grid_spec, out_shape=jax.ShapeDtypeStruc...  12.6 us
    pallas_call x2, Pallas kernels, project(): pl.pallas_call(projection_kernel, grid=(n_blocks,), in_specs=[pl.BlockSpe...  10.4 us
    ppermute x2, starting transfers between devices, from_behind(): return lax.ppermute(shard, axis, pairs)  4.82 us
  transfers between devices with their start and end apart: 3, of which 2 were waited for; matrix products, arithmetic and copies ran while one was open for 8% of the time, Pallas kernels for 4%

profile of v9, /device:TPU:1, one launch (start us, length us, event | category | flops | bytes accessed | tf_op | source)
XLA Modules:
  0.0 177.5 jit_solution(15898380879166791129)
XLA Ops:
  7.2 0.0 all-gather.2.cloned.1.call-start
  7.2 1.0 copy.28
  8.2 0.8 slice_bitcast_fusion.4
  9.0 1.8 maximum_maximum_fusion
  10.8 0.7 convert_element_type.51
  11.5 0.7 convert_element_type.60
  12.2 0.7 copy.21
  12.9 0.1 reduce-window.8
  13.0 0.1 reduce
  13.1 0.7 sub.9
  13.7 0.7 reshape.165
  14.4 0.1 pad.31.clone
  14.5 0.2 convert_reduce_fusion
  14.7 1.0 select_reduce_fusion
  15.8 0.1 dynamic-slice_bitcast_fusion
  15.9 0.1 add_add_fusion.1
  15.9 0.1 copy.22
  16.1 0.3 compare_reduce_fusion.1
  16.4 0.1 reduce_or.18
  16.6 0.1 copy.23
  16.7 0.1 reduce_or.19
  16.8 0.1 copy.24
  17.0 3.1 %gather_fusion = s32[512]{0:T(512)S(1)} fusion(s32[8192]{0:T(1024)S(1)} %convert_reduce_fusion, s32[1024]{0:T(1024)S(1)} %pad_clamp_fusion), kind=kCustom, calls=%fused_computation | custom fusion | bytes 6144 | tf_op jit(solution)/shard_map/gather | solution.py:236
  20.1 0.1 pad.13.clone
  20.2 0.1 fusion.10
  20.3 0.1 add_convert_fusion.refs_0_
  20.4 0.5 fusion
  20.9 0.1 add_add_fusion.refs_3_
  21.0 0.3 multiply_cosine_fusion
  21.3 2.2 %fusion.2.x_ref = bf16[128,8192]{1,0:T(8,128)(2,1)S(1)} fusion(bf16[128,8192]{1,0:T(8,128)(2,1)} %param.10, f32[8192]{0:T(1024)S(1)} %convert_element_type.51, f32[128]{0:T(128)S(1)} %add_rsqrt_fusion), kind=kLoop, calls=%fused_computation.5 | loop fusion | flops 4194304 | bytes 4227584 | tf_op jit(solution)/shard_map/convert_element_type | solution.py:193
  23.4 112.2 %all-gather.2.cloned.1.call-done.w_ref = bf16[8192,1536]{1,0:T(8,128)(2,1)} async-done(((bf16[128,1536]{1,0:T(8,128)(2,1)}), bf16[8192,1536]{1,0:T(8,128)(2,1)}) %all-gather.2.cloned.1.call-update) | async-done | bytes 25165840 | tf_op jit(solution)/shard_map/all_gather | solution.py:210
  135.6 2.9 %shard_map.122 = f32[128,256]{1,0:T(8,128)S(1)} custom-call(bf16[128,8192]{1,0:T(8,128)(2,1)S(1)} %fusion.2.x_ref, bf16[8192,1536]{1,0:T(8,128)(2,1)} %all-gather.2.cloned.1.call-done.w_ref, f32[1,256]{1,0:T(1,128)S(1)} %bitcast.50), custom_call_target="tpu_custom_call" | custom-call | flops 536870912 | bytes 6291456 | tf_op jit(solution)/shard_map/pallas_call | solution.py:148
  138.6 0.1 fusion.6
  138.7 0.1 fusion.8
  138.8 0.6 pad_maximum_fusion.2
  139.5 1.9 %collective-permute-start = (bf16[128,256]{1,0:T(8,128)(2,1)}, bf16[128,256]{1,0:T(8,128)(2,1)}, u32[]{:S(2)}, u32[]{:S(2)}) collective-permute-start(bf16[128,256]{1,0:T(8,128)(2,1)} %pad_maximum_fusion.2), channel_id=1, source_target_pairs={{0,4},{4,8},{8,12},{12,16},{16,20},{20,24},{24,28},{28,32},{32,36}... | collective-permute-start | bytes 196616 | tf_op jit(solution)/shard_map/ppermute | solution.py:17
  141.4 7.5 %shard_map.121 = f32[128,1024]{1,0:T(8,128)S(1)} custom-call(bf16[128,8192]{1,0:T(8,128)(2,1)S(1)} %fusion.2.x_ref, bf16[8192,1536]{1,0:T(8,128)(2,1)} %all-gather.2.cloned.1.call-done.w_ref, f32[1,1024]{1,0:T(1,128)S(1)} %bitcast.49), custom_call_target="tpu_custom_call" | custom-call | flops 2147483648 | bytes 18874368 | tf_op jit(solution)/shard_map/pallas_call | solution.py:148
  148.9 0.1 reshape.160
  149.0 0.1 copy.26
  149.1 0.2 fusion.3
  149.3 0.2 fusion.5.refs_1_
  149.5 0.9 maximum_maximum_fusion.2
  150.4 2.9 %collective-permute-start.1 = (bf16[256,256]{1,0:T(8,128)(2,1)S(1)}, bf16[256,256]{1,0:T(8,128)(2,1)S(1)}, u32[]{:S(2)}, u32[]{:S(2)}) collective-permute-start(bf16[256,256]{1,0:T(8,128)(2,1)S(1)} %maximum_maximum_fusion.2), channel_id=1, source_target_pairs={{0,8},{4,12},{8,16},{12,20},{16,24},{20,28},{24,32},{28,36},{32,40... | collective-permute-start | bytes 393224 | tf_op jit(solution)/shard_map/ppermute | solution.py:17
  153.3 0.6 slice_bitcast_fusion.7
  153.9 2.4 %collective-permute-done.1 = bf16[256,256]{1,0:T(8,128)(2,1)S(1)} collective-permute-done((bf16[256,256]{1,0:T(8,128)(2,1)S(1)}, bf16[256,256]{1,0:T(8,128)(2,1)S(1)}, u32[]{:S(2)}, u32[]{:S(2)}) %collective-permute-start.1) | collective-permute-done | bytes 131104 | tf_op jit(solution)/shard_map/ppermute | solution.py:17
  156.3 0.9 maximum_maximum_fusion.1.refs_8_
  157.2 12.6 %shard_map.123 = bf16[1024,128]{1,0:T(8,128)(2,1)S(1)} custom-call(s32[4,2]{1,0:T(4,128)S(1)} %add_convert_fusion.refs_0_, bf16[1024,128]{1,0:T(8,128)(2,1)S(1)} %fusion.5.refs_1_, s32[1024,4]{1,0:T(8,128)S(1)} %broadcast_bitcast_fusion.refs_2_, s32[8,512]{1,0:T(8,128)S(1)} %add_add_fusion.refs_3_, bf16[64,2,64,1536]{3,2,1,0:T(8,128)(2,1)} %bitcast.51, ...), custom_call_target="tpu_custom_call" | custom-call | flops 2415919104 | bytes 4980736 | tf_op jit(solution)/shard_map/pallas_call | solution.py:127
  169.8 0.8 reshape.164
  (18 shorter events, 0.2 us)
Async XLA Ops:
  7.2 13.2 %copy-start = (bf16[128,8192]{1,0:T(8,128)(2,1)S(1)}, bf16[128,8192]{1,0:T(8,128)(2,1)}, u32[]{:S(2)}) copy-start(bf16[128,8192]{1,0:T(8,128)(2,1)} %param.10) | copy-start | bytes 6291460
  7.2 128.4 %all-gather.2.cloned.1.call-start = ((), (), s32[]{:S(2)}) async-start(), calls=%async_computation | async-start | bytes 25559040 | tf_op jit(solution)/shard_map/all_gather | solution.py:210
  138.8 17.5 %copy-start.1 = (bf16[128,128]{1,0:T(8,128)(2,1)}, bf16[128,128]{1,0:T(8,128)(2,1)S(1)}, u32[]{:S(2)}) copy-start(bf16[128,128]{1,0:T(8,128)(2,1)S(1)} %get-tuple-element.9) | copy-start | bytes 98308
  139.5 10.1 %collective-permute-start = (bf16[128,256]{1,0:T(8,128)(2,1)}, bf16[128,256]{1,0:T(8,128)(2,1)}, u32[]{:S(2)}, u32[]{:S(2)}) collective-permute-start(bf16[128,256]{1,0:T(8,128)(2,1)} %pad_maximum_fusion.2), channel_id=1, source_target_pairs={{0,4},{4,8},{8,12},{12,16},{16,20},{20,24},{24,28},{28,32},{32,36}... | collective-permute-start | bytes 196616 | tf_op jit(solution)/shard_map/ppermute | solution.py:17
  150.4 5.9 %collective-permute-start.1 = (bf16[256,256]{1,0:T(8,128)(2,1)S(1)}, bf16[256,256]{1,0:T(8,128)(2,1)S(1)}, u32[]{:S(2)}, u32[]{:S(2)}) collective-permute-start(bf16[256,256]{1,0:T(8,128)(2,1)S(1)} %maximum_maximum_fusion.2), channel_id=1, source_target_pairs={{0,8},{4,12},{8,16},{12,20},{16,24},{20,28},{24,32},{28,36},{32,40... | collective-permute-start | bytes 393224 | tf_op jit(solution)/shard_map/ppermute | solution.py:17
Sparse Core Ops, SparseCore 0:
  10.9 124.6 all-gather.1

commit v10 on v9

--- a/solution.py
+++ b/solution.py
@@ -198,7 +198,7 @@
     own_prefix = lax.dynamic_slice_in_dim(prefix, first_row, row_count)
 
     w_pairs = w_keyval.reshape(w_keyval.shape[0], pair_width)
-    block_width = math.gcd(query_width, pair_width)
+    block_width = head_dim
     cache_width = 2 * head_dim
     assert 2 * cache_local == row_count and cache_width % block_width == 0
     cache_keys = jnp.concatenate([prefix_keys[0, :, 0, :], prefix_keys[1, :, 0, :]], axis=1)

time: 180 us -> 183 us (1.017)
  Pallas kernels: 23.1 us -> 26.2 us
    pallas_call x2, Pallas kernels: 10.4 us -> 13.6 us  [project(): pl.pallas_call(projection_kernel, grid=(n_blocks,), in_specs=[pl.BlockSpe...]
  transfers between devices with their start and end apart: 3 -> 3, of which waited for: 2 -> 2; matrix products, arithmetic and copies ran while one was open for 8% -> 8% of each run, Pallas kernels for 4% -> 6%
where the time goes in v10:
time: 183 us; the launch traced here: 181 us
  waiting for transfers between devices  115 us (63%)
  Pallas kernels  26.2 us (14%)
  between operations  14.2 us (8%)
  other arithmetic  12.8 us (7%)
  local copies, waits for them, and re-layouts  7.92 us (4%)
  starting transfers between devices  4.86 us (3%)
    all_gather x1, waiting for transfers between devices, local(): gathered = lax.all_gather(combined, 'seq', axis=0, tiled=True)  112 us
    pallas_call x2, Pallas kernels, project(): pl.pallas_call(projection_kernel, grid=(n_blocks,), in_specs=[pl.BlockSpe...  13.6 us
    pallas_call x1, Pallas kernels, attend(): pl.pallas_call(kernel, grid_spec=grid_spec, out_shape=jax.ShapeDtypeStruc...  12.6 us
    ppermute x2, starting transfers between devices, from_behind(): return lax.ppermute(shard, axis, pairs)  4.82 us
  transfers between devices with their start and end apart: 3, of which 2 were waited for; matrix products, arithmetic and copies ran while one was open for 8% of the time, Pallas kernels for 6%

profile of v10, /device:TPU:1, one launch (start us, length us, event | category | flops | bytes accessed | tf_op | source)
XLA Modules:
  0.0 180.7 jit_solution(2625048441723408950)
XLA Ops:
  7.2 0.0 all-gather.2.cloned.1.call-start
  7.2 1.0 copy.28
  8.2 0.8 slice_bitcast_fusion.4
  9.0 1.8 maximum_maximum_fusion
  10.8 0.7 convert_element_type.51
  11.5 0.7 convert_element_type.60
  12.2 0.7 copy.21
  12.9 0.1 reduce-window.8
  13.0 0.1 reduce
  13.1 0.7 sub.9
  13.7 0.7 reshape.165
  14.4 0.1 pad.31.clone
  14.5 0.2 convert_reduce_fusion
  14.7 1.0 select_reduce_fusion
  15.8 0.1 dynamic-slice_bitcast_fusion
  15.9 0.1 add_add_fusion.1
  15.9 0.1 copy.22
  16.1 0.3 compare_reduce_fusion.1
  16.4 0.1 reduce_or.18
  16.6 0.1 copy.23
  16.7 0.1 reduce_or.19
  16.8 0.1 copy.24
  17.0 3.1 %gather_fusion = s32[512]{0:T(512)S(1)} fusion(s32[8192]{0:T(1024)S(1)} %convert_reduce_fusion, s32[1024]{0:T(1024)S(1)} %pad_clamp_fusion), kind=kCustom, calls=%fused_computation | custom fusion | bytes 6144 | tf_op jit(solution)/shard_map/gather | solution.py:236
  20.1 0.1 pad.13.clone
  20.2 0.1 fusion.10
  20.3 0.1 add_convert_fusion.refs_0_
  20.4 0.5 fusion
  20.9 0.1 add_add_fusion.refs_3_
  21.0 0.3 multiply_cosine_fusion
  21.3 2.2 %fusion.2.x_ref = bf16[128,8192]{1,0:T(8,128)(2,1)S(1)} fusion(bf16[128,8192]{1,0:T(8,128)(2,1)} %param.10, f32[8192]{0:T(1024)S(1)} %convert_element_type.51, f32[128]{0:T(128)S(1)} %add_rsqrt_fusion), kind=kLoop, calls=%fused_computation.5 | loop fusion | flops 4194304 | bytes 4227584 | tf_op jit(solution)/shard_map/convert_element_type | solution.py:193
  23.4 112.2 %all-gather.2.cloned.1.call-done.w_ref = bf16[8192,1536]{1,0:T(8,128)(2,1)} async-done(((bf16[128,1536]{1,0:T(8,128)(2,1)}), bf16[8192,1536]{1,0:T(8,128)(2,1)}) %all-gather.2.cloned.1.call-update) | async-done | bytes 25165840 | tf_op jit(solution)/shard_map/all_gather | solution.py:210
  135.6 3.1 %shard_map.122 = f32[128,256]{1,0:T(8,128)S(1)} custom-call(bf16[128,8192]{1,0:T(8,128)(2,1)S(1)} %fusion.2.x_ref, bf16[8192,1536]{1,0:T(8,128)(2,1)} %all-gather.2.cloned.1.call-done.w_ref, f32[1,256]{1,0:T(1,128)S(1)} %bitcast.50), custom_call_target="tpu_custom_call" | custom-call | flops 536870912 | bytes 6291456 | tf_op jit(solution)/shard_map/pallas_call | solution.py:148
  138.7 0.1 fusion.6
  138.8 0.1 fusion.8
  139.0 0.6 pad_maximum_fusion.2
  139.6 1.9 %collective-permute-start = (bf16[128,256]{1,0:T(8,128)(2,1)}, bf16[128,256]{1,0:T(8,128)(2,1)}, u32[]{:S(2)}, u32[]{:S(2)}) collective-permute-start(bf16[128,256]{1,0:T(8,128)(2,1)} %pad_maximum_fusion.2), channel_id=1, source_target_pairs={{0,4},{4,8},{8,12},{12,16},{16,20},{20,24},{24,28},{28,32},{32,36}... | collective-permute-start | bytes 196616 | tf_op jit(solution)/shard_map/ppermute | solution.py:17
  141.5 10.5 %shard_map.121 = f32[128,1024]{1,0:T(8,128)S(1)} custom-call(bf16[128,8192]{1,0:T(8,128)(2,1)S(1)} %fusion.2.x_ref, bf16[8192,1536]{1,0:T(8,128)(2,1)} %all-gather.2.cloned.1.call-done.w_ref, f32[1,1024]{1,0:T(1,128)S(1)} %bitcast.49), custom_call_target="tpu_custom_call" | custom-call | flops 2147483648 | bytes 18874368 | tf_op jit(solution)/shard_map/pallas_call | solution.py:148
  152.1 0.1 reshape.160
  152.2 0.1 copy.26
  152.3 0.2 fusion.3
  152.5 0.2 fusion.5.refs_1_
  152.7 0.9 maximum_maximum_fusion.2
  153.6 2.9 %collective-permute-start.1 = (bf16[256,256]{1,0:T(8,128)(2,1)S(1)}, bf16[256,256]{1,0:T(8,128)(2,1)S(1)}, u32[]{:S(2)}, u32[]{:S(2)}) collective-permute-start(bf16[256,256]{1,0:T(8,128)(2,1)S(1)} %maximum_maximum_fusion.2), channel_id=1, source_target_pairs={{0,8},{4,12},{8,16},{12,20},{16,24},{20,28},{24,32},{28,36},{32,40... | collective-permute-start | bytes 393224 | tf_op jit(solution)/shard_map/ppermute | solution.py:17
  156.5 0.6 slice_bitcast_fusion.7
  157.1 2.4 %collective-permute-done.1 = bf16[256,256]{1,0:T(8,128)(2,1)S(1)} collective-permute-done((bf16[256,256]{1,0:T(8,128)(2,1)S(1)}, bf16[256,256]{1,0:T(8,128)(2,1)S(1)}, u32[]{:S(2)}, u32[]{:S(2)}) %collective-permute-start.1) | collective-permute-done | bytes 131104 | tf_op jit(solution)/shard_map/ppermute | solution.py:17
  159.5 0.9 maximum_maximum_fusion.1.refs_8_
  160.4 12.6 %shard_map.123 = bf16[1024,128]{1,0:T(8,128)(2,1)S(1)} custom-call(s32[4,2]{1,0:T(4,128)S(1)} %add_convert_fusion.refs_0_, bf16[1024,128]{1,0:T(8,128)(2,1)S(1)} %fusion.5.refs_1_, s32[1024,4]{1,0:T(8,128)S(1)} %broadcast_bitcast_fusion.refs_2_, s32[8,512]{1,0:T(8,128)S(1)} %add_add_fusion.refs_3_, bf16[64,2,64,1536]{3,2,1,0:T(8,128)(2,1)} %bitcast.51, ...), custom_call_target="tpu_custom_call" | custom-call | flops 2415919104 | bytes 4980736 | tf_op jit(solution)/shard_map/pallas_call | solution.py:127
  173.0 0.8 reshape.164
  (18 shorter events, 0.2 us)
Async XLA Ops:
  7.2 13.2 %copy-start = (bf16[128,8192]{1,0:T(8,128)(2,1)S(1)}, bf16[128,8192]{1,0:T(8,128)(2,1)}, u32[]{:S(2)}) copy-start(bf16[128,8192]{1,0:T(8,128)(2,1)} %param.10) | copy-start | bytes 6291460
  7.2 128.4 %all-gather.2.cloned.1.call-start = ((), (), s32[]{:S(2)}) async-start(), calls=%async_computation | async-start | bytes 25559040 | tf_op jit(solution)/shard_map/all_gather | solution.py:210
  139.0 20.6 %copy-start.1 = (bf16[128,128]{1,0:T(8,128)(2,1)}, bf16[128,128]{1,0:T(8,128)(2,1)S(1)}, u32[]{:S(2)}) copy-start(bf16[128,128]{1,0:T(8,128)(2,1)S(1)} %get-tuple-element.9) | copy-start | bytes 98308
  139.6 13.1 %collective-permute-start = (bf16[128,256]{1,0:T(8,128)(2,1)}, bf16[128,256]{1,0:T(8,128)(2,1)}, u32[]{:S(2)}, u32[]{:S(2)}) collective-permute-start(bf16[128,256]{1,0:T(8,128)(2,1)} %pad_maximum_fusion.2), channel_id=1, source_target_pairs={{0,4},{4,8},{8,12},{12,16},{16,20},{20,24},{24,28},{28,32},{32,36}... | collective-permute-start | bytes 196616 | tf_op jit(solution)/shard_map/ppermute | solution.py:17
  153.6 5.9 %collective-permute-start.1 = (bf16[256,256]{1,0:T(8,128)(2,1)S(1)}, bf16[256,256]{1,0:T(8,128)(2,1)S(1)}, u32[]{:S(2)}, u32[]{:S(2)}) collective-permute-start(bf16[256,256]{1,0:T(8,128)(2,1)S(1)} %maximum_maximum_fusion.2), channel_id=1, source_target_pairs={{0,8},{4,12},{8,16},{12,20},{16,24},{20,28},{24,32},{28,36},{32,40... | collective-permute-start | bytes 393224 | tf_op jit(solution)/shard_map/ppermute | solution.py:17
Sparse Core Ops, SparseCore 0:
  10.9 124.6 all-gather.1

commit v11 on v9

--- a/solution.py
+++ b/solution.py
@@ -227,7 +227,8 @@
         near_rows = jnp.concatenate([from_behind(near_rows, "seq", depth), near_rows], axis=0)
         depth = 2 * depth
     depth = depth - 1
-    query_own = project(normed, gathered, q_bias.astype(jnp.float32), 0, query_width // block_width, block_width)
+    query_block = math.gcd(query_width, 4 * block_width)
+    query_own = project(normed, gathered, q_bias.astype(jnp.float32), 0, query_width // query_block, query_block)
     own_queries = rotate(query_own.reshape(row_count, heads_local, head_dim), own_positions).astype(
         jnp.bfloat16
     )

time: 180 us -> 180 us (level)
  transfers between devices with their start and end apart: 3 -> 3, of which waited for: 2 -> 2; matrix products, arithmetic and copies ran while one was open for 8% -> 8% of each run, Pallas kernels for 4% -> 5%
where the time goes in v11:
time: 180 us; the launch traced here: 178 us
  waiting for transfers between devices  115 us (64%)
  Pallas kernels  23.7 us (13%)
  between operations  14.2 us (8%)
  other arithmetic  12.8 us (7%)
  local copies, waits for them, and re-layouts  7.92 us (4%)
  starting transfers between devices  4.86 us (3%)
    all_gather x1, waiting for transfers between devices, local(): gathered = lax.all_gather(combined, 'seq', axis=0, tiled=True)  112 us
    pallas_call x1, Pallas kernels, attend(): pl.pallas_call(kernel, grid_spec=grid_spec, out_shape=jax.ShapeDtypeStruc...  12.6 us
    pallas_call x2, Pallas kernels, project(): pl.pallas_call(projection_kernel, grid=(n_blocks,), in_specs=[pl.BlockSpe...  11.1 us
    ppermute x2, starting transfers between devices, from_behind(): return lax.ppermute(shard, axis, pairs)  4.82 us
  transfers between devices with their start and end apart: 3, of which 2 were waited for; matrix products, arithmetic and copies ran while one was open for 8% of the time, Pallas kernels for 5%

profile of v11, /device:TPU:1, one launch (start us, length us, event | category | flops | bytes accessed | tf_op | source)
XLA Modules:
  0.0 178.2 jit_solution(1862517933122440639)
XLA Ops:
  7.2 0.0 all-gather.2.cloned.1.call-start
  7.2 1.0 copy.28
  8.2 0.8 slice_bitcast_fusion.4
  9.0 1.8 maximum_maximum_fusion
  10.8 0.7 convert_element_type.51
  11.5 0.7 convert_element_type.60
  12.2 0.7 copy.21
  12.9 0.1 reduce-window.8
  13.0 0.1 reduce
  13.1 0.7 sub.9
  13.7 0.7 reshape.165
  14.4 0.1 pad.31.clone
  14.5 0.2 convert_reduce_fusion
  14.7 1.0 select_reduce_fusion
  15.8 0.1 dynamic-slice_bitcast_fusion
  15.9 0.1 add_add_fusion.1
  15.9 0.1 copy.22
  16.1 0.3 compare_reduce_fusion.1
  16.4 0.1 reduce_or.18
  16.6 0.1 copy.23
  16.7 0.1 reduce_or.19
  16.8 0.1 copy.24
  17.0 3.1 %gather_fusion = s32[512]{0:T(512)S(1)} fusion(s32[8192]{0:T(1024)S(1)} %convert_reduce_fusion, s32[1024]{0:T(1024)S(1)} %pad_clamp_fusion), kind=kCustom, calls=%fused_computation | custom fusion | bytes 6144 | tf_op jit(solution)/shard_map/gather | solution.py:237
  20.1 0.1 pad.13.clone
  20.2 0.1 fusion.10
  20.3 0.1 add_convert_fusion.refs_0_
  20.4 0.5 fusion
  20.9 0.1 add_add_fusion.refs_3_
  21.0 0.3 multiply_cosine_fusion
  21.3 2.2 %fusion.2.x_ref = bf16[128,8192]{1,0:T(8,128)(2,1)S(1)} fusion(bf16[128,8192]{1,0:T(8,128)(2,1)} %param.10, f32[8192]{0:T(1024)S(1)} %convert_element_type.51, f32[128]{0:T(128)S(1)} %add_rsqrt_fusion), kind=kLoop, calls=%fused_computation.5 | loop fusion | flops 4194304 | bytes 4227584 | tf_op jit(solution)/shard_map/convert_element_type | solution.py:193
  23.4 112.2 %all-gather.2.cloned.1.call-done.w_ref = bf16[8192,1536]{1,0:T(8,128)(2,1)} async-done(((bf16[128,1536]{1,0:T(8,128)(2,1)}), bf16[8192,1536]{1,0:T(8,128)(2,1)}) %all-gather.2.cloned.1.call-update) | async-done | bytes 25165840 | tf_op jit(solution)/shard_map/all_gather | solution.py:210
  135.6 2.9 %shard_map.122 = f32[128,256]{1,0:T(8,128)S(1)} custom-call(bf16[128,8192]{1,0:T(8,128)(2,1)S(1)} %fusion.2.x_ref, bf16[8192,1536]{1,0:T(8,128)(2,1)} %all-gather.2.cloned.1.call-done.w_ref, f32[1,256]{1,0:T(1,128)S(1)} %bitcast.50), custom_call_target="tpu_custom_call" | custom-call | flops 536870912 | bytes 6291456 | tf_op jit(solution)/shard_map/pallas_call | solution.py:148
  138.6 0.1 fusion.6
  138.7 0.1 fusion.8
  138.8 0.6 pad_maximum_fusion.2
  139.5 1.9 %collective-permute-start = (bf16[128,256]{1,0:T(8,128)(2,1)}, bf16[128,256]{1,0:T(8,128)(2,1)}, u32[]{:S(2)}, u32[]{:S(2)}) collective-permute-start(bf16[128,256]{1,0:T(8,128)(2,1)} %pad_maximum_fusion.2), channel_id=1, source_target_pairs={{0,4},{4,8},{8,12},{12,16},{16,20},{20,24},{24,28},{28,32},{32,36}... | collective-permute-start | bytes 196616 | tf_op jit(solution)/shard_map/ppermute | solution.py:17
  141.4 8.2 %shard_map.121 = f32[128,1024]{1,0:T(8,128)S(1)} custom-call(bf16[128,8192]{1,0:T(8,128)(2,1)S(1)} %fusion.2.x_ref, bf16[8192,1536]{1,0:T(8,128)(2,1)} %all-gather.2.cloned.1.call-done.w_ref, f32[1,1024]{1,0:T(1,128)S(1)} %bitcast.49), custom_call_target="tpu_custom_call" | custom-call | flops 2147483648 | bytes 18874368 | tf_op jit(solution)/shard_map/pallas_call | solution.py:148
  149.5 0.1 reshape.160
  149.6 0.1 copy.26
  149.7 0.2 fusion.3
  149.9 0.2 fusion.5.refs_1_
  150.2 0.9 maximum_maximum_fusion.2
  151.1 2.9 %collective-permute-start.1 = (bf16[256,256]{1,0:T(8,128)(2,1)S(1)}, bf16[256,256]{1,0:T(8,128)(2,1)S(1)}, u32[]{:S(2)}, u32[]{:S(2)}) collective-permute-start(bf16[256,256]{1,0:T(8,128)(2,1)S(1)} %maximum_maximum_fusion.2), channel_id=1, source_target_pairs={{0,8},{4,12},{8,16},{12,20},{16,24},{20,28},{24,32},{28,36},{32,40... | collective-permute-start | bytes 393224 | tf_op jit(solution)/shard_map/ppermute | solution.py:17
  154.0 0.6 slice_bitcast_fusion.7
  154.6 2.4 %collective-permute-done.1 = bf16[256,256]{1,0:T(8,128)(2,1)S(1)} collective-permute-done((bf16[256,256]{1,0:T(8,128)(2,1)S(1)}, bf16[256,256]{1,0:T(8,128)(2,1)S(1)}, u32[]{:S(2)}, u32[]{:S(2)}) %collective-permute-start.1) | collective-permute-done | bytes 131104 | tf_op jit(solution)/shard_map/ppermute | solution.py:17
  157.0 0.9 maximum_maximum_fusion.1.refs_8_
  157.9 12.6 %shard_map.123 = bf16[1024,128]{1,0:T(8,128)(2,1)S(1)} custom-call(s32[4,2]{1,0:T(4,128)S(1)} %add_convert_fusion.refs_0_, bf16[1024,128]{1,0:T(8,128)(2,1)S(1)} %fusion.5.refs_1_, s32[1024,4]{1,0:T(8,128)S(1)} %broadcast_bitcast_fusion.refs_2_, s32[8,512]{1,0:T(8,128)S(1)} %add_add_fusion.refs_3_, bf16[64,2,64,1536]{3,2,1,0:T(8,128)(2,1)} %bitcast.51, ...), custom_call_target="tpu_custom_call" | custom-call | flops 2415919104 | bytes 4980736 | tf_op jit(solution)/shard_map/pallas_call | solution.py:127
  170.5 0.8 reshape.164
  (18 shorter events, 0.2 us)
Async XLA Ops:
  7.2 13.2 %copy-start = (bf16[128,8192]{1,0:T(8,128)(2,1)S(1)}, bf16[128,8192]{1,0:T(8,128)(2,1)}, u32[]{:S(2)}) copy-start(bf16[128,8192]{1,0:T(8,128)(2,1)} %param.10) | copy-start | bytes 6291460
  7.2 128.4 %all-gather.2.cloned.1.call-start = ((), (), s32[]{:S(2)}) async-start(), calls=%async_computation | async-start | bytes 25559040 | tf_op jit(solution)/shard_map/all_gather | solution.py:210
  138.8 18.2 %copy-start.1 = (bf16[128,128]{1,0:T(8,128)(2,1)}, bf16[128,128]{1,0:T(8,128)(2,1)S(1)}, u32[]{:S(2)}) copy-start(bf16[128,128]{1,0:T(8,128)(2,1)S(1)} %get-tuple-element.9) | copy-start | bytes 98308
  139.5 10.7 %collective-permute-start = (bf16[128,256]{1,0:T(8,128)(2,1)}, bf16[128,256]{1,0:T(8,128)(2,1)}, u32[]{:S(2)}, u32[]{:S(2)}) collective-permute-start(bf16[128,256]{1,0:T(8,128)(2,1)} %pad_maximum_fusion.2), channel_id=1, source_target_pairs={{0,4},{4,8},{8,12},{12,16},{16,20},{20,24},{24,28},{28,32},{32,36}... | collective-permute-start | bytes 196616 | tf_op jit(solution)/shard_map/ppermute | solution.py:17
  151.1 6.0 %collective-permute-start.1 = (bf16[256,256]{1,0:T(8,128)(2,1)S(1)}, bf16[256,256]{1,0:T(8,128)(2,1)S(1)}, u32[]{:S(2)}, u32[]{:S(2)}) collective-permute-start(bf16[256,256]{1,0:T(8,128)(2,1)S(1)} %maximum_maximum_fusion.2), channel_id=1, source_target_pairs={{0,8},{4,12},{8,16},{12,20},{16,24},{20,28},{24,32},{28,36},{32,40... | collective-permute-start | bytes 393224 | tf_op jit(solution)/shard_map/ppermute | solution.py:17
Sparse Core Ops, SparseCore 0:
  10.9 124.6 all-gather.1
